TPU v7x, 128 devices: a whole 4x4x4 slice. The times are simulated.
128 devices in a mesh: mgrp: 8 (over x, core), band: 16 (over y, z).
Axes of the slice: x: 4, y: 4, z: 4, core: 2. Of those that a mesh axis runs over, the one named last changes fastest.
Arguments:
- solution: float32 [2, 64, 8, 8192], P(None, None, 'mgrp', 'band'), may hold values from -6 to 6
- residual: float32 [2, 64, 8, 8192], P(None, None, 'mgrp', 'band'), may hold values from -16 to 16
- direction: float32 [2, 64, 8, 8192], P(None, None, 'mgrp', 'band'), may hold values from -16 to 16
- legendre: bfloat16 [8, 1024, 8192], P('mgrp', None, 'band'), may hold values from -0.0625 to 0.0625
- prior_inv: float32 [8192], P('band'), may hold values from 0.1 to 20, as said below
- noise_mats: bfloat16 [8, 64, 64], replicated, may hold values from -1 to 4, as said below
- noise_index: int32 [1024, 256], P(('band', 'mgrp')), may hold values from 0 to 7
- cycle_lengths: int32 [1024], P(('band', 'mgrp')), may hold values from 4096 to 16384, as said below
- m_values: int32 [8], replicated, may hold values from 0 to 8191, as said below
- cut_pattern: int32 [8, 16], P('mgrp'), may hold values from 0 to 1, as said below
Outputs:
- solution_new: float32 [2, 64, 8, 8192], P(None, None, 'mgrp', 'band')
- residual_new: float32 [2, 64, 8, 8192], P(None, None, 'mgrp', 'band')
- direction_new: float32 [2, 64, 8, 8192], P(None, None, 'mgrp', 'band')
Inputs may be any that keep to these rules, and one draw needn't show every extreme that they name: `noise_mats`: symmetric; in every row the diagonal entry exceeds the sum of the magnitudes of the other entries. `prior_inv`: positive. `cycle_lengths`: every length is a multiple of 4; cycle 0 has exactly 16384 pixels. `m_values`: distinct values; 0 and 8191 are among them. `cut_pattern`: row m is 1 on cycle blocks c_m to 15 - c_m and 0 elsewhere, for some c_m from 0 to 5.
All inputs are finite; a program needn't handle non-finite values.
Results may differ from a plain program's by a relative error of at most 0.00095.
The roundings to bfloat16 on the way count: a program that leaves them out, or rounds other values in their place, can miss the bound.
Values may be sent and summed in bfloat16 or wider, within the bound.
No kernel may reach another device: no remote copies, remote signals or barrier semaphores. Data moves between devices by JAX's collectives and lax.ppermute only.
A program may use at most 192 MiB of HBM per device.

v0:
```python
import math

import jax
import jax.numpy as jnp
from jax import lax
from jax.sharding import PartitionSpec as P

L = 8192
RLEN = 16384
BLK = 64
RB = 64


def cycle_tables(m_values, lengths, pixels):
    high_count = pixels // 128
    coarse = jnp.arange(high_count, dtype=jnp.int32) * 128
    fine = jnp.arange(128, dtype=jnp.int32)
    cycle_size = lengths[:, None, None].astype(jnp.float32)
    phase_high = m_values[None, :, None] * coarse[None, None, :] % lengths[:, None, None]
    phase_low = m_values[None, :, None] * fine[None, None, :] % lengths[:, None, None]
    angle_high = 2.0 * math.pi * phase_high.astype(jnp.float32) / cycle_size
    angle_low = 2.0 * math.pi * phase_low.astype(jnp.float32) / cycle_size
    cos_high = jnp.cos(angle_high)[:, :, :, None]
    sin_high = jnp.sin(angle_high)[:, :, :, None]
    cos_low = jnp.cos(angle_low)[:, :, None, :]
    sin_low = jnp.sin(angle_low)[:, :, None, :]
    cycle_count = lengths.shape[0]
    mode_count = m_values.shape[0]
    cos_full = (cos_high * cos_low - sin_high * sin_low).reshape(cycle_count, mode_count, pixels)
    sin_full = (sin_high * cos_low + cos_high * sin_low).reshape(cycle_count, mode_count, pixels)
    column = jnp.arange(pixels, dtype=jnp.int32)
    factor = jnp.where(m_values == 0, 1.0, 2.0).astype(jnp.float32)[None, :, None]
    inside = (column[None, None, :] < lengths[:, None, None]).astype(jnp.float32)
    cosine = factor * cos_full * inside
    sine_part = -factor * sin_full * inside
    return jnp.stack([cosine, sine_part], axis=1).astype(jnp.bfloat16)


def pair_table(noise_mats):
    kinds = noise_mats.shape[0]
    first = jnp.broadcast_to(noise_mats[:, None], (kinds, kinds, BLK, BLK))
    second = jnp.broadcast_to(noise_mats[None, :], (kinds, kinds, BLK, BLK))
    empty = jnp.zeros((kinds, kinds, BLK, BLK), noise_mats.dtype)
    upper = jnp.concatenate([first, empty], axis=3)
    lower = jnp.concatenate([empty, second], axis=3)
    return jnp.concatenate([upper, lower], axis=2).reshape(kinds * kinds, 2 * BLK, 2 * BLK)


def cycle_segment(coeffs, lengths, indices, m_values, pairs, kinds, weight):
    cycle_count, mode_count, columns = coeffs.shape
    map_count = columns // 2
    tables = cycle_tables(m_values, lengths, RLEN)
    split_coeffs = coeffs.reshape(cycle_count, mode_count, 2, map_count)
    sky_map = jnp.einsum(
        "rmcb,rcmk->rbk", split_coeffs, tables, preferred_element_type=jnp.float32
    ).astype(jnp.bfloat16)
    pair_count = RLEN // (2 * BLK)
    kind_pairs = indices.reshape(cycle_count, pair_count, 2)
    pair_index = kind_pairs[:, :, 0] * kinds + kind_pairs[:, :, 1]
    matrices = pairs.reshape(kinds * kinds, 4 * BLK * BLK)[pair_index].reshape(
        cycle_count, pair_count, 2 * BLK, 2 * BLK
    )
    blocked = sky_map.reshape(cycle_count, map_count, pair_count, 2 * BLK)
    noisy_map = weight * jnp.einsum(
        "rbqj,rqij->rbqi", blocked, matrices, preferred_element_type=jnp.float32
    )
    noisy_map = noisy_map.reshape(cycle_count, map_count, RLEN).astype(jnp.bfloat16)
    backward = jnp.einsum("rbk,rcmk->rmcb", noisy_map, tables, preferred_element_type=jnp.float32)
    return backward.reshape(cycle_count, mode_count, columns).astype(jnp.bfloat16)


def shards(
    solution,
    residual,
    direction,
    legendre,
    prior_inv,
    noise_mats,
    noise_index,
    cycle_lengths,
    m_values,
    cut_pattern,
):
    band_count = lax.axis_size("band")
    mode_local, cycle_total, l_local = legendre.shape
    map_count = direction.shape[1]
    columns = 2 * map_count
    band_rows = cycle_total // band_count
    weight = L / (cycle_total * RLEN)
    rounded = direction.astype(jnp.bfloat16).reshape(columns, mode_local, l_local)

    def row_mask(first_row, row_count):
        block_flags = lax.dynamic_slice_in_dim(cut_pattern, first_row // RB, row_count // RB, 1)
        return jnp.repeat(block_flags, RB, axis=1).T

    section = legendre
    products = jnp.einsum("mrl,nml->rmn", section, rounded, preferred_element_type=jnp.float32)
    summed = lax.psum_scatter(
        products
        * row_mask(jnp.int32(0), band_rows * lax.axis_size("band")).astype(jnp.float32)[:, :, None],
        "band",
        scatter_dimension=0,
        tiled=True,
    )
    coeffs = lax.all_to_all(
        summed.astype(jnp.bfloat16), "mgrp", split_axis=0, concat_axis=1, tiled=True
    )
    cycle_local = coeffs.shape[0]
    mode_total = coeffs.shape[1]
    kinds = noise_mats.shape[0]
    pairs = pair_table(noise_mats)
    outputs = lax.map(
        lambda operands: cycle_segment(
            operands[0], operands[1], operands[2], m_values, pairs, kinds, weight
        ),
        (
            coeffs.reshape(cycle_local // 8, 8, mode_total, columns),
            cycle_lengths.reshape(cycle_local // 8, 8),
            noise_index.reshape(cycle_local // 8, 8, RLEN // BLK),
        ),
    )
    backward = outputs.reshape(cycle_local, mode_total, columns)
    returned = lax.all_to_all(backward, "mgrp", split_axis=1, concat_axis=0, tiled=True)
    own_start = lax.axis_index("band") * band_rows
    masked = returned * row_mask(own_start, band_rows).astype(jnp.bfloat16)[:, :, None]
    section = legendre
    image_data = jnp.einsum(
        "mrl,rmn->nml",
        section,
        lax.all_gather(masked, "band", axis=0, tiled=True),
        preferred_element_type=jnp.float32,
    )
    image_data = image_data.reshape(2, map_count, mode_local, l_local)
    image_field = prior_inv[None, None, None, :] * direction + image_data
    norm_now, curvature = lax.psum(
        (
            jnp.sum(residual * residual, axis=(0, 2, 3)),
            jnp.sum(direction * image_field, axis=(0, 2, 3)),
        ),
        ("mgrp", "band"),
    )
    step_size = norm_now / curvature
    new_residual = residual - step_size[None, :, None, None] * image_field
    norm_next = lax.psum(jnp.sum(new_residual * new_residual, axis=(0, 2, 3)), ("mgrp", "band"))
    growth = norm_next / norm_now
    new_solution = solution + step_size[None, :, None, None] * direction
    new_direction = new_residual + growth[None, :, None, None] * direction
    return (new_solution, new_residual, new_direction)


def solution(mesh):
    in_specs = (
        P(None, None, "mgrp", "band"),
        P(None, None, "mgrp", "band"),
        P(None, None, "mgrp", "band"),
        P("mgrp", None, "band"),
        P("band"),
        P(),
        P(("band", "mgrp"), None),
        P(("band", "mgrp")),
        P(),
        P("mgrp", None),
    )
    out_specs = (
        P(None, None, "mgrp", "band"),
        P(None, None, "mgrp", "band"),
        P(None, None, "mgrp", "band"),
    )
    return jax.shard_map(shards, mesh=mesh, in_specs=in_specs, out_specs=out_specs, check_vma=False)
```

profile of v0, /device:TPU:1, one launch (start us, length us, event | category | flops | bytes accessed | tf_op | source)
XLA Modules:
  0.0 405.6 jit_solution(9658227207942841159)
XLA Ops:
  7.3 1.2 convert_element_type.85
  8.5 0.7 convert_bitcast_fusion
  9.8 1.0 copy.54
  11.1 1.0 fusion.46
  12.9 4.5 %fusion.15 = (bf16[8,1,8,16384]{3,2,1,0:T(8,128)(2,1)}, bf16[8,1,8,16384]{3,2,1,0:T(8,128)(2,1)}) fusion(f32[8,16384]{1,0:T(8,128)S(1)} %fusion.31, f32[8,8,128]{2,1,0:T(8,128)S(1)} %get-tuple-element.46, f32[8,8,128]{1,2,0:T(8,128)S(1)} %copy.50, f32[8,8,128]{2,1,0:T(8,128)S(1)} %get-tuple-element.47, f32[8,8,128]{1,2,0:T(8,128)S(1)} %copy.49, ...), kind=kLoop, calls=%fused_computation.19 | loop fusion | flops 12582912 | bytes 4849728 | tf_op jit(solution)/shard_map/convert
  17.7 0.5 fusion.19
  18.2 68.2 %reduce-scatter.2.cloned.1.call-done = f32[64,1,128]{2,1,0:T(1,128)} async-done(((f32[1024,1,128]{2,1,0:T(1,128)}), f32[64,1,128]{2,1,0:T(1,128)}) %reduce-scatter.2.cloned.1.call-update) | async-done | bytes 32784 | tf_op jit(solution)/shard_map/reduce_scatter | solution.py:98
  86.4 0.8 convert_element_type.89
  87.2 0.5 broadcast.277
  87.7 0.7 reduce
  88.4 0.6 reshape.351
  89.1 6.6 %all-to-all-start = ((bf16[8,2,512]{2,1,0:T(2,128)(2,1)}), bf16[8,2,512]{2,1,0:T(2,128)(2,1)S(1)}, u32[]{:S(2)}, u32[]{:S(2)}) async-start(bf16[8,2,512]{2,1,0:T(2,128)(2,1)} %reshape.351), calls=%async_computation.1 | async-start | bytes 32768 | tf_op jit(solution)/shard_map/all_to_all | solution.py:105
  95.7 23.8 %gather_fusion = bf16[1024,16384]{1,0:T(8,128)(2,1)} fusion(bf16[64,16384]{1,0:T(8,128)(2,1)S(1)} %fusion.19, s32[1024]{0:T(1024)S(1)} %bitcast_clamp_fusion), kind=kCustom, calls=%fused_computation | custom fusion | bytes 67112960 | tf_op jit(solution)/shard_map/while/body/eval_jaxpr/gather | solution.py:60
  119.4 23.2 %copy.79 = bf16[128,8,128,128]{3,2,1,0:T(8,128)(2,1)} copy(bf16[128,8,128,128]{3,1,2,0:T(8,128)(2,1)} %bitcast.114) | data formatting | bytes 67108864
  142.8 9.3 %fusion.11 = bf16[8,8,128,8,128]{4,3,2,1,0:T(8,128)(2,1)} fusion(bf16[8,1,8,16384]{3,2,1,0:T(8,128)(2,1)} %get-tuple-element.39, bf16[8,1,8,16384]{3,2,1,0:T(8,128)(2,1)S(1)} %copy-done.1, bf16[8,8,2,64]{3,2,0,1:T(2,128)(2,1)S(1)} %reshape.348), kind=kOutput, calls=%fused_computation.10 | convolution fusion | flops 278921216 | bytes 20987904 | tf_op jit(solution)/shard_map/while/body/eval_jaxpr/rmcb,rcmk->rbk/dot_general | solution.py:54
  152.1 30.0 %fusion.2 = bf16[8,64,128,128]{3,1,2,0:T(8,128)(2,1)} fusion(bf16[8,8,128,8,128]{4,3,2,1,0:T(8,128)(2,1)} %fusion.11, bf16[8,128,128,128]{3,2,1,0:T(8,128)(2,1)} %bitcast.115), kind=kOutput, calls=%fused_computation.5 | convolution fusion | flops 2164260864 | bytes 67108864 | tf_op jit(solution)/shard_map/while/body/eval_jaxpr/rbqj,rqij->rbqi/dot_general | solution.py:64
  182.1 18.5 %copy.58 = bf16[8,64,128,128]{3,2,1,0:T(8,128)(2,1)} copy(bf16[8,64,128,128]{3,1,2,0:T(8,128)(2,1)} %fusion.2) | data formatting | bytes 33554432 | tf_op jit(solution)/shard_map/while/body/eval_jaxpr/convert_element_type | solution.py:67
  200.6 25.3 %reshape.346 = bf16[8,64,16384,1]{2,1,0,3:T(8,128)(2,1)} reshape(bf16[8,64,128,128]{3,2,1,0:T(8,128)(2,1)} %copy.58) | data formatting | bytes 33554432 | tf_op jit(solution)/shard_map/while/body/eval_jaxpr/convert_element_type | solution.py:67
  225.9 8.7 %fusion.26 = bf16[8,8,2,64]{3,1,2,0:T(8,128)(2,1)S(1)} fusion(bf16[8,64,16384,1]{2,1,0,3:T(8,128)(2,1)} %reshape.346, bf16[8,1,8,16384]{3,2,1,0:T(8,128)(2,1)} %get-tuple-element.39, bf16[8,1,8,16384]{3,2,1,0:T(8,128)(2,1)S(1)} %copy-done.1), kind=kOutput, calls=%fused_computation.30 | convolution fusion | flops 270540800 | bytes 20987904 | tf_op jit(solution)/shard_map/while/body/eval_jaxpr/rbk,rcmk->rmcb/dot_general | solution.py:68
  234.7 0.7 reshape.350
  235.4 4.8 %all-to-all-start.1 = ((bf16[8,8,128]{2,0,1:T(8,128)(2,1)}), bf16[8,8,128]{2,0,1:T(8,128)(2,1)S(1)}, u32[]{:S(2)}, u32[]{:S(2)}) async-start(bf16[8,8,128]{2,0,1:T(8,128)(2,1)} %reshape.350), calls=%async_computation.2 | async-start | bytes 32768 | tf_op jit(solution)/shard_map/all_to_all | solution.py:123
  240.2 1.5 multiply_reduce_fusion.2
  241.7 0.6 fusion.51
  242.3 2.5 all-to-all-done.1
  244.9 0.7 multiply_bitcast_fusion
  245.5 17.9 %all_gather.3 = bf16[1024,1,128]{2,0,1:T(8,128)(2,1)S(1)} all-gather(bf16[64,1,128]{2,0,1:T(8,128)(2,1)S(1)} %multiply_bitcast_fusion), channel_id=1, replica_groups=mesh['mgrp'=8,'band'=16] {'band'}, dimensions={0}, use_global_device_ids=true | all-gather | bytes 278528 | tf_op jit(solution)/shard_map/all_gather | solution.py:130
  264.0 67.9 %all-reduce.2 = (f32[64]{0:T(128)S(1)}, f32[64]{0:T(128)S(1)}) all-reduce(f32[64]{0:T(128)S(1)} %multiply_reduce_fusion.2, f32[64]{0:T(128)S(1)} %get-tuple-element.52), channel_id=1, replica_groups=mesh['mgrp'=8,'band'=16] {'mgrp','band'}, use_global_device_ids=true, to_apply=%region_1.2 | all-reduce | flops 128 | bytes 1024 | tf_op jit(solution)/shard_map/psum | solution.py:135
  331.9 1.2 multiply_reduce_fusion
  333.1 62.7 %psum.23 = f32[64]{0:T(128)S(1)} all-reduce(f32[64]{0:T(128)S(1)} %get-tuple-element.36), channel_id=1, replica_groups=mesh['mgrp'=8,'band'=16] {'mgrp','band'}, use_global_device_ids=true, to_apply=%region_6.8 | all-reduce | flops 64 | bytes 512 | tf_op jit(solution)/shard_map/psum | solution.py:144
  395.7 1.0 copy.68
  396.8 1.0 copy.67
  397.8 1.0 copy.69
  (52 shorter events, 2.8 us)
Async XLA Ops:
  7.2 2.2 copy-start
  7.2 3.7 copy-start.7
  7.2 3.8 copy-start.8
  7.2 5.3 %copy-start.3 = (bf16[8,64,64]{2,1,0:T(8,128)(2,1)S(1)}, bf16[8,64,64]{2,1,0:T(8,128)(2,1)}, u32[]{:S(2)}) copy-start(bf16[8,64,64]{2,1,0:T(8,128)(2,1)} %param.17) | copy-start | bytes 196612
  7.2 5.4 %copy-start.5 = (s32[8,256]{1,0:T(8,128)S(1)}, s32[8,256]{1,0:T(8,128)}, u32[]{:S(2)}) copy-start(s32[8,256]{1,0:T(8,128)} %param.18) | copy-start | bytes 24580
  7.2 79.2 %reduce-scatter.2.cloned.1.call-start = ((), (), s32[]{:S(2)}) async-start(), calls=%async_computation.3 | async-start | bytes 557056 | tf_op jit(solution)/shard_map/reduce_scatter | solution.py:98
  89.1 53.6 %all-to-all-start = ((bf16[8,2,512]{2,1,0:T(2,128)(2,1)}), bf16[8,2,512]{2,1,0:T(2,128)(2,1)S(1)}, u32[]{:S(2)}, u32[]{:S(2)}) async-start(bf16[8,2,512]{2,1,0:T(2,128)(2,1)} %reshape.351), calls=%async_computation.1 | async-start | bytes 32768 | tf_op jit(solution)/shard_map/all_to_all | solution.py:105
  119.4 23.4 %copy-start.1 = (bf16[8,1,8,16384]{3,2,1,0:T(8,128)(2,1)S(1)}, bf16[8,1,8,16384]{3,2,1,0:T(8,128)(2,1)}, u32[]{:S(2)}) copy-start(bf16[8,1,8,16384]{3,2,1,0:T(8,128)(2,1)} %get-tuple-element.38) | copy-start | bytes 6291460
  225.9 15.8 %copy-start.9 = (s32[1,16]{1,0:T(1,128)S(1)}, s32[1,16]{1,0:T(1,128)}, u32[]{:S(2)}) copy-start(s32[1,16]{1,0:T(1,128)} %param.21) | copy-start | bytes 196
  225.9 37.6 %copy-start.2 = (f32[2,64,1,512]{3,2,1,0:T(1,128)S(1)}, f32[2,64,1,512]{3,2,1,0:T(1,128)}, u32[]{:S(2)}) copy-start(f32[2,64,1,512]{3,2,1,0:T(1,128)} %param.14) | copy-start | bytes 786436
  225.9 37.6 %copy-start.6 = (f32[512]{0:T(512)S(1)}, f32[512]{0:T(512)}, u32[]{:S(2)}) copy-start(f32[512]{0:T(512)} %param.16) | copy-start | bytes 6148
  234.7 162.0 %copy-start.4 = (f32[2,64,1,512]{3,2,1,0:T(1,128)S(1)}, f32[2,64,1,512]{3,2,1,0:T(1,128)}, u32[]{:S(2)}) copy-start(f32[2,64,1,512]{3,2,1,0:T(1,128)} %param.12) | copy-start | bytes 786436
  235.4 9.5 %all-to-all-start.1 = ((bf16[8,8,128]{2,0,1:T(8,128)(2,1)}), bf16[8,8,128]{2,0,1:T(8,128)(2,1)S(1)}, u32[]{:S(2)}, u32[]{:S(2)}) async-start(bf16[8,8,128]{2,0,1:T(8,128)(2,1)} %reshape.350), calls=%async_computation.2 | async-start | bytes 32768 | tf_op jit(solution)/shard_map/all_to_all | solution.py:123
Sparse Core Ops, SparseCore 0:
  11.2 75.1 reduce-scatter.1
where the time goes:
time: 407 us; the launch traced here: 406 us
  blocking collectives  148 us (36%)
  local copies, waits for them, and re-layouts  98.1 us (24%)
  waiting for transfers between devices  70.7 us (17%)
  matrix products  48.9 us (12%)
  between operations  14.3 us (4%)
  other arithmetic  13.7 us (3%)
  starting transfers between devices  11.4 us (3%)
    reduce_scatter x1, waiting for transfers between devices, shards(): lax.psum_scatter(products * row_mask(jnp.int32(0), band_rows * lax.axis_s...  68.2 us
    psum x1, blocking collectives, shards(): lax.psum((jnp.sum(residual * residual, axis=(0, 2, 3)), jnp.sum(direction...  67.9 us
    psum x1, blocking collectives, shards(): lax.psum(jnp.sum(new_residual * new_residual, axis=(0, 2, 3)), ('mgrp', '...  62.7 us
    convert_element_type x2, local copies, waits for them, and re-layouts, cycle_segment(): noisy_map.reshape(cycle_count, map_count, RLEN).astype(jnp.bfloat16)  43.8 us
    dot_general x1, matrix products, cycle_segment(): jnp.einsum('rbqj,rqij->rbqi', blocked, matrices, preferred_element_type=j...  30 us
    unnamed x30, local copies, waits for them, and re-layouts  27.1 us
    gather x1, local copies, waits for them, and re-layouts, cycle_segment(): pairs.reshape(kinds * kinds, 4 * BLK * BLK)[pair_index]  23.8 us
    all_gather x1, blocking collectives, shards(): lax.all_gather(masked, 'band', axis=0, tiled=True)  17.9 us
  transfers between devices with their start and end apart: 3, of which 2 were waited for; matrix products, arithmetic and copies ran while one was open for 14% of the time, Pallas kernels for 0%

commit v1 on v0

--- a/solution.py
+++ b/solution.py
@@ -9,6 +9,36 @@
 RLEN = 16384
 BLK = 64
 RB = 64
+
+
+MESH_AXES = ("mgrp", "band")
+
+
+def total_over_mesh(values):
+    count = lax.axis_size(MESH_AXES)
+    copies = jnp.broadcast_to(values[None], (count,) + values.shape)
+    return jnp.sum(lax.all_to_all(copies, MESH_AXES, 0, 0, tiled=True), axis=0)
+
+
+def gather_cycles(partials, band_count):
+    cycle_total, columns = partials.shape
+    group_count = lax.axis_size("mgrp")
+    own = cycle_total // (band_count * group_count)
+    pieces = partials.reshape(band_count, group_count, own, columns).transpose(1, 0, 2, 3)
+    pieces = pieces.reshape(group_count * band_count, own, columns)
+    received = lax.all_to_all(pieces, MESH_AXES, 0, 0, tiled=True)
+    received = received.reshape(group_count, band_count, own, columns)
+    return jnp.sum(received, axis=1).transpose(1, 0, 2)
+
+
+def spread_cycles(backward, band_count):
+    own, group_count, columns = backward.shape
+    pieces = jnp.broadcast_to(
+        backward.transpose(1, 0, 2)[:, None], (group_count, band_count, own, columns)
+    ).reshape(group_count * band_count, own, columns)
+    received = lax.all_to_all(pieces, MESH_AXES, 0, 0, tiled=True)
+    received = received.reshape(group_count, band_count, own, columns).transpose(1, 0, 2, 3)
+    return received.reshape(band_count * group_count * own, columns)
 
 
 def cycle_tables(m_values, lengths, pixels):
@@ -95,16 +125,8 @@
 
     section = legendre
     products = jnp.einsum("mrl,nml->rmn", section, rounded, preferred_element_type=jnp.float32)
-    summed = lax.psum_scatter(
-        products
-        * row_mask(jnp.int32(0), band_rows * lax.axis_size("band")).astype(jnp.float32)[:, :, None],
-        "band",
-        scatter_dimension=0,
-        tiled=True,
-    )
-    coeffs = lax.all_to_all(
-        summed.astype(jnp.bfloat16), "mgrp", split_axis=0, concat_axis=1, tiled=True
-    )
+    masked_products = products * row_mask(jnp.int32(0), cycle_total).astype(jnp.float32)[:, :, None]
+    coeffs = gather_cycles(masked_products.reshape(cycle_total, columns), band_count).astype(jnp.bfloat16)
     cycle_local = coeffs.shape[0]
     mode_total = coeffs.shape[1]
     kinds = noise_mats.shape[0]
@@ -120,28 +142,24 @@
         ),
     )
     backward = outputs.reshape(cycle_local, mode_total, columns)
-    returned = lax.all_to_all(backward, "mgrp", split_axis=1, concat_axis=0, tiled=True)
-    own_start = lax.axis_index("band") * band_rows
-    masked = returned * row_mask(own_start, band_rows).astype(jnp.bfloat16)[:, :, None]
-    section = legendre
+    returned = spread_cycles(backward, band_count)
+    masked = returned * row_mask(jnp.int32(0), cycle_total).astype(jnp.bfloat16)
     image_data = jnp.einsum(
-        "mrl,rmn->nml",
-        section,
-        lax.all_gather(masked, "band", axis=0, tiled=True),
-        preferred_element_type=jnp.float32,
+        "mrl,rn->nml", legendre, masked, preferred_element_type=jnp.float32
     )
     image_data = image_data.reshape(2, map_count, mode_local, l_local)
     image_field = prior_inv[None, None, None, :] * direction + image_data
-    norm_now, curvature = lax.psum(
-        (
-            jnp.sum(residual * residual, axis=(0, 2, 3)),
-            jnp.sum(direction * image_field, axis=(0, 2, 3)),
-        ),
-        ("mgrp", "band"),
+    norm_now, curvature = total_over_mesh(
+        jnp.stack(
+            [
+                jnp.sum(residual * residual, axis=(0, 2, 3)),
+                jnp.sum(direction * image_field, axis=(0, 2, 3)),
+            ]
+        )
     )
     step_size = norm_now / curvature
     new_residual = residual - step_size[None, :, None, None] * image_field
-    norm_next = lax.psum(jnp.sum(new_residual * new_residual, axis=(0, 2, 3)), ("mgrp", "band"))
+    norm_next = total_over_mesh(jnp.sum(new_residual * new_residual, axis=(0, 2, 3)))
     growth = norm_next / norm_now
     new_solution = solution + step_size[None, :, None, None] * direction
     new_direction = new_residual + growth[None, :, None, None] * direction

time: 407 us -> 221 us (0.54)
  blocking collectives: 148 us -> 13.6 us
  waiting for transfers between devices: 70.7 us -> 18.1 us
  starting transfers between devices: 11.4 us -> 26.2 us
  between operations: 14.3 us -> 1.01 us
    psum x2 -> x0, blocking collectives: 131 us -> none  [the longest x1 67.9 us: shards(): lax.psum((jnp.sum(residual * residual, axis=(0, 2, 3)), jnp.sum(direction...]
    reduce_scatter x1 -> x0, waiting for transfers between devices: 68.2 us -> none  [shards(): lax.psum_scatter(products * row_mask(jnp.int32(0), band_rows * lax.axis_s...]
    all_gather x1 -> x0, blocking collectives: 17.9 us -> none  [shards(): lax.all_gather(masked, 'band', axis=0, tiled=True)]
    all_to_all x2 -> x3, waiting for transfers between devices: 2.54 us -> 18.1 us  [the longest x1 9.53 us: spread_cycles(): received = lax.all_to_all(pieces, MESH_AXES, 0, 0, tiled=True)]
    all_to_all x2 -> x3, starting transfers between devices: 11.4 us -> 26.2 us  [the longest x1 11.9 us: gather_cycles(): received = lax.all_to_all(pieces, MESH_AXES, 0, 0, tiled=True)]
    all_to_all x0 -> x1, blocking collectives: none -> 13.6 us  [total_over_mesh(): return jnp.sum(lax.all_to_all(copies, MESH_AXES, 0, 0, tiled=True), axis=0)]
    unnamed x30 -> x31, local copies, waits for them, and re-layouts: 27.1 us -> 26.7 us
  transfers between devices with their start and end apart: 3 -> 3, of which waited for: 2 -> 2; matrix products, arithmetic and copies ran while one was open for 14% -> 26% of each run, Pallas kernels for 0% -> 0%
where the time goes in v1:
time: 221 us; the launch traced here: 220 us
  local copies, waits for them, and re-layouts  98.8 us (45%)
  matrix products  48.9 us (22%)
  starting transfers between devices  26.2 us (12%)
  waiting for transfers between devices  18.1 us (8%)
  blocking collectives  13.6 us (6%)
  other arithmetic  13 us (6%)
    convert_element_type x2, local copies, waits for them, and re-layouts, cycle_segment(): noisy_map.reshape(cycle_count, map_count, RLEN).astype(jnp.bfloat16)  43.8 us
    dot_general x1, matrix products, cycle_segment(): jnp.einsum('rbqj,rqij->rbqi', blocked, matrices, preferred_element_type=j...  30 us
    unnamed x31, local copies, waits for them, and re-layouts  26.7 us
    gather x1, local copies, waits for them, and re-layouts, cycle_segment(): pairs.reshape(kinds * kinds, 4 * BLK * BLK)[pair_index]  23.8 us
    all_to_all x1, blocking collectives, total_over_mesh(): return jnp.sum(lax.all_to_all(copies, MESH_AXES, 0, 0, tiled=True), axis=0)  13.6 us
    all_to_all x1, starting transfers between devices, gather_cycles(): received = lax.all_to_all(pieces, MESH_AXES, 0, 0, tiled=True)  11.9 us
    all_to_all x1, starting transfers between devices, spread_cycles(): received = lax.all_to_all(pieces, MESH_AXES, 0, 0, tiled=True)  9.76 us
    all_to_all x1, waiting for transfers between devices, spread_cycles(): received = lax.all_to_all(pieces, MESH_AXES, 0, 0, tiled=True)  9.53 us
  transfers between devices with their start and end apart: 3, of which 2 were waited for; matrix products, arithmetic and copies ran while one was open for 26% of the time, Pallas kernels for 0%

profile of v1, /device:TPU:1, one launch (start us, length us, event | category | flops | bytes accessed | tf_op | source)
XLA Modules:
  0.0 219.5 jit_solution(6760913990189348138)
XLA Ops:
  0.7 1.3 convert_bitcast_fusion.1
  2.1 1.1 convert_element_type.93
  3.3 0.5 fusion.21
  3.9 0.8 copy.128
  4.8 11.9 %all-to-all-start = ((f32[128,8,128]{2,1,0:T(8,128)}), f32[128,8,128]{2,1,0:T(8,128)}, u32[]{:S(2)}, u32[]{:S(2)}) async-start(f32[128,8,128]{2,1,0:T(8,128)} %bitcast.19), calls=%async_computation | async-start | bytes 1048576 | tf_op jit(solution)/shard_map/all_to_all | solution.py:29
  17.0 1.0 fusion.46
  18.5 4.5 %fusion.15 = (bf16[8,1,8,16384]{3,2,1,0:T(8,128)(2,1)}, bf16[8,1,8,16384]{3,2,1,0:T(8,128)(2,1)}) fusion(f32[8,16384]{1,0:T(8,128)S(1)} %fusion.31, f32[8,8,128]{2,1,0:T(8,128)S(1)} %get-tuple-element.53, f32[8,8,128]{1,2,0:T(8,128)S(1)} %copy.123, f32[8,8,128]{2,1,0:T(8,128)S(1)} %get-tuple-element.54, f32[8,8,128]{1,2,0:T(8,128)S(1)} %copy.122, ...), kind=kLoop, calls=%fused_computation.19 | loop fusion | flops 12582912 | bytes 4849728 | tf_op jit(solution)/shard_map/convert
  23.3 0.5 fusion.19
  24.1 23.8 %gather_fusion = bf16[1024,16384]{1,0:T(8,128)(2,1)} fusion(bf16[64,16384]{1,0:T(8,128)(2,1)S(1)} %fusion.19, s32[1024]{0:T(1024)S(1)} %bitcast_clamp_fusion), kind=kCustom, calls=%fused_computation | custom fusion | bytes 67112960 | tf_op jit(solution)/shard_map/while/body/eval_jaxpr/gather | solution.py:90
  47.9 23.2 %copy.157 = bf16[128,8,128,128]{3,2,1,0:T(8,128)(2,1)} copy(bf16[128,8,128,128]{3,1,2,0:T(8,128)(2,1)} %bitcast.121) | data formatting | bytes 67108864
  71.2 1.1 bitcast_reduce_fusion
  72.3 9.3 %fusion.11 = bf16[8,8,128,8,128]{4,3,2,1,0:T(8,128)(2,1)} fusion(bf16[8,1,8,16384]{3,2,1,0:T(8,128)(2,1)} %get-tuple-element.46, bf16[8,1,8,16384]{3,2,1,0:T(8,128)(2,1)S(1)} %copy-done.1, bf16[8,8,2,64]{3,2,0,1:T(2,128)(2,1)S(1)} %reshape.376), kind=kOutput, calls=%fused_computation.10 | convolution fusion | flops 278921216 | bytes 20987904 | tf_op jit(solution)/shard_map/while/body/eval_jaxpr/rmcb,rcmk->rbk/dot_general | solution.py:84
  81.7 30.0 %fusion.2 = bf16[8,64,128,128]{3,1,2,0:T(8,128)(2,1)} fusion(bf16[8,8,128,8,128]{4,3,2,1,0:T(8,128)(2,1)} %fusion.11, bf16[8,128,128,128]{3,2,1,0:T(8,128)(2,1)} %bitcast.122), kind=kOutput, calls=%fused_computation.5 | convolution fusion | flops 2164260864 | bytes 67108864 | tf_op jit(solution)/shard_map/while/body/eval_jaxpr/rbqj,rqij->rbqi/dot_general | solution.py:94
  111.6 18.5 %copy.132 = bf16[8,64,128,128]{3,2,1,0:T(8,128)(2,1)} copy(bf16[8,64,128,128]{3,1,2,0:T(8,128)(2,1)} %fusion.2) | data formatting | bytes 33554432 | tf_op jit(solution)/shard_map/while/body/eval_jaxpr/convert_element_type | solution.py:97
  130.1 25.3 %reshape.374 = bf16[8,64,16384,1]{2,1,0,3:T(8,128)(2,1)} reshape(bf16[8,64,128,128]{3,2,1,0:T(8,128)(2,1)} %copy.132) | data formatting | bytes 33554432 | tf_op jit(solution)/shard_map/while/body/eval_jaxpr/convert_element_type | solution.py:97
  155.5 8.7 %fusion.26 = bf16[8,8,2,64]{3,1,2,0:T(8,128)(2,1)S(1)} fusion(bf16[8,64,16384,1]{2,1,0,3:T(8,128)(2,1)} %reshape.374, bf16[8,1,8,16384]{3,2,1,0:T(8,128)(2,1)} %get-tuple-element.46, bf16[8,1,8,16384]{3,2,1,0:T(8,128)(2,1)S(1)} %copy-done.1), kind=kOutput, calls=%fused_computation.30 | convolution fusion | flops 270540800 | bytes 20987904 | tf_op jit(solution)/shard_map/while/body/eval_jaxpr/rbk,rcmk->rmcb/dot_general | solution.py:98
  164.4 0.7 broadcast_in_dim.61
  165.1 9.8 %all-to-all-start.1 = ((bf16[128,8,128]{2,1,0:T(8,128)(2,1)}), bf16[128,8,128]{2,1,0:T(8,128)(2,1)S(1)}, u32[]{:S(2)}, u32[]{:S(2)}) async-start(bf16[128,8,128]{2,1,0:T(8,128)(2,1)} %bitcast.28), calls=%async_computation.1 | async-start | bytes 524288 | tf_op jit(solution)/shard_map/all_to_all | solution.py:39
  175.0 1.5 multiply_reduce_fusion.2
  176.6 9.5 %all-to-all-done.1 = bf16[128,8,128]{2,1,0:T(8,128)(2,1)S(1)} async-done(((bf16[128,8,128]{2,1,0:T(8,128)(2,1)}), bf16[128,8,128]{2,1,0:T(8,128)(2,1)S(1)}, u32[]{:S(2)}, u32[]{:S(2)}) %all-to-all-start.1) | async-done | bytes 262176 | tf_op jit(solution)/shard_map/all_to_all | solution.py:39
  186.2 0.2 bitcast_multiply_fusion.2
  186.5 0.4 multiply_reduce_fusion.1
  187.2 13.6 %all_to_all.21 = f32[128,1,128]{2,1,0:T(1,128)S(1)} all-to-all(f32[128,1,128]{2,1,0:T(1,128)S(1)} %reshape.378), channel_id=1, replica_groups=mesh['mgrp'=8,'band'=16] {'mgrp','band'}, dimensions={0} | all-to-all | bytes 131072 | tf_op jit(solution)/shard_map/all_to_all | solution.py:20
  200.8 0.5 broadcast.254
  201.3 0.8 reduce.1
  202.4 0.2 multiply_reduce_fusion
  202.6 0.7 broadcast_in_dim.64
  203.3 4.5 %all-to-all-start.3 = ((f32[128,1,64]{2,1,0:T(1,128)}), f32[128,1,64]{2,1,0:T(1,128)S(1)}, u32[]{:S(2)}, u32[]{:S(2)}) async-start(f32[128,1,64]{2,1,0:T(1,128)} %broadcast_in_dim.64), calls=%async_computation.3 | async-start | bytes 131072 | tf_op jit(solution)/shard_map/all_to_all | solution.py:20
  207.8 1.0 copy.145
  208.7 8.6 %all-to-all-done.3 = f32[128,1,64]{2,1,0:T(1,128)S(1)} async-done(((f32[128,1,64]{2,1,0:T(1,128)}), f32[128,1,64]{2,1,0:T(1,128)S(1)}, u32[]{:S(2)}, u32[]{:S(2)}) %all-to-all-start.3) | async-done | bytes 32800 | tf_op jit(solution)/shard_map/all_to_all | solution.py:20
  217.6 1.0 copy.144
  218.6 1.0 copy.146
  (60 shorter events, 3.0 us)
Async XLA Ops:
  0.6 2.6 %copy-start = (bf16[1,1024,512]{2,1,0:T(8,128)(2,1)S(1)}, bf16[1,1024,512]{2,1,0:T(8,128)(2,1)}, u32[]{:S(2)}) copy-start(bf16[1,1024,512]{2,1,0:T(8,128)(2,1)} %param.15) | copy-start | bytes 3145732
  0.6 16.1 %copy-start.8 = (s32[8]{0:T(128)S(1)}, s32[8]{0:T(128)}, u32[]{:S(2)}) copy-start(s32[8]{0:T(128)} %param.19) | copy-start | bytes 100
  0.7 16.3 %copy-start.9 = (s32[8]{0:T(128)S(1)}, s32[8]{0:T(128)}, u32[]{:S(2)}) copy-start(s32[8]{0:T(128)} %param.20) | copy-start | bytes 100
  0.7 17.7 %copy-start.4 = (bf16[8,64,64]{2,1,0:T(8,128)(2,1)S(1)}, bf16[8,64,64]{2,1,0:T(8,128)(2,1)}, u32[]{:S(2)}) copy-start(bf16[8,64,64]{2,1,0:T(8,128)(2,1)} %param.17) | copy-start | bytes 196612
  4.8 66.4 %all-to-all-start = ((f32[128,8,128]{2,1,0:T(8,128)}), f32[128,8,128]{2,1,0:T(8,128)}, u32[]{:S(2)}, u32[]{:S(2)}) async-start(f32[128,8,128]{2,1,0:T(8,128)} %bitcast.19), calls=%async_computation | async-start | bytes 1048576 | tf_op jit(solution)/shard_map/all_to_all | solution.py:29
  23.0 0.8 copy-start.6
  47.9 24.4 %copy-start.1 = (bf16[8,1,8,16384]{3,2,1,0:T(8,128)(2,1)S(1)}, bf16[8,1,8,16384]{3,2,1,0:T(8,128)(2,1)}, u32[]{:S(2)}) copy-start(bf16[8,1,8,16384]{3,2,1,0:T(8,128)(2,1)} %get-tuple-element.45) | copy-start | bytes 6291460
  155.5 19.4 %copy-start.10 = (bf16[16]{0:T(256)(128)(2,1)S(1)}, bf16[16]{0:T(256)(128)(2,1)}, u32[]{:S(2)}) copy-start(bf16[16]{0:T(256)(128)(2,1)} %get-tuple-element.55) | copy-start | bytes 100
  155.5 31.1 %copy-start.2 = (f32[2,64,1,512]{3,2,1,0:T(1,128)S(1)}, f32[2,64,1,512]{3,2,1,0:T(1,128)}, u32[]{:S(2)}) copy-start(f32[2,64,1,512]{3,2,1,0:T(1,128)} %param.14) | copy-start | bytes 786436
  155.5 31.1 %copy-start.7 = (f32[512]{0:T(512)S(1)}, f32[512]{0:T(512)}, u32[]{:S(2)}) copy-start(f32[512]{0:T(512)} %param.16) | copy-start | bytes 6148
  164.2 38.2 %copy-start.3 = (f32[2,64,1,512]{3,2,1,0:T(1,128)S(1)}, f32[2,64,1,512]{3,2,1,0:T(1,128)}, u32[]{:S(2)}) copy-start(f32[2,64,1,512]{3,2,1,0:T(1,128)} %param.13) | copy-start | bytes 786436
  164.2 53.3 %copy-start.5 = (f32[2,64,1,512]{3,2,1,0:T(1,128)S(1)}, f32[2,64,1,512]{3,2,1,0:T(1,128)}, u32[]{:S(2)}) copy-start(f32[2,64,1,512]{3,2,1,0:T(1,128)} %param.12) | copy-start | bytes 786436
  165.1 21.0 %all-to-all-start.1 = ((bf16[128,8,128]{2,1,0:T(8,128)(2,1)}), bf16[128,8,128]{2,1,0:T(8,128)(2,1)S(1)}, u32[]{:S(2)}, u32[]{:S(2)}) async-start(bf16[128,8,128]{2,1,0:T(8,128)(2,1)} %bitcast.28), calls=%async_computation.1 | async-start | bytes 524288 | tf_op jit(solution)/shard_map/all_to_all | solution.py:39
  203.3 14.0 %all-to-all-start.3 = ((f32[128,1,64]{2,1,0:T(1,128)}), f32[128,1,64]{2,1,0:T(1,128)S(1)}, u32[]{:S(2)}, u32[]{:S(2)}) async-start(f32[128,1,64]{2,1,0:T(1,128)} %broadcast_in_dim.64), calls=%async_computation.3 | async-start | bytes 131072 | tf_op jit(solution)/shard_map/all_to_all | solution.py:20

commit v2 on v1

--- a/solution.py
+++ b/solution.py
@@ -1,8 +1,11 @@
+import functools
 import math
 
 import jax
 import jax.numpy as jnp
 from jax import lax
+from jax.experimental import pallas as pl
+from jax.experimental.pallas import tpu as pltpu
 from jax.sharding import PartitionSpec as P
 
 L = 8192
@@ -99,6 +102,75 @@
     return backward.reshape(cycle_count, mode_count, columns).astype(jnp.bfloat16)
 
 
+def noise_kernel(index_ref, coeff_ref, table_ref, pair_ref, back_ref, noisy_ref, *, weight):
+    cycle = pl.program_id(0)
+    span = 1024
+    pair_width = 2 * BLK
+    coeff = coeff_ref[0]
+
+    def chunk(step, carry):
+        start = pl.multiple_of(step * span, span)
+        sky = jnp.dot(
+            coeff, table_ref[0, :, pl.ds(start, span)], preferred_element_type=jnp.float32
+        ).astype(jnp.bfloat16)
+        for inner in range(span // pair_width):
+            block = (start + inner * pair_width) // BLK
+            kinds = pair_ref.shape[0]
+            side = int(round(kinds ** 0.5))
+            pick = index_ref[cycle, block] * side + index_ref[cycle, block + 1]
+            noisy = jnp.dot(
+                sky[:, inner * pair_width:(inner + 1) * pair_width],
+                pair_ref[pick],
+                preferred_element_type=jnp.float32,
+            )
+            noisy_ref[:, pl.ds(start + inner * pair_width, pair_width)] = (
+                weight * noisy
+            ).astype(jnp.bfloat16)
+        return carry
+
+    lax.fori_loop(0, table_ref.shape[2] // span, chunk, 0)
+    back_ref[0] = lax.dot_general(
+        noisy_ref[...],
+        table_ref[0],
+        (((1,), (1,)), ((), ())),
+        preferred_element_type=jnp.float32,
+    ).astype(back_ref.dtype)
+
+
+def cycle_transform(coeffs, lengths, indices, m_values, noise_mats, weight):
+    cycle_count, mode_count, columns = coeffs.shape
+    map_count = columns // 2
+    kinds = noise_mats.shape[0]
+    tables = cycle_tables(m_values, lengths, RLEN).reshape(cycle_count, 2 * mode_count, RLEN)
+    coeff_t = (
+        coeffs.reshape(cycle_count, mode_count, 2, map_count)
+        .transpose(0, 3, 2, 1)
+        .reshape(cycle_count, map_count, 2 * mode_count)
+    )
+    pairs_t = jnp.swapaxes(pair_table(noise_mats), 1, 2)
+    grid_spec = pltpu.PrefetchScalarGridSpec(
+        num_scalar_prefetch=1,
+        grid=(cycle_count,),
+        in_specs=[
+            pl.BlockSpec((1, map_count, 2 * mode_count), lambda r, idx: (r, 0, 0)),
+            pl.BlockSpec((1, 2 * mode_count, RLEN), lambda r, idx: (r, 0, 0)),
+            pl.BlockSpec(pairs_t.shape, lambda r, idx: (0, 0, 0)),
+        ],
+        out_specs=pl.BlockSpec((1, map_count, 2 * mode_count), lambda r, idx: (r, 0, 0)),
+        scratch_shapes=[pltpu.VMEM((map_count, RLEN), jnp.bfloat16)],
+    )
+    back = pl.pallas_call(
+        functools.partial(noise_kernel, weight=weight),
+        grid_spec=grid_spec,
+        out_shape=jax.ShapeDtypeStruct((cycle_count, map_count, 2 * mode_count), jnp.bfloat16),
+    )(indices, coeff_t, tables, pairs_t)
+    return (
+        back.reshape(cycle_count, map_count, 2, mode_count)
+        .transpose(0, 3, 2, 1)
+        .reshape(cycle_count, mode_count, columns)
+    )
+
+
 def shards(
     solution,
     residual,
@@ -129,18 +201,7 @@
     coeffs = gather_cycles(masked_products.reshape(cycle_total, columns), band_count).astype(jnp.bfloat16)
     cycle_local = coeffs.shape[0]
     mode_total = coeffs.shape[1]
-    kinds = noise_mats.shape[0]
-    pairs = pair_table(noise_mats)
-    outputs = lax.map(
-        lambda operands: cycle_segment(
-            operands[0], operands[1], operands[2], m_values, pairs, kinds, weight
-        ),
-        (
-            coeffs.reshape(cycle_local // 8, 8, mode_total, columns),
-            cycle_lengths.reshape(cycle_local // 8, 8),
-            noise_index.reshape(cycle_local // 8, 8, RLEN // BLK),
-        ),
-    )
+    outputs = cycle_transform(coeffs, cycle_lengths, noise_index, m_values, noise_mats, weight)
     backward = outputs.reshape(cycle_local, mode_total, columns)
     returned = spread_cycles(backward, band_count)
     masked = returned * row_mask(jnp.int32(0), cycle_total).astype(jnp.bfloat16)

time: 221 us -> 132 us (0.60)
  local copies, waits for them, and re-layouts: 98.8 us -> 9.79 us
  Pallas kernels: 0 us -> 48.9 us
  matrix products: 48.9 us -> 0.89 us
  waiting for transfers between devices: 18.1 us -> 23.3 us
  starting transfers between devices: 26.2 us -> 21.5 us
    pallas_call x0 -> x1, Pallas kernels: none -> 48.9 us  [cycle_transform(): pl.pallas_call(functools.partial(noise_kernel, weight=weight), grid_spec=...]
    dot_general x3 -> x0, matrix products: 48 us -> none  [the longest x1 30 us: cycle_segment(): jnp.einsum('rbqj,rqij->rbqi', blocked, matrices, preferred_element_type=j...]
    convert_element_type x4 -> x1, local copies, waits for them, and re-layouts: 44 us -> 0.01 us  [shards(): gather_cycles(masked_products.reshape(cycle_total, columns), band_count)]
    gather x1 -> x0, local copies, waits for them, and re-layouts: 23.8 us -> none  [cycle_segment(): pairs.reshape(kinds * kinds, 4 * BLK * BLK)[pair_index]]
    unnamed x31 -> x23, local copies, waits for them, and re-layouts: 26.7 us -> 3.38 us
    all_to_all x1, starting transfers between devices: 9.76 us -> 5.53 us  [spread_cycles(): received = lax.all_to_all(pieces, MESH_AXES, 0, 0, tiled=True)]
    all_to_all x1, waiting for transfers between devices: 0.01 us -> 4.23 us  [gather_cycles(): received = lax.all_to_all(pieces, MESH_AXES, 0, 0, tiled=True)]
    convert_element_type x0 -> x1, other arithmetic: none -> 2.3 us  [cycle_tables(): return jnp.stack([cosine, sine_part], axis=1).astype(jnp.bfloat16)]
  transfers between devices with their start and end apart: 3 -> 3, of which waited for: 2 -> 3; matrix products, arithmetic and copies ran while one was open for 26% -> 9% of each run, Pallas kernels for 0% -> 0%
where the time goes in v2:
time: 132 us
  Pallas kernels  48.9 us (37%)
  waiting for transfers between devices  23.3 us (18%)
  starting transfers between devices  21.5 us (16%)
  blocking collectives  13.6 us (10%)
  other arithmetic  12.6 us (10%)
  local copies, waits for them, and re-layouts  9.79 us (7%)
    pallas_call x1, Pallas kernels, cycle_transform(): pl.pallas_call(functools.partial(noise_kernel, weight=weight), grid_spec=...  48.9 us
    all_to_all x1, blocking collectives, total_over_mesh(): return jnp.sum(lax.all_to_all(copies, MESH_AXES, 0, 0, tiled=True), axis=0)  13.6 us
    all_to_all x1, starting transfers between devices, gather_cycles(): received = lax.all_to_all(pieces, MESH_AXES, 0, 0, tiled=True)  11.5 us
    all_to_all x1, waiting for transfers between devices, spread_cycles(): received = lax.all_to_all(pieces, MESH_AXES, 0, 0, tiled=True)  10.5 us
    all_to_all x1, waiting for transfers between devices, total_over_mesh(): return jnp.sum(lax.all_to_all(copies, MESH_AXES, 0, 0, tiled=True), axis=0)  8.57 us
    all_to_all x1, starting transfers between devices, spread_cycles(): received = lax.all_to_all(pieces, MESH_AXES, 0, 0, tiled=True)  5.53 us
    all_to_all x1, starting transfers between devices, total_over_mesh(): return jnp.sum(lax.all_to_all(copies, MESH_AXES, 0, 0, tiled=True), axis=0)  4.48 us
    all_to_all x1, waiting for transfers between devices, gather_cycles(): received = lax.all_to_all(pieces, MESH_AXES, 0, 0, tiled=True)  4.23 us
  transfers between devices with their start and end apart: 3, of which 3 were waited for; matrix products, arithmetic and copies ran while one was open for 9% of the time, Pallas kernels for 0%

profile of v2, /device:TPU:1, one launch (start us, length us, event | category | flops | bytes accessed | tf_op | source)
XLA Modules:
  0.0 131.6 jit_solution(5622844190870118753)
XLA Ops:
  0.7 0.8 convert_bitcast_fusion.1
  1.6 1.1 convert_element_type.63
  2.7 0.5 fusion.8
  3.4 0.8 copy.119
  4.3 11.5 %all-to-all-start = ((f32[128,8,128]{2,1,0:T(8,128)}), f32[128,8,128]{2,1,0:T(8,128)S(1)}, u32[]{:S(2)}, u32[]{:S(2)}) async-start(f32[128,8,128]{2,1,0:T(8,128)} %bitcast.7), calls=%async_computation | async-start | bytes 1048576 | tf_op jit(solution)/shard_map/all_to_all | solution.py:32
  16.0 1.0 fusion.26
  17.2 0.2 copy.123
  17.4 2.8 %fusion.3 = (bf16[8,1,8,16384]{3,2,1,0:T(8,128)(2,1)S(1)}, bf16[8,1,8,16384]{3,2,1,0:T(8,128)(2,1)S(1)}) fusion(f32[8,16384]{1,0:T(8,128)S(1)} %fusion.12, f32[8,8,128]{2,1,0:T(8,128)S(1)} %get-tuple-element.32, f32[8,8,128]{1,2,0:T(8,128)S(1)} %copy.123, f32[8,8,128]{2,1,0:T(8,128)S(1)} %get-tuple-element.33, f32[8,8,128]{1,2,0:T(8,128)S(1)} %copy.122, ...), kind=kLoop, calls=%fused_computation.8 | loop fusion | flops 12582912 | bytes 4849728 | tf_op jit(solution)/shard_map/convert
  20.3 2.3 %maximum_bitcast_fusion.table_ref = bf16[8,16,16384]{2,1,0:T(8,128)(2,1)} fusion(bf16[8,1,8,16384]{3,2,1,0:T(8,128)(2,1)S(1)} %get-tuple-element.25, bf16[8,1,8,16384]{3,2,1,0:T(8,128)(2,1)S(1)} %get-tuple-element.24), kind=kLoop, calls=%fused_computation.2 | loop fusion | flops 2097152 | bytes 8388608 | tf_op jit(solution)/shard_map/convert_element_type | solution.py:69
  22.7 0.2 broadcast_in_dim.28
  22.9 0.2 broadcast_in_dim.29
  23.2 2.2 %fusion.6 = bf16[8,8,128,128]{2,3,1,0:T(8,128)(2,1)} fusion(bf16[8,8,64,64]{2,3,1,0:T(8,128)(2,1)S(1)} %broadcast_in_dim.29, bf16[8,8,64,64]{2,3,1,0:T(8,128)(2,1)S(1)} %broadcast_in_dim.28), kind=kLoop, calls=%fused_computation.11 | loop fusion | flops 8388608 | bytes 3145728 | tf_op jit(solution)/shard_map/concatenate | solution.py:79
  25.4 4.2 %all-to-all-done = f32[128,8,128]{2,1,0:T(8,128)S(1)} async-done(((f32[128,8,128]{2,1,0:T(8,128)}), f32[128,8,128]{2,1,0:T(8,128)S(1)}, u32[]{:S(2)}, u32[]{:S(2)}) %all-to-all-start) | async-done | bytes 524320 | tf_op jit(solution)/shard_map/all_to_all | solution.py:32
  29.8 0.8 copy.126.coeff_ref
  30.5 48.9 %shard_map.121 = bf16[8,64,16]{2,1,0:T(8,128)(2,1)} custom-call(s32[8,256]{1,0:T(8,128)} %index_ref.1, bf16[8,64,16]{2,1,0:T(8,128)(2,1)} %copy.126.coeff_ref, bf16[8,16,16384]{2,1,0:T(8,128)(2,1)} %maximum_bitcast_fusion.table_ref, bf16[64,128,128]{2,1,0:T(8,128)(2,1)} %bitcast.92), custom_call_target="tpu_custom_call" | custom-call | tf_op jit(solution)/shard_map/pallas_call | solution.py:162
  79.4 1.0 copy.127
  80.6 0.7 broadcast_in_dim.30
  81.3 5.5 %all-to-all-start.1 = ((bf16[128,8,128]{2,1,0:T(8,128)(2,1)}), bf16[128,8,128]{2,1,0:T(8,128)(2,1)S(1)}, u32[]{:S(2)}, u32[]{:S(2)}) async-start(bf16[128,8,128]{2,1,0:T(8,128)(2,1)} %bitcast.27), calls=%async_computation.1 | async-start | bytes 524288 | tf_op jit(solution)/shard_map/all_to_all | solution.py:42
  87.0 0.6 multiply_reduce_fusion.2
  87.6 10.5 %all-to-all-done.1 = bf16[128,8,128]{2,1,0:T(8,128)(2,1)S(1)} async-done(((bf16[128,8,128]{2,1,0:T(8,128)(2,1)}), bf16[128,8,128]{2,1,0:T(8,128)(2,1)S(1)}, u32[]{:S(2)}, u32[]{:S(2)}) %all-to-all-start.1) | async-done | bytes 262176 | tf_op jit(solution)/shard_map/all_to_all | solution.py:42
  98.2 0.2 bitcast_multiply_fusion.2
  98.5 0.4 multiply_reduce_fusion.1
  99.2 13.6 %all_to_all.21 = f32[128,1,128]{2,1,0:T(1,128)S(1)} all-to-all(f32[128,1,128]{2,1,0:T(1,128)S(1)} %reshape.344), channel_id=1, replica_groups=mesh['mgrp'=8,'band'=16] {'mgrp','band'}, dimensions={0} | all-to-all | bytes 131072 | tf_op jit(solution)/shard_map/all_to_all | solution.py:23
  112.8 0.5 broadcast.213
  113.3 0.8 reduce.1
  114.4 0.2 multiply_reduce_fusion
  114.6 0.7 broadcast_in_dim.33
  115.3 4.5 %all-to-all-start.3 = ((f32[128,1,64]{2,1,0:T(1,128)}), f32[128,1,64]{2,1,0:T(1,128)S(1)}, u32[]{:S(2)}, u32[]{:S(2)}) async-start(f32[128,1,64]{2,1,0:T(1,128)} %broadcast_in_dim.33), calls=%async_computation.3 | async-start | bytes 131072 | tf_op jit(solution)/shard_map/all_to_all | solution.py:23
  119.8 1.0 copy.140
  120.8 8.6 %all-to-all-done.3 = f32[128,1,64]{2,1,0:T(1,128)S(1)} async-done(((f32[128,1,64]{2,1,0:T(1,128)}), f32[128,1,64]{2,1,0:T(1,128)S(1)}, u32[]{:S(2)}, u32[]{:S(2)}) %all-to-all-start.3) | async-done | bytes 32800 | tf_op jit(solution)/shard_map/all_to_all | solution.py:23
  129.6 1.0 copy.139
  130.6 1.0 copy.141
  (49 shorter events, 2.3 us)
Async XLA Ops:
  0.6 2.1 %copy-start = (bf16[1,1024,512]{2,1,0:T(8,128)(2,1)S(1)}, bf16[1,1024,512]{2,1,0:T(8,128)(2,1)}, u32[]{:S(2)}) copy-start(bf16[1,1024,512]{2,1,0:T(8,128)(2,1)} %param.15) | copy-start | bytes 3145732
  0.6 15.1 %copy-start.6 = (s32[8]{0:T(128)S(1)}, s32[8]{0:T(128)}, u32[]{:S(2)}) copy-start(s32[8]{0:T(128)} %param.19) | copy-start | bytes 100
  0.7 15.3 %copy-start.7 = (s32[8]{0:T(128)S(1)}, s32[8]{0:T(128)}, u32[]{:S(2)}) copy-start(s32[8]{0:T(128)} %param.20) | copy-start | bytes 100
  4.3 25.4 %all-to-all-start = ((f32[128,8,128]{2,1,0:T(8,128)}), f32[128,8,128]{2,1,0:T(8,128)S(1)}, u32[]{:S(2)}, u32[]{:S(2)}) async-start(f32[128,8,128]{2,1,0:T(8,128)} %bitcast.7), calls=%async_computation | async-start | bytes 1048576 | tf_op jit(solution)/shard_map/all_to_all | solution.py:32
  20.2 2.3 %copy-start.4 = (bf16[8,64,64]{2,1,0:T(8,128)(2,1)S(1)}, bf16[8,64,64]{2,1,0:T(8,128)(2,1)}, u32[]{:S(2)}) copy-start(bf16[8,64,64]{2,1,0:T(8,128)(2,1)} %param.17) | copy-start | bytes 196612
  25.4 61.7 %copy-start.2 = (f32[2,64,1,512]{3,2,1,0:T(1,128)S(1)}, f32[2,64,1,512]{3,2,1,0:T(1,128)}, u32[]{:S(2)}) copy-start(f32[2,64,1,512]{3,2,1,0:T(1,128)} %param.13) | copy-start | bytes 786436
  30.5 68.0 %copy-start.1 = (f32[2,64,1,512]{3,2,1,0:T(1,128)S(1)}, f32[2,64,1,512]{3,2,1,0:T(1,128)}, u32[]{:S(2)}) copy-start(f32[2,64,1,512]{3,2,1,0:T(1,128)} %param.14) | copy-start | bytes 786436
  30.5 68.0 %copy-start.5 = (f32[512]{0:T(512)S(1)}, f32[512]{0:T(512)}, u32[]{:S(2)}) copy-start(f32[512]{0:T(512)} %param.16) | copy-start | bytes 6148
  79.4 50.1 %copy-start.3 = (f32[2,64,1,512]{3,2,1,0:T(1,128)S(1)}, f32[2,64,1,512]{3,2,1,0:T(1,128)}, u32[]{:S(2)}) copy-start(f32[2,64,1,512]{3,2,1,0:T(1,128)} %param.12) | copy-start | bytes 786436
  81.3 16.8 %all-to-all-start.1 = ((bf16[128,8,128]{2,1,0:T(8,128)(2,1)}), bf16[128,8,128]{2,1,0:T(8,128)(2,1)S(1)}, u32[]{:S(2)}, u32[]{:S(2)}) async-start(bf16[128,8,128]{2,1,0:T(8,128)(2,1)} %bitcast.27), calls=%async_computation.1 | async-start | bytes 524288 | tf_op jit(solution)/shard_map/all_to_all | solution.py:42
  115.3 14.0 %all-to-all-start.3 = ((f32[128,1,64]{2,1,0:T(1,128)}), f32[128,1,64]{2,1,0:T(1,128)S(1)}, u32[]{:S(2)}, u32[]{:S(2)}) async-start(f32[128,1,64]{2,1,0:T(1,128)} %broadcast_in_dim.33), calls=%async_computation.3 | async-start | bytes 131072 | tf_op jit(solution)/shard_map/all_to_all | solution.py:23

commit v3 on v2

--- a/solution.py
+++ b/solution.py
@@ -102,7 +102,7 @@
     return backward.reshape(cycle_count, mode_count, columns).astype(jnp.bfloat16)
 
 
-def noise_kernel(index_ref, coeff_ref, table_ref, pair_ref, back_ref, noisy_ref, *, weight):
+def noise_kernel(index_ref, coeff_ref, table_ref, pair_ref, back_ref, noisy_ref):
     cycle = pl.program_id(0)
     span = 1024
     pair_width = 2 * BLK
@@ -123,9 +123,9 @@
                 pair_ref[pick],
                 preferred_element_type=jnp.float32,
             )
-            noisy_ref[:, pl.ds(start + inner * pair_width, pair_width)] = (
-                weight * noisy
-            ).astype(jnp.bfloat16)
+            noisy_ref[:, pl.ds(start + inner * pair_width, pair_width)] = noisy.astype(
+                jnp.bfloat16
+            )
         return carry
 
     lax.fori_loop(0, table_ref.shape[2] // span, chunk, 0)
@@ -147,7 +147,7 @@
         .transpose(0, 3, 2, 1)
         .reshape(cycle_count, map_count, 2 * mode_count)
     )
-    pairs_t = jnp.swapaxes(pair_table(noise_mats), 1, 2)
+    pairs_t = jnp.swapaxes(pair_table(noise_mats), 1, 2) * jnp.asarray(weight, jnp.bfloat16)
     grid_spec = pltpu.PrefetchScalarGridSpec(
         num_scalar_prefetch=1,
         grid=(cycle_count,),
@@ -160,7 +160,7 @@
         scratch_shapes=[pltpu.VMEM((map_count, RLEN), jnp.bfloat16)],
     )
     back = pl.pallas_call(
-        functools.partial(noise_kernel, weight=weight),
+        noise_kernel,
         grid_spec=grid_spec,
         out_shape=jax.ShapeDtypeStruct((cycle_count, map_count, 2 * mode_count), jnp.bfloat16),
     )(indices, coeff_t, tables, pairs_t)
@@ -210,17 +210,19 @@
     )
     image_data = image_data.reshape(2, map_count, mode_local, l_local)
     image_field = prior_inv[None, None, None, :] * direction + image_data
-    norm_now, curvature = total_over_mesh(
+    norm_now, curvature, cross, image_norm = total_over_mesh(
         jnp.stack(
             [
                 jnp.sum(residual * residual, axis=(0, 2, 3)),
                 jnp.sum(direction * image_field, axis=(0, 2, 3)),
+                jnp.sum(residual * image_field, axis=(0, 2, 3)),
+                jnp.sum(image_field * image_field, axis=(0, 2, 3)),
             ]
         )
     )
     step_size = norm_now / curvature
     new_residual = residual - step_size[None, :, None, None] * image_field
-    norm_next = total_over_mesh(jnp.sum(new_residual * new_residual, axis=(0, 2, 3)))
+    norm_next = norm_now - 2.0 * step_size * cross + step_size * step_size * image_norm
     growth = norm_next / norm_now
     new_solution = solution + step_size[None, :, None, None] * direction
     new_direction = new_residual + growth[None, :, None, None] * direction

time: 132 us -> 119 us (0.902)
  waiting for transfers between devices: 23.3 us -> 14.6 us
  starting transfers between devices: 21.5 us -> 17.2 us
    all_to_all x1 -> x0, waiting for transfers between devices: 8.57 us -> none  [total_over_mesh(): return jnp.sum(lax.all_to_all(copies, MESH_AXES, 0, 0, tiled=True), axis=0)]
    all_to_all x1 -> x0, starting transfers between devices: 4.48 us -> none  [total_over_mesh(): return jnp.sum(lax.all_to_all(copies, MESH_AXES, 0, 0, tiled=True), axis=0)]
    mul x0 -> x1, other arithmetic: none -> 2.32 us  [cycle_transform(): jnp.swapaxes(pair_table(noise_mats), 1, 2)]
    concatenate x1 -> x0, other arithmetic: 2.19 us -> none  [pair_table(): jnp.concatenate([upper, lower], axis=2)]
  transfers between devices with their start and end apart: 3 -> 2, of which waited for: 3 -> 2; matrix products, arithmetic and copies ran while one was open for 9% -> 9% of each run, Pallas kernels for 0% -> 0%
where the time goes in v3:
time: 119 us; the launch traced here: 118 us
  Pallas kernels  48.8 us (41%)
  starting transfers between devices  17.2 us (14%)
  waiting for transfers between devices  14.6 us (12%)
  blocking collectives  14.2 us (12%)
  other arithmetic  12.6 us (11%)
  local copies, waits for them, and re-layouts  9.25 us (8%)
    pallas_call x1, Pallas kernels, cycle_transform(): pl.pallas_call(noise_kernel, grid_spec=grid_spec, out_shape=jax.ShapeDtyp...  48.8 us
    all_to_all x1, blocking collectives, total_over_mesh(): return jnp.sum(lax.all_to_all(copies, MESH_AXES, 0, 0, tiled=True), axis=0)  14.2 us
    all_to_all x1, starting transfers between devices, gather_cycles(): received = lax.all_to_all(pieces, MESH_AXES, 0, 0, tiled=True)  11.5 us
    all_to_all x1, waiting for transfers between devices, spread_cycles(): received = lax.all_to_all(pieces, MESH_AXES, 0, 0, tiled=True)  10.5 us
    all_to_all x1, starting transfers between devices, spread_cycles(): received = lax.all_to_all(pieces, MESH_AXES, 0, 0, tiled=True)  5.66 us
    all_to_all x1, waiting for transfers between devices, gather_cycles(): received = lax.all_to_all(pieces, MESH_AXES, 0, 0, tiled=True)  4.1 us
    unnamed x23, local copies, waits for them, and re-layouts  3.5 us
    another operation x1, other arithmetic  2.81 us
  transfers between devices with their start and end apart: 2, of which 2 were waited for; matrix products, arithmetic and copies ran while one was open for 9% of the time, Pallas kernels for 0%

profile of v3, /device:TPU:1, one launch (start us, length us, event | category | flops | bytes accessed | tf_op | source)
XLA Modules:
  0.0 118.5 jit_solution(13117409667384904286)
XLA Ops:
  0.7 0.8 convert_bitcast_fusion.1
  1.6 1.1 convert_element_type.63
  2.7 0.5 fusion.9
  3.2 0.2 copy.123
  3.4 0.8 copy.124
  4.3 11.5 %all-to-all-start = ((f32[128,8,128]{2,1,0:T(8,128)}), f32[128,8,128]{2,1,0:T(8,128)S(1)}, u32[]{:S(2)}, u32[]{:S(2)}) async-start(f32[128,8,128]{2,1,0:T(8,128)} %bitcast.7), calls=%async_computation | async-start | bytes 1048576 | tf_op jit(solution)/shard_map/all_to_all | solution.py:32
  16.0 1.0 fusion.27
  17.0 0.2 copy.127
  17.2 0.2 copy.128
  17.4 2.8 %fusion.3 = (bf16[8,1,8,16384]{3,2,1,0:T(8,128)(2,1)S(1)}, bf16[8,1,8,16384]{3,2,1,0:T(8,128)(2,1)S(1)}) fusion(f32[8,16384]{1,0:T(8,128)S(1)} %fusion.13, f32[8,8,128]{2,1,0:T(8,128)S(1)} %get-tuple-element.36, f32[8,8,128]{1,2,0:T(8,128)S(1)} %copy.128, f32[8,8,128]{2,1,0:T(8,128)S(1)} %get-tuple-element.37, f32[8,8,128]{1,2,0:T(8,128)S(1)} %copy.127, ...), kind=kLoop, calls=%fused_computation.8 | loop fusion | flops 12582912 | bytes 4849728 | tf_op jit(solution)/shard_map/convert
  20.3 2.3 %maximum_bitcast_fusion.table_ref = bf16[8,16,16384]{2,1,0:T(8,128)(2,1)} fusion(bf16[8,1,8,16384]{3,2,1,0:T(8,128)(2,1)S(1)} %get-tuple-element.30, bf16[8,1,8,16384]{3,2,1,0:T(8,128)(2,1)S(1)} %get-tuple-element.29), kind=kLoop, calls=%fused_computation.2 | loop fusion | flops 2097152 | bytes 8388608 | tf_op jit(solution)/shard_map/convert_element_type | solution.py:69
  22.7 0.2 broadcast_in_dim.26
  22.9 0.2 broadcast_in_dim.27
  23.2 2.3 %fusion.7 = bf16[8,8,128,128]{2,3,1,0:T(8,128)(2,1)} fusion(bf16[8,8,64,64]{2,3,1,0:T(8,128)(2,1)S(1)} %broadcast_in_dim.27, bf16[8,8,64,64]{2,3,1,0:T(8,128)(2,1)S(1)} %broadcast_in_dim.26), kind=kLoop, calls=%fused_computation.12 | loop fusion | flops 10485760 | bytes 3145728 | tf_op jit(solution)/shard_map/mul | solution.py:150
  25.5 4.1 %all-to-all-done = f32[128,8,128]{2,1,0:T(8,128)S(1)} async-done(((f32[128,8,128]{2,1,0:T(8,128)}), f32[128,8,128]{2,1,0:T(8,128)S(1)}, u32[]{:S(2)}, u32[]{:S(2)}) %all-to-all-start) | async-done | bytes 524320 | tf_op jit(solution)/shard_map/all_to_all | solution.py:32
  29.8 0.8 copy.131.coeff_ref
  30.5 48.8 %shard_map.121 = bf16[8,64,16]{2,1,0:T(8,128)(2,1)} custom-call(s32[8,256]{1,0:T(8,128)} %index_ref.1, bf16[8,64,16]{2,1,0:T(8,128)(2,1)} %copy.131.coeff_ref, bf16[8,16,16384]{2,1,0:T(8,128)(2,1)} %maximum_bitcast_fusion.table_ref, bf16[64,128,128]{2,1,0:T(8,128)(2,1)} %bitcast.108), custom_call_target="tpu_custom_call" | custom-call | tf_op jit(solution)/shard_map/pallas_call | solution.py:162
  79.4 1.0 copy.132
  80.6 0.7 broadcast_in_dim.28
  81.3 5.7 %all-to-all-start.1 = ((bf16[128,8,128]{2,1,0:T(8,128)(2,1)}), bf16[128,8,128]{2,1,0:T(8,128)(2,1)S(1)}, u32[]{:S(2)}, u32[]{:S(2)}) async-start(bf16[128,8,128]{2,1,0:T(8,128)(2,1)} %bitcast.27), calls=%async_computation.1 | async-start | bytes 524288 | tf_op jit(solution)/shard_map/all_to_all | solution.py:42
  87.1 0.6 multiply_reduce_fusion.3
  87.7 10.5 %all-to-all-done.1 = bf16[128,8,128]{2,1,0:T(8,128)(2,1)S(1)} async-done(((bf16[128,8,128]{2,1,0:T(8,128)(2,1)}), bf16[128,8,128]{2,1,0:T(8,128)(2,1)S(1)}, u32[]{:S(2)}, u32[]{:S(2)}) %all-to-all-start.1) | async-done | bytes 262176 | tf_op jit(solution)/shard_map/all_to_all | solution.py:42
  98.2 0.2 bitcast_multiply_fusion.2
  98.6 0.5 multiply_reduce_fusion.2
  99.2 0.2 reshape.357
  99.4 14.2 %all_to_all.15 = f32[128,1,256]{2,1,0:T(1,128)S(1)} all-to-all(f32[128,1,256]{2,1,0:T(1,128)S(1)} %reshape.357), channel_id=1, replica_groups=mesh['mgrp'=8,'band'=16] {'mgrp','band'}, dimensions={0} | all-to-all | bytes 262144 | tf_op jit(solution)/shard_map/all_to_all | solution.py:23
  113.6 0.5 broadcast.218
  114.1 1.0 reduce
  115.1 0.2 reshape.358
  115.6 1.0 copy.144
  116.5 1.0 copy.145
  117.5 1.0 copy.146
  (43 shorter events, 1.5 us)
Async XLA Ops:
  0.6 2.1 %copy-start = (bf16[1,1024,512]{2,1,0:T(8,128)(2,1)S(1)}, bf16[1,1024,512]{2,1,0:T(8,128)(2,1)}, u32[]{:S(2)}) copy-start(bf16[1,1024,512]{2,1,0:T(8,128)(2,1)} %param.15) | copy-start | bytes 3145732
  0.6 15.1 %copy-start.6 = (s32[8]{0:T(128)S(1)}, s32[8]{0:T(128)}, u32[]{:S(2)}) copy-start(s32[8]{0:T(128)} %param.19) | copy-start | bytes 100
  0.7 15.3 %copy-start.7 = (s32[8]{0:T(128)S(1)}, s32[8]{0:T(128)}, u32[]{:S(2)}) copy-start(s32[8]{0:T(128)} %param.20) | copy-start | bytes 100
  4.3 25.4 %all-to-all-start = ((f32[128,8,128]{2,1,0:T(8,128)}), f32[128,8,128]{2,1,0:T(8,128)S(1)}, u32[]{:S(2)}, u32[]{:S(2)}) async-start(f32[128,8,128]{2,1,0:T(8,128)} %bitcast.7), calls=%async_computation | async-start | bytes 1048576 | tf_op jit(solution)/shard_map/all_to_all | solution.py:32
  20.3 2.3 %copy-start.4 = (bf16[8,64,64]{2,1,0:T(8,128)(2,1)S(1)}, bf16[8,64,64]{2,1,0:T(8,128)(2,1)}, u32[]{:S(2)}) copy-start(bf16[8,64,64]{2,1,0:T(8,128)(2,1)} %param.17) | copy-start | bytes 196612
  25.5 61.6 %copy-start.2 = (f32[2,64,1,512]{3,2,1,0:T(1,128)S(1)}, f32[2,64,1,512]{3,2,1,0:T(1,128)}, u32[]{:S(2)}) copy-start(f32[2,64,1,512]{3,2,1,0:T(1,128)} %param.13) | copy-start | bytes 786436
  30.5 68.1 %copy-start.1 = (f32[2,64,1,512]{3,2,1,0:T(1,128)S(1)}, f32[2,64,1,512]{3,2,1,0:T(1,128)}, u32[]{:S(2)}) copy-start(f32[2,64,1,512]{3,2,1,0:T(1,128)} %param.14) | copy-start | bytes 786436
  30.5 68.1 %copy-start.5 = (f32[512]{0:T(512)S(1)}, f32[512]{0:T(512)}, u32[]{:S(2)}) copy-start(f32[512]{0:T(512)} %param.16) | copy-start | bytes 6148
  79.4 36.0 %copy-start.3 = (f32[2,64,1,512]{3,2,1,0:T(1,128)S(1)}, f32[2,64,1,512]{3,2,1,0:T(1,128)}, u32[]{:S(2)}) copy-start(f32[2,64,1,512]{3,2,1,0:T(1,128)} %param.12) | copy-start | bytes 786436
  81.3 16.9 %all-to-all-start.1 = ((bf16[128,8,128]{2,1,0:T(8,128)(2,1)}), bf16[128,8,128]{2,1,0:T(8,128)(2,1)S(1)}, u32[]{:S(2)}, u32[]{:S(2)}) async-start(bf16[128,8,128]{2,1,0:T(8,128)(2,1)} %bitcast.27), calls=%async_computation.1 | async-start | bytes 524288 | tf_op jit(solution)/shard_map/all_to_all | solution.py:42

commit v4 on v3

--- a/solution.py
+++ b/solution.py
@@ -104,7 +104,7 @@
 
 def noise_kernel(index_ref, coeff_ref, table_ref, pair_ref, back_ref, noisy_ref):
     cycle = pl.program_id(0)
-    span = 1024
+    span = 4096
     pair_width = 2 * BLK
     coeff = coeff_ref[0]
 

time: 119 us -> 97.8 us (0.82)
  Pallas kernels: 48.8 us -> 27.8 us
    pallas_call x1, Pallas kernels: 48.8 us -> 27.8 us  [cycle_transform(): pl.pallas_call(noise_kernel, grid_spec=grid_spec, out_shape=jax.ShapeDtyp...]
  transfers between devices with their start and end apart: 2 -> 2, of which waited for: 2 -> 2; matrix products, arithmetic and copies ran while one was open for 9% -> 11% of each run, Pallas kernels for 0% -> 0%
where the time goes in v4:
time: 97.8 us; the launch traced here: 97.5 us
  Pallas kernels  27.8 us (28%)
  starting transfers between devices  17.2 us (18%)
  waiting for transfers between devices  14.6 us (15%)
  blocking collectives  14.2 us (15%)
  other arithmetic  12.6 us (13%)
  local copies, waits for them, and re-layouts  9.25 us (9%)
    pallas_call x1, Pallas kernels, cycle_transform(): pl.pallas_call(noise_kernel, grid_spec=grid_spec, out_shape=jax.ShapeDtyp...  27.8 us
    all_to_all x1, blocking collectives, total_over_mesh(): return jnp.sum(lax.all_to_all(copies, MESH_AXES, 0, 0, tiled=True), axis=0)  14.2 us
    all_to_all x1, starting transfers between devices, gather_cycles(): received = lax.all_to_all(pieces, MESH_AXES, 0, 0, tiled=True)  11.5 us
    all_to_all x1, waiting for transfers between devices, spread_cycles(): received = lax.all_to_all(pieces, MESH_AXES, 0, 0, tiled=True)  10.5 us
    all_to_all x1, starting transfers between devices, spread_cycles(): received = lax.all_to_all(pieces, MESH_AXES, 0, 0, tiled=True)  5.66 us
    all_to_all x1, waiting for transfers between devices, gather_cycles(): received = lax.all_to_all(pieces, MESH_AXES, 0, 0, tiled=True)  4.1 us
    unnamed x23, local copies, waits for them, and re-layouts  3.5 us
    another operation x1, other arithmetic  2.81 us
  transfers between devices with their start and end apart: 2, of which 2 were waited for; matrix products, arithmetic and copies ran while one was open for 11% of the time, Pallas kernels for 0%

profile of v4, /device:TPU:1, one launch (start us, length us, event | category | flops | bytes accessed | tf_op | source)
XLA Modules:
  0.0 97.5 jit_solution(17715863301467628531)
XLA Ops:
  0.7 0.8 convert_bitcast_fusion.1
  1.6 1.1 %convert_element_type.63 = bf16[2,64,1,512]{3,2,1,0:T(2,128)(2,1)S(1)} convert(f32[2,64,1,512]{3,2,1,0:T(1,128)} %param.14) | non-fusion elementwise | flops 65536 | bytes 393216 | tf_op jit(solution)/shard_map/convert_element_type | solution.py:192
  2.7 0.5 fusion.9
  3.2 0.2 copy.123
  3.4 0.8 copy.124
  4.3 11.5 %all-to-all-start = ((f32[128,8,128]{2,1,0:T(8,128)}), f32[128,8,128]{2,1,0:T(8,128)S(1)}, u32[]{:S(2)}, u32[]{:S(2)}) async-start(f32[128,8,128]{2,1,0:T(8,128)} %bitcast.7), calls=%async_computation | async-start | bytes 1048576 | tf_op jit(solution)/shard_map/all_to_all | solution.py:32
  16.0 1.0 %fusion.27 = (f32[8,8,128]{2,1,0:T(8,128)S(1)}, f32[8,8,128]{2,1,0:T(8,128)S(1)}, f32[8,8,128]{2,1,0:T(8,128)S(1)}, f32[8,8,128]{2,1,0:T(8,128)S(1)}) fusion(f32[8]{0:T(128)S(1)} %convert_element_type.70, pred[8]{0:T(512)(128)(4,1)S(1)} %compare_bitcast_fusion, s32[8]{0:T(128)S(1)} %fusion.31, s32[8,128]{1,0:T(8,128)S(1)} %get-tuple-element.42, ...), kind=kLoop, calls=%fused_computation.54 | loop fusion | flops 163840 | bytes 139336 | tf_op jit(solution)/shard_map/cos | solution.py:56
  17.0 0.2 copy.127
  17.2 0.2 copy.128
  17.4 2.8 %fusion.3 = (bf16[8,1,8,16384]{3,2,1,0:T(8,128)(2,1)S(1)}, bf16[8,1,8,16384]{3,2,1,0:T(8,128)(2,1)S(1)}) fusion(f32[8,16384]{1,0:T(8,128)S(1)} %fusion.13, f32[8,8,128]{2,1,0:T(8,128)S(1)} %get-tuple-element.36, f32[8,8,128]{1,2,0:T(8,128)S(1)} %copy.128, f32[8,8,128]{2,1,0:T(8,128)S(1)} %get-tuple-element.37, f32[8,8,128]{1,2,0:T(8,128)S(1)} %copy.127, ...), kind=kLoop, calls=%fused_computation.8 | loop fusion | flops 12582912 | bytes 4849728 | tf_op jit(solution)/shard_map/convert
  20.3 2.3 %maximum_bitcast_fusion.table_ref = bf16[8,16,16384]{2,1,0:T(8,128)(2,1)} fusion(bf16[8,1,8,16384]{3,2,1,0:T(8,128)(2,1)S(1)} %get-tuple-element.30, bf16[8,1,8,16384]{3,2,1,0:T(8,128)(2,1)S(1)} %get-tuple-element.29), kind=kLoop, calls=%fused_computation.2 | loop fusion | flops 2097152 | bytes 8388608 | tf_op jit(solution)/shard_map/convert_element_type | solution.py:69
  22.7 0.2 broadcast_in_dim.26
  22.9 0.2 broadcast_in_dim.27
  23.2 2.3 %fusion.7 = bf16[8,8,128,128]{2,3,1,0:T(8,128)(2,1)} fusion(bf16[8,8,64,64]{2,3,1,0:T(8,128)(2,1)S(1)} %broadcast_in_dim.27, bf16[8,8,64,64]{2,3,1,0:T(8,128)(2,1)S(1)} %broadcast_in_dim.26), kind=kLoop, calls=%fused_computation.12 | loop fusion | flops 10485760 | bytes 3145728 | tf_op jit(solution)/shard_map/mul | solution.py:150
  25.5 4.1 %all-to-all-done = f32[128,8,128]{2,1,0:T(8,128)S(1)} async-done(((f32[128,8,128]{2,1,0:T(8,128)}), f32[128,8,128]{2,1,0:T(8,128)S(1)}, u32[]{:S(2)}, u32[]{:S(2)}) %all-to-all-start) | async-done | bytes 524320 | tf_op jit(solution)/shard_map/all_to_all | solution.py:32
  29.8 0.8 copy.131.coeff_ref
  30.5 27.8 %shard_map.121 = bf16[8,64,16]{2,1,0:T(8,128)(2,1)} custom-call(s32[8,256]{1,0:T(8,128)} %index_ref.1, bf16[8,64,16]{2,1,0:T(8,128)(2,1)} %copy.131.coeff_ref, bf16[8,16,16384]{2,1,0:T(8,128)(2,1)} %maximum_bitcast_fusion.table_ref, bf16[64,128,128]{2,1,0:T(8,128)(2,1)} %bitcast.108), custom_call_target="tpu_custom_call" | custom-call | tf_op jit(solution)/shard_map/pallas_call | solution.py:162
  58.4 1.0 %copy.132 = bf16[8,64,16]{1,2,0:T(8,128)(2,1)S(1)} copy(bf16[8,64,16]{2,1,0:T(8,128)(2,1)} %shard_map.121) | data formatting | bytes 32768 | tf_op jit(solution)/shard_map/pallas_call | solution.py:162
  59.5 0.7 broadcast_in_dim.28
  60.3 5.7 %all-to-all-start.1 = ((bf16[128,8,128]{2,1,0:T(8,128)(2,1)}), bf16[128,8,128]{2,1,0:T(8,128)(2,1)S(1)}, u32[]{:S(2)}, u32[]{:S(2)}) async-start(bf16[128,8,128]{2,1,0:T(8,128)(2,1)} %bitcast.27), calls=%async_computation.1 | async-start | bytes 524288 | tf_op jit(solution)/shard_map/all_to_all | solution.py:42
  66.1 0.6 multiply_reduce_fusion.3
  66.7 10.5 %all-to-all-done.1 = bf16[128,8,128]{2,1,0:T(8,128)(2,1)S(1)} async-done(((bf16[128,8,128]{2,1,0:T(8,128)(2,1)}), bf16[128,8,128]{2,1,0:T(8,128)(2,1)S(1)}, u32[]{:S(2)}, u32[]{:S(2)}) %all-to-all-start.1) | async-done | bytes 262176 | tf_op jit(solution)/shard_map/all_to_all | solution.py:42
  77.2 0.2 bitcast_multiply_fusion.2
  77.6 0.5 multiply_reduce_fusion.2
  78.2 0.2 reshape.357
  78.4 14.2 %all_to_all.15 = f32[128,1,256]{2,1,0:T(1,128)S(1)} all-to-all(f32[128,1,256]{2,1,0:T(1,128)S(1)} %reshape.357), channel_id=1, replica_groups=mesh['mgrp'=8,'band'=16] {'mgrp','band'}, dimensions={0} | all-to-all | bytes 262144 | tf_op jit(solution)/shard_map/all_to_all | solution.py:23
  92.6 0.5 broadcast.218
  93.1 1.0 reduce
  94.1 0.2 reshape.358
  94.5 1.0 copy.144
  95.5 1.0 copy.145
  96.5 1.0 copy.146
  (43 shorter events, 1.5 us)
Async XLA Ops:
  0.6 2.1 %copy-start = (bf16[1,1024,512]{2,1,0:T(8,128)(2,1)S(1)}, bf16[1,1024,512]{2,1,0:T(8,128)(2,1)}, u32[]{:S(2)}) copy-start(bf16[1,1024,512]{2,1,0:T(8,128)(2,1)} %param.15) | copy-start | bytes 3145732
  0.6 15.1 %copy-start.6 = (s32[8]{0:T(128)S(1)}, s32[8]{0:T(128)}, u32[]{:S(2)}) copy-start(s32[8]{0:T(128)} %param.19) | copy-start | bytes 100
  0.7 15.3 %copy-start.7 = (s32[8]{0:T(128)S(1)}, s32[8]{0:T(128)}, u32[]{:S(2)}) copy-start(s32[8]{0:T(128)} %param.20) | copy-start | bytes 100
  4.3 25.4 %all-to-all-start = ((f32[128,8,128]{2,1,0:T(8,128)}), f32[128,8,128]{2,1,0:T(8,128)S(1)}, u32[]{:S(2)}, u32[]{:S(2)}) async-start(f32[128,8,128]{2,1,0:T(8,128)} %bitcast.7), calls=%async_computation | async-start | bytes 1048576 | tf_op jit(solution)/shard_map/all_to_all | solution.py:32
  20.3 2.3 %copy-start.4 = (bf16[8,64,64]{2,1,0:T(8,128)(2,1)S(1)}, bf16[8,64,64]{2,1,0:T(8,128)(2,1)}, u32[]{:S(2)}) copy-start(bf16[8,64,64]{2,1,0:T(8,128)(2,1)} %param.17) | copy-start | bytes 196612
  25.5 40.6 %copy-start.2 = (f32[2,64,1,512]{3,2,1,0:T(1,128)S(1)}, f32[2,64,1,512]{3,2,1,0:T(1,128)}, u32[]{:S(2)}) copy-start(f32[2,64,1,512]{3,2,1,0:T(1,128)} %param.13) | copy-start | bytes 786436
  30.5 47.1 %copy-start.1 = (f32[2,64,1,512]{3,2,1,0:T(1,128)S(1)}, f32[2,64,1,512]{3,2,1,0:T(1,128)}, u32[]{:S(2)}) copy-start(f32[2,64,1,512]{3,2,1,0:T(1,128)} %param.14) | copy-start | bytes 786436
  30.5 47.1 %copy-start.5 = (f32[512]{0:T(512)S(1)}, f32[512]{0:T(512)}, u32[]{:S(2)}) copy-start(f32[512]{0:T(512)} %param.16) | copy-start | bytes 6148
  58.4 36.0 %copy-start.3 = (f32[2,64,1,512]{3,2,1,0:T(1,128)S(1)}, f32[2,64,1,512]{3,2,1,0:T(1,128)}, u32[]{:S(2)}) copy-start(f32[2,64,1,512]{3,2,1,0:T(1,128)} %param.12) | copy-start | bytes 786436
  60.3 16.9 %all-to-all-start.1 = ((bf16[128,8,128]{2,1,0:T(8,128)(2,1)}), bf16[128,8,128]{2,1,0:T(8,128)(2,1)S(1)}, u32[]{:S(2)}, u32[]{:S(2)}) async-start(bf16[128,8,128]{2,1,0:T(8,128)(2,1)} %bitcast.27), calls=%async_computation.1 | async-start | bytes 524288 | tf_op jit(solution)/shard_map/all_to_all | solution.py:42

commit v5 on v4

--- a/solution.py
+++ b/solution.py
@@ -102,39 +102,33 @@
     return backward.reshape(cycle_count, mode_count, columns).astype(jnp.bfloat16)
 
 
-def noise_kernel(index_ref, coeff_ref, table_ref, pair_ref, back_ref, noisy_ref):
+def noise_kernel(index_ref, length_ref, coeff_ref, table_ref, pair_ref, back_ref, noisy_ref):
     cycle = pl.program_id(0)
-    span = 4096
+    span = noisy_ref.shape[1]
     pair_width = 2 * BLK
     coeff = coeff_ref[0]
-
-    def chunk(step, carry):
+    side = int(round(pair_ref.shape[0] ** 0.5))
+
+    def chunk(step, total):
         start = pl.multiple_of(step * span, span)
-        sky = jnp.dot(
-            coeff, table_ref[0, :, pl.ds(start, span)], preferred_element_type=jnp.float32
-        ).astype(jnp.bfloat16)
+        table = table_ref[0, :, pl.ds(start, span)]
+        sky = jnp.dot(coeff, table, preferred_element_type=jnp.float32).astype(jnp.bfloat16)
         for inner in range(span // pair_width):
             block = (start + inner * pair_width) // BLK
-            kinds = pair_ref.shape[0]
-            side = int(round(kinds ** 0.5))
             pick = index_ref[cycle, block] * side + index_ref[cycle, block + 1]
             noisy = jnp.dot(
                 sky[:, inner * pair_width:(inner + 1) * pair_width],
                 pair_ref[pick],
                 preferred_element_type=jnp.float32,
             )
-            noisy_ref[:, pl.ds(start + inner * pair_width, pair_width)] = noisy.astype(
-                jnp.bfloat16
-            )
-        return carry
-
-    lax.fori_loop(0, table_ref.shape[2] // span, chunk, 0)
-    back_ref[0] = lax.dot_general(
-        noisy_ref[...],
-        table_ref[0],
-        (((1,), (1,)), ((), ())),
-        preferred_element_type=jnp.float32,
-    ).astype(back_ref.dtype)
+            noisy_ref[:, inner * pair_width:(inner + 1) * pair_width] = noisy.astype(jnp.bfloat16)
+        return total + lax.dot_general(
+            noisy_ref[...], table, (((1,), (1,)), ((), ())), preferred_element_type=jnp.float32
+        )
+
+    used = (length_ref[cycle] + span - 1) // span
+    total = lax.fori_loop(0, used, chunk, jnp.zeros(back_ref.shape[1:], jnp.float32))
+    back_ref[0] = total.astype(back_ref.dtype)
 
 
 def cycle_transform(coeffs, lengths, indices, m_values, noise_mats, weight):
@@ -149,21 +143,21 @@
     )
     pairs_t = jnp.swapaxes(pair_table(noise_mats), 1, 2) * jnp.asarray(weight, jnp.bfloat16)
     grid_spec = pltpu.PrefetchScalarGridSpec(
-        num_scalar_prefetch=1,
+        num_scalar_prefetch=2,
         grid=(cycle_count,),
         in_specs=[
-            pl.BlockSpec((1, map_count, 2 * mode_count), lambda r, idx: (r, 0, 0)),
-            pl.BlockSpec((1, 2 * mode_count, RLEN), lambda r, idx: (r, 0, 0)),
-            pl.BlockSpec(pairs_t.shape, lambda r, idx: (0, 0, 0)),
+            pl.BlockSpec((1, map_count, 2 * mode_count), lambda r, idx, n: (r, 0, 0)),
+            pl.BlockSpec((1, 2 * mode_count, RLEN), lambda r, idx, n: (r, 0, 0)),
+            pl.BlockSpec(pairs_t.shape, lambda r, idx, n: (0, 0, 0)),
         ],
-        out_specs=pl.BlockSpec((1, map_count, 2 * mode_count), lambda r, idx: (r, 0, 0)),
-        scratch_shapes=[pltpu.VMEM((map_count, RLEN), jnp.bfloat16)],
+        out_specs=pl.BlockSpec((1, map_count, 2 * mode_count), lambda r, idx, n: (r, 0, 0)),
+        scratch_shapes=[pltpu.VMEM((map_count, 4096), jnp.bfloat16)],
     )
     back = pl.pallas_call(
         noise_kernel,
         grid_spec=grid_spec,
         out_shape=jax.ShapeDtypeStruct((cycle_count, map_count, 2 * mode_count), jnp.bfloat16),
-    )(indices, coeff_t, tables, pairs_t)
+    )(indices, lengths, coeff_t, tables, pairs_t)
     return (
         back.reshape(cycle_count, map_count, 2, mode_count)
         .transpose(0, 3, 2, 1)

time: 97.8 us -> 92.8 us (0.949)
  Pallas kernels: 27.8 us -> 20.5 us
  starting transfers between devices: 17.2 us -> 19.7 us
    pallas_call x1, Pallas kernels: 27.8 us -> 20.5 us  [cycle_transform(): pl.pallas_call(noise_kernel, grid_spec=grid_spec, out_shape=jax.ShapeDtyp...]
    all_to_all x1, starting transfers between devices: 5.66 us -> 8.27 us  [spread_cycles(): received = lax.all_to_all(pieces, MESH_AXES, 0, 0, tiled=True)]
where the time goes in v5:
time: 92.8 us
  Pallas kernels  20.5 us (22%)
  starting transfers between devices  19.7 us (21%)
  waiting for transfers between devices  14.6 us (16%)
  blocking collectives  14.2 us (15%)
  other arithmetic  12.6 us (14%)
  local copies, waits for them, and re-layouts  9.25 us (10%)
  matrix products  0.95 us (1%)
  between operations  0.94 us (1%)
    pallas_call x1, Pallas kernels, cycle_transform(): pl.pallas_call(noise_kernel, grid_spec=grid_spec, out_shape=jax.ShapeDtyp...  20.5 us
    all_to_all x1, blocking collectives, total_over_mesh(): return jnp.sum(lax.all_to_all(copies, MESH_AXES, 0, 0, tiled=True), axis=0)  14.2 us
    all_to_all x1, starting transfers between devices, gather_cycles(): received = lax.all_to_all(pieces, MESH_AXES, 0, 0, tiled=True)  11.5 us
    all_to_all x1, waiting for transfers between devices, spread_cycles(): received = lax.all_to_all(pieces, MESH_AXES, 0, 0, tiled=True)  10.5 us
    all_to_all x1, starting transfers between devices, spread_cycles(): received = lax.all_to_all(pieces, MESH_AXES, 0, 0, tiled=True)  8.27 us
    all_to_all x1, waiting for transfers between devices, gather_cycles(): received = lax.all_to_all(pieces, MESH_AXES, 0, 0, tiled=True)  4.1 us
    unnamed x23, local copies, waits for them, and re-layouts  3.5 us
    another operation x1, other arithmetic  2.81 us
  transfers between devices with their start and end apart: 2, of which 2 were waited for; matrix products, arithmetic and copies ran while one was open for 11% of the time, Pallas kernels for 0%

profile of v5, /device:TPU:1, one launch (start us, length us, event | category | flops | bytes accessed | tf_op | source)
XLA Modules:
  0.0 92.8 jit_solution(7618555468848827992)
XLA Ops:
  0.7 0.8 convert_bitcast_fusion.1
  1.6 1.1 %convert_element_type.63 = bf16[2,64,1,512]{3,2,1,0:T(2,128)(2,1)S(1)} convert(f32[2,64,1,512]{3,2,1,0:T(1,128)} %param.14) | non-fusion elementwise | flops 65536 | bytes 393216 | tf_op jit(solution)/shard_map/convert_element_type | solution.py:186
  2.7 0.5 fusion.9
  3.2 0.2 copy.123
  3.4 0.8 copy.124
  4.3 11.5 %all-to-all-start = ((f32[128,8,128]{2,1,0:T(8,128)}), f32[128,8,128]{2,1,0:T(8,128)S(1)}, u32[]{:S(2)}, u32[]{:S(2)}) async-start(f32[128,8,128]{2,1,0:T(8,128)} %bitcast.7), calls=%async_computation | async-start | bytes 1048576 | tf_op jit(solution)/shard_map/all_to_all | solution.py:32
  16.0 1.0 %fusion.27 = (f32[8,8,128]{2,1,0:T(8,128)S(1)}, f32[8,8,128]{2,1,0:T(8,128)S(1)}, f32[8,8,128]{2,1,0:T(8,128)S(1)}, f32[8,8,128]{2,1,0:T(8,128)S(1)}) fusion(f32[8]{0:T(128)S(1)} %convert_element_type.70, pred[8]{0:T(512)(128)(4,1)S(1)} %compare_bitcast_fusion, s32[8]{0:T(128)S(1)} %fusion.31, s32[8,128]{1,0:T(8,128)S(1)} %get-tuple-element.42, ...), kind=kLoop, calls=%fused_computation.54 | loop fusion | flops 163840 | bytes 139336 | tf_op jit(solution)/shard_map/cos | solution.py:56
  17.0 0.2 copy.127
  17.2 0.2 copy.128
  17.4 2.8 %fusion.3 = (bf16[8,1,8,16384]{3,2,1,0:T(8,128)(2,1)S(1)}, bf16[8,1,8,16384]{3,2,1,0:T(8,128)(2,1)S(1)}) fusion(f32[8,16384]{1,0:T(8,128)S(1)} %fusion.13, f32[8,8,128]{2,1,0:T(8,128)S(1)} %get-tuple-element.36, f32[8,8,128]{1,2,0:T(8,128)S(1)} %copy.128, f32[8,8,128]{2,1,0:T(8,128)S(1)} %get-tuple-element.37, f32[8,8,128]{1,2,0:T(8,128)S(1)} %copy.127, ...), kind=kLoop, calls=%fused_computation.8 | loop fusion | flops 12582912 | bytes 4849728 | tf_op jit(solution)/shard_map/convert
  20.3 2.3 %maximum_bitcast_fusion.table_ref = bf16[8,16,16384]{2,1,0:T(8,128)(2,1)} fusion(bf16[8,1,8,16384]{3,2,1,0:T(8,128)(2,1)S(1)} %get-tuple-element.30, bf16[8,1,8,16384]{3,2,1,0:T(8,128)(2,1)S(1)} %get-tuple-element.29), kind=kLoop, calls=%fused_computation.2 | loop fusion | flops 2097152 | bytes 8388608 | tf_op jit(solution)/shard_map/convert_element_type | solution.py:69
  22.7 0.2 broadcast_in_dim.26
  22.9 0.2 broadcast_in_dim.27
  23.2 2.3 %fusion.7 = bf16[8,8,128,128]{2,3,1,0:T(8,128)(2,1)} fusion(bf16[8,8,64,64]{2,3,1,0:T(8,128)(2,1)S(1)} %broadcast_in_dim.27, bf16[8,8,64,64]{2,3,1,0:T(8,128)(2,1)S(1)} %broadcast_in_dim.26), kind=kLoop, calls=%fused_computation.12 | loop fusion | flops 10485760 | bytes 3145728 | tf_op jit(solution)/shard_map/mul | solution.py:144
  25.5 4.1 %all-to-all-done = f32[128,8,128]{2,1,0:T(8,128)S(1)} async-done(((f32[128,8,128]{2,1,0:T(8,128)}), f32[128,8,128]{2,1,0:T(8,128)S(1)}, u32[]{:S(2)}, u32[]{:S(2)}) %all-to-all-start) | async-done | bytes 524320 | tf_op jit(solution)/shard_map/all_to_all | solution.py:32
  29.8 0.8 copy.131.coeff_ref
  30.5 20.5 %shard_map.121 = bf16[8,64,16]{2,1,0:T(8,128)(2,1)} custom-call(s32[8,256]{1,0:T(8,128)} %index_ref.1, s32[8]{0:T(128)} %length_ref.1, bf16[8,64,16]{2,1,0:T(8,128)(2,1)} %copy.131.coeff_ref, bf16[8,16,16384]{2,1,0:T(8,128)(2,1)} %maximum_bitcast_fusion.table_ref, bf16[64,128,128]{2,1,0:T(8,128)(2,1)} %bitcast.108), custom_call_target="tpu_custom_call" | custom-call | tf_op jit(solution)/shard_map/pallas_call | solution.py:156
  51.1 1.0 %copy.132 = bf16[8,64,16]{1,2,0:T(8,128)(2,1)S(1)} copy(bf16[8,64,16]{2,1,0:T(8,128)(2,1)} %shard_map.121) | data formatting | bytes 32768 | tf_op jit(solution)/shard_map/pallas_call | solution.py:156
  52.2 0.7 broadcast_in_dim.28
  53.0 8.3 %all-to-all-start.1 = ((bf16[128,8,128]{2,1,0:T(8,128)(2,1)}), bf16[128,8,128]{2,1,0:T(8,128)(2,1)S(1)}, u32[]{:S(2)}, u32[]{:S(2)}) async-start(bf16[128,8,128]{2,1,0:T(8,128)(2,1)} %bitcast.27), calls=%async_computation.1 | async-start | bytes 524288 | tf_op jit(solution)/shard_map/all_to_all | solution.py:42
  61.4 0.6 multiply_reduce_fusion.3
  62.0 10.5 %all-to-all-done.1 = bf16[128,8,128]{2,1,0:T(8,128)(2,1)S(1)} async-done(((bf16[128,8,128]{2,1,0:T(8,128)(2,1)}), bf16[128,8,128]{2,1,0:T(8,128)(2,1)S(1)}, u32[]{:S(2)}, u32[]{:S(2)}) %all-to-all-start.1) | async-done | bytes 262176 | tf_op jit(solution)/shard_map/all_to_all | solution.py:42
  72.5 0.2 bitcast_multiply_fusion.2
  72.9 0.5 multiply_reduce_fusion.2
  73.5 0.2 reshape.357
  73.7 14.2 %all_to_all.15 = f32[128,1,256]{2,1,0:T(1,128)S(1)} all-to-all(f32[128,1,256]{2,1,0:T(1,128)S(1)} %reshape.357), channel_id=1, replica_groups=mesh['mgrp'=8,'band'=16] {'mgrp','band'}, dimensions={0} | all-to-all | bytes 262144 | tf_op jit(solution)/shard_map/all_to_all | solution.py:23
  87.9 0.5 broadcast.218
  88.4 1.0 %reduce = f32[128,256]{1,0:T(8,128)S(1)} reduce(f32[128,1,256]{2,1,0:T(1,128)S(1)} %all_to_all.15, f32[]{:T(128)} %broadcast.218), dimensions={1}, to_apply=%all_to_all.11.reduce_sub_computation | reduce | bytes 262148 | tf_op jit(solution)/shard_map/all_to_all | solution.py:23
  89.4 0.2 reshape.358
  89.9 1.0 %copy.144 = f32[2,64,1,512]{3,2,1,0:T(1,128)} copy(f32[2,64,1,512]{3,1,0,2:T(8,128)S(1)} %get-tuple-element.31) | data formatting | bytes 524288
  90.8 1.0 %copy.145 = f32[2,64,1,512]{3,2,1,0:T(1,128)} copy(f32[2,64,1,512]{3,1,0,2:T(8,128)S(1)} %get-tuple-element.26) | data formatting | bytes 524288
  91.8 1.0 %copy.146 = f32[2,64,1,512]{3,2,1,0:T(1,128)} copy(f32[2,64,1,512]{3,1,0,2:T(8,128)S(1)} %get-tuple-element.25) | data formatting | bytes 524288
  (43 shorter events, 1.5 us)
Async XLA Ops:
  0.6 2.1 %copy-start = (bf16[1,1024,512]{2,1,0:T(8,128)(2,1)S(1)}, bf16[1,1024,512]{2,1,0:T(8,128)(2,1)}, u32[]{:S(2)}) copy-start(bf16[1,1024,512]{2,1,0:T(8,128)(2,1)} %param.15) | copy-start | bytes 3145732
  0.6 15.1 %copy-start.6 = (s32[8]{0:T(128)S(1)}, s32[8]{0:T(128)}, u32[]{:S(2)}) copy-start(s32[8]{0:T(128)} %length_ref.1) | copy-start | bytes 100
  0.7 15.3 %copy-start.7 = (s32[8]{0:T(128)S(1)}, s32[8]{0:T(128)}, u32[]{:S(2)}) copy-start(s32[8]{0:T(128)} %param.20) | copy-start | bytes 100
  4.3 25.3 %all-to-all-start = ((f32[128,8,128]{2,1,0:T(8,128)}), f32[128,8,128]{2,1,0:T(8,128)S(1)}, u32[]{:S(2)}, u32[]{:S(2)}) async-start(f32[128,8,128]{2,1,0:T(8,128)} %bitcast.7), calls=%async_computation | async-start | bytes 1048576 | tf_op jit(solution)/shard_map/all_to_all | solution.py:32
  20.2 2.3 %copy-start.4 = (bf16[8,64,64]{2,1,0:T(8,128)(2,1)S(1)}, bf16[8,64,64]{2,1,0:T(8,128)(2,1)}, u32[]{:S(2)}) copy-start(bf16[8,64,64]{2,1,0:T(8,128)(2,1)} %param.17) | copy-start | bytes 196612
  25.5 35.9 %copy-start.2 = (f32[2,64,1,512]{3,2,1,0:T(1,128)S(1)}, f32[2,64,1,512]{3,2,1,0:T(1,128)}, u32[]{:S(2)}) copy-start(f32[2,64,1,512]{3,2,1,0:T(1,128)} %param.13) | copy-start | bytes 786436
  30.5 42.4 %copy-start.1 = (f32[2,64,1,512]{3,2,1,0:T(1,128)S(1)}, f32[2,64,1,512]{3,2,1,0:T(1,128)}, u32[]{:S(2)}) copy-start(f32[2,64,1,512]{3,2,1,0:T(1,128)} %param.14) | copy-start | bytes 786436
  30.5 42.4 %copy-start.5 = (f32[512]{0:T(512)S(1)}, f32[512]{0:T(512)}, u32[]{:S(2)}) copy-start(f32[512]{0:T(512)} %param.16) | copy-start | bytes 6148
  51.1 38.7 %copy-start.3 = (f32[2,64,1,512]{3,2,1,0:T(1,128)S(1)}, f32[2,64,1,512]{3,2,1,0:T(1,128)}, u32[]{:S(2)}) copy-start(f32[2,64,1,512]{3,2,1,0:T(1,128)} %param.12) | copy-start | bytes 786436
  53.0 19.5 %all-to-all-start.1 = ((bf16[128,8,128]{2,1,0:T(8,128)(2,1)}), bf16[128,8,128]{2,1,0:T(8,128)(2,1)S(1)}, u32[]{:S(2)}, u32[]{:S(2)}) async-start(bf16[128,8,128]{2,1,0:T(8,128)(2,1)} %bitcast.27), calls=%async_computation.1 | async-start | bytes 524288 | tf_op jit(solution)/shard_map/all_to_all | solution.py:42

commit v6 on v5

--- a/solution.py
+++ b/solution.py
@@ -23,12 +23,9 @@
     return jnp.sum(lax.all_to_all(copies, MESH_AXES, 0, 0, tiled=True), axis=0)
 
 
-def gather_cycles(partials, band_count):
-    cycle_total, columns = partials.shape
-    group_count = lax.axis_size("mgrp")
-    own = cycle_total // (band_count * group_count)
-    pieces = partials.reshape(band_count, group_count, own, columns).transpose(1, 0, 2, 3)
-    pieces = pieces.reshape(group_count * band_count, own, columns)
+def gather_cycles(partials):
+    group_count, band_count, own, columns = partials.shape
+    pieces = partials.reshape(group_count * band_count, own, columns)
     received = lax.all_to_all(pieces, MESH_AXES, 0, 0, tiled=True)
     received = received.reshape(group_count, band_count, own, columns)
     return jnp.sum(received, axis=1).transpose(1, 0, 2)
@@ -66,7 +63,7 @@
     inside = (column[None, None, :] < lengths[:, None, None]).astype(jnp.float32)
     cosine = factor * cos_full * inside
     sine_part = -factor * sin_full * inside
-    return jnp.stack([cosine, sine_part], axis=1).astype(jnp.bfloat16)
+    return jnp.stack([cosine, sine_part], axis=2).astype(jnp.bfloat16)
 
 
 def pair_table(noise_mats):
@@ -112,7 +109,9 @@
     def chunk(step, total):
         start = pl.multiple_of(step * span, span)
         table = table_ref[0, :, pl.ds(start, span)]
-        sky = jnp.dot(coeff, table, preferred_element_type=jnp.float32).astype(jnp.bfloat16)
+        sky = lax.dot_general(
+            coeff, table, (((0,), (0,)), ((), ())), preferred_element_type=jnp.float32
+        ).astype(jnp.bfloat16)
         for inner in range(span // pair_width):
             block = (start + inner * pair_width) // BLK
             pick = index_ref[cycle, block] * side + index_ref[cycle, block + 1]
@@ -123,7 +122,7 @@
             )
             noisy_ref[:, inner * pair_width:(inner + 1) * pair_width] = noisy.astype(jnp.bfloat16)
         return total + lax.dot_general(
-            noisy_ref[...], table, (((1,), (1,)), ((), ())), preferred_element_type=jnp.float32
+            table, noisy_ref[...], (((1,), (1,)), ((), ())), preferred_element_type=jnp.float32
         )
 
     used = (length_ref[cycle] + span - 1) // span
@@ -136,33 +135,25 @@
     map_count = columns // 2
     kinds = noise_mats.shape[0]
     tables = cycle_tables(m_values, lengths, RLEN).reshape(cycle_count, 2 * mode_count, RLEN)
-    coeff_t = (
-        coeffs.reshape(cycle_count, mode_count, 2, map_count)
-        .transpose(0, 3, 2, 1)
-        .reshape(cycle_count, map_count, 2 * mode_count)
-    )
+    coeff_t = coeffs.reshape(cycle_count, 2 * mode_count, map_count)
     pairs_t = jnp.swapaxes(pair_table(noise_mats), 1, 2) * jnp.asarray(weight, jnp.bfloat16)
     grid_spec = pltpu.PrefetchScalarGridSpec(
         num_scalar_prefetch=2,
         grid=(cycle_count,),
         in_specs=[
-            pl.BlockSpec((1, map_count, 2 * mode_count), lambda r, idx, n: (r, 0, 0)),
+            pl.BlockSpec((1, 2 * mode_count, map_count), lambda r, idx, n: (r, 0, 0)),
             pl.BlockSpec((1, 2 * mode_count, RLEN), lambda r, idx, n: (r, 0, 0)),
             pl.BlockSpec(pairs_t.shape, lambda r, idx, n: (0, 0, 0)),
         ],
-        out_specs=pl.BlockSpec((1, map_count, 2 * mode_count), lambda r, idx, n: (r, 0, 0)),
+        out_specs=pl.BlockSpec((1, 2 * mode_count, map_count), lambda r, idx, n: (r, 0, 0)),
         scratch_shapes=[pltpu.VMEM((map_count, 4096), jnp.bfloat16)],
     )
     back = pl.pallas_call(
         noise_kernel,
         grid_spec=grid_spec,
-        out_shape=jax.ShapeDtypeStruct((cycle_count, map_count, 2 * mode_count), jnp.bfloat16),
+        out_shape=jax.ShapeDtypeStruct((cycle_count, 2 * mode_count, map_count), jnp.bfloat16),
     )(indices, lengths, coeff_t, tables, pairs_t)
-    return (
-        back.reshape(cycle_count, map_count, 2, mode_count)
-        .transpose(0, 3, 2, 1)
-        .reshape(cycle_count, mode_count, columns)
-    )
+    return back.reshape(cycle_count, mode_count, columns)
 
 
 def shards(
@@ -189,10 +180,15 @@
         block_flags = lax.dynamic_slice_in_dim(cut_pattern, first_row // RB, row_count // RB, 1)
         return jnp.repeat(block_flags, RB, axis=1).T
 
-    section = legendre
-    products = jnp.einsum("mrl,nml->rmn", section, rounded, preferred_element_type=jnp.float32)
-    masked_products = products * row_mask(jnp.int32(0), cycle_total).astype(jnp.float32)[:, :, None]
-    coeffs = gather_cycles(masked_products.reshape(cycle_total, columns), band_count).astype(jnp.bfloat16)
+    group_count = lax.axis_size("mgrp")
+    own = cycle_total // (band_count * group_count)
+    section = legendre[0].reshape(band_count, group_count, own, l_local)
+    products = jnp.einsum(
+        "jgcl,nl->gjcn", section, rounded[:, 0, :], preferred_element_type=jnp.float32
+    )
+    keep = row_mask(jnp.int32(0), cycle_total).reshape(band_count, group_count, own)
+    keep = keep.transpose(1, 0, 2).astype(jnp.float32)[:, :, :, None]
+    coeffs = gather_cycles(products * keep).astype(jnp.bfloat16)
     cycle_local = coeffs.shape[0]
     mode_total = coeffs.shape[1]
     outputs = cycle_transform(coeffs, cycle_lengths, noise_index, m_values, noise_mats, weight)

time: 92.8 us -> 124 us (1.34)
  other arithmetic: 12.6 us -> 36.7 us
  local copies, waits for them, and re-layouts: 9.25 us -> 15.5 us
  waiting for transfers between devices: 14.6 us -> 10.5 us
  Pallas kernels: 20.5 us -> 23 us
  starting transfers between devices: 19.7 us -> 21.7 us
    another operation x1 -> x2, other arithmetic: 2.81 us -> 26.8 us
    convert_element_type x2, local copies, waits for them, and re-layouts: 0.08 us -> 7.25 us  [the longest x1 7.24 us: cycle_tables(): return jnp.stack([cosine, sine_part], axis=2).astype(jnp.bfloat16)]
    all_to_all x1, waiting for transfers between devices: 4.1 us -> 0.01 us  [gather_cycles(): received = lax.all_to_all(pieces, MESH_AXES, 0, 0, tiled=True)]
    pallas_call x1, Pallas kernels: 20.5 us -> 23 us  [cycle_transform(): pl.pallas_call(noise_kernel, grid_spec=grid_spec, out_shape=jax.ShapeDtyp...]
    sub x0 -> x1, other arithmetic: none -> 2.38 us  [cycle_tables(): cos_high * cos_low - sin_high * sin_low]
    convert_element_type x1 -> x0, other arithmetic: 2.29 us -> none  [cycle_tables(): return jnp.stack([cosine, sine_part], axis=1).astype(jnp.bfloat16)]
    all_to_all x1, starting transfers between devices: 8.27 us -> 10.2 us  [spread_cycles(): received = lax.all_to_all(pieces, MESH_AXES, 0, 0, tiled=True)]
  transfers between devices with their start and end apart: 2 -> 2, of which waited for: 2 -> 1; matrix products, arithmetic and copies ran while one was open for 11% -> 33% of each run, Pallas kernels for 0% -> 0%
where the time goes in v6:
time: 124 us
  other arithmetic  36.7 us (30%)
  Pallas kernels  23 us (19%)
  starting transfers between devices  21.7 us (18%)
  local copies, waits for them, and re-layouts  15.5 us (12%)
  blocking collectives  14.2 us (11%)
  waiting for transfers between devices  10.5 us (8%)
    pallas_call x1, Pallas kernels, cycle_transform(): pl.pallas_call(noise_kernel, grid_spec=grid_spec, out_shape=jax.ShapeDtyp...  23 us
    another operation x1, other arithmetic  16.3 us
    all_to_all x1, blocking collectives, total_over_mesh(): return jnp.sum(lax.all_to_all(copies, MESH_AXES, 0, 0, tiled=True), axis=0)  14.2 us
    all_to_all x1, starting transfers between devices, gather_cycles(): received = lax.all_to_all(pieces, MESH_AXES, 0, 0, tiled=True)  11.5 us
    another operation x1, other arithmetic, cycle_tables(): return jnp.stack([cosine, sine_part], axis=2).astype(jnp.bfloat16)  10.5 us
    all_to_all x1, waiting for transfers between devices, spread_cycles(): received = lax.all_to_all(pieces, MESH_AXES, 0, 0, tiled=True)  10.5 us
    all_to_all x1, starting transfers between devices, spread_cycles(): received = lax.all_to_all(pieces, MESH_AXES, 0, 0, tiled=True)  10.2 us
    convert_element_type x1, local copies, waits for them, and re-layouts, cycle_tables(): return jnp.stack([cosine, sine_part], axis=2).astype(jnp.bfloat16)  7.24 us
  transfers between devices with their start and end apart: 2, of which 1 were waited for; matrix products, arithmetic and copies ran while one was open for 33% of the time, Pallas kernels for 0%

profile of v6, /device:TPU:1, one launch (start us, length us, event | category | flops | bytes accessed | tf_op | source)
XLA Modules:
  0.0 123.6 jit_solution(14125479821222751428)
XLA Ops:
  0.7 0.8 convert_bitcast_fusion.1
  1.4 1.1 convert_element_type.55
  2.6 0.7 fusion.4
  3.3 1.0 copy.99
  4.3 11.5 %all-to-all-start = ((f32[128,8,128]{2,1,0:T(8,128)}), f32[128,8,128]{2,1,0:T(8,128)S(1)}, u32[]{:S(2)}, u32[]{:S(2)}) async-start(f32[128,8,128]{2,1,0:T(8,128)} %bitcast.5), calls=%async_computation | async-start | bytes 1048576 | tf_op jit(solution)/shard_map/all_to_all | solution.py:29
  16.1 1.0 fusion.22
  17.1 2.4 %multiply_subtract_fusion = (f32[8,8,128,128]{3,2,1,0:T(8,128)S(1)}, f32[8,8,128,128]{3,2,1,0:T(8,128)S(1)}) fusion(f32[8,8,128]{2,1,0:T(8,128)S(1)} %get-tuple-element.38, f32[8,8,128]{2,1,0:T(8,128)S(1)} %get-tuple-element.35, f32[8,8,128]{2,1,0:T(8,128)S(1)} %get-tuple-element.39, f32[8,8,128]{2,1,0:T(8,128)S(1)} %get-tuple-element.34), kind=kLoop, calls=%fused_computation.6 | loop fusion | flops 6291456 | bytes 8519680 | tf_op jit(solution)/shard_map/sub | solution.py:59
  19.5 16.3 %multiply_convert_fusion.1 = (bf16[8,8,1,16384]{3,2,1,0:T(2,128)(2,1)S(1)}, bf16[8,8,1,16384]{3,2,1,0:T(2,128)(2,1)S(1)}) fusion(f32[8,8,1,16384]{3,2,1,0:T(1,128)S(1)} %bitcast.82, f32[8]{0:T(128)S(1)} %get-tuple-element.42, f32[8,16384]{1,0:T(8,128)S(1)} %fusion.8, f32[8,8,1,16384]{3,2,1,0:T(1,128)S(1)} %bitcast.83, f32[8]{0:T(128)S(1)} %get-tuple-element.43), kind=kLoop, calls=%fused_computation.5 | loop fusion | flops 6291456 | bytes 13107264 | tf_op jit(solution)/shard_map/convert
  35.8 10.5 %pad_maximum_fusion = bf16[8,8,2,16384]{3,2,1,0:T(2,128)(2,1)} fusion(bf16[8,8,1,16384]{3,2,1,0:T(2,128)(2,1)S(1)} %get-tuple-element.30, bf16[8,8,1,16384]{3,2,1,0:T(2,128)(2,1)S(1)} %get-tuple-element.29), kind=kLoop, calls=%fused_computation.2 | loop fusion | flops 8388608 | bytes 8388608 | tf_op jit(solution)/shard_map/stack | solution.py:66
  46.3 7.2 %convert_element_type.64.table_ref = bf16[8,16,16384]{2,1,0:T(8,128)(2,1)} reshape(bf16[8,8,2,16384]{3,2,1,0:T(2,128)(2,1)} %pad_maximum_fusion) | data formatting | bytes 8388608 | tf_op jit(solution)/shard_map/convert_element_type | solution.py:66
  53.7 0.2 broadcast_in_dim.23
  53.9 0.2 broadcast_in_dim.24
  54.2 2.3 %fusion.3 = bf16[8,8,128,128]{2,3,1,0:T(8,128)(2,1)} fusion(bf16[8,8,64,64]{2,3,1,0:T(8,128)(2,1)S(1)} %broadcast_in_dim.24, bf16[8,8,64,64]{2,3,1,0:T(8,128)(2,1)S(1)} %broadcast_in_dim.23), kind=kLoop, calls=%fused_computation.10 | loop fusion | flops 10485760 | bytes 3145728 | tf_op jit(solution)/shard_map/mul | solution.py:139
  56.6 0.7 reshape.320.coeff_ref
  57.3 23.0 %shard_map.121 = bf16[8,16,64]{2,1,0:T(8,128)(2,1)} custom-call(s32[8,256]{1,0:T(8,128)} %index_ref.1, s32[8]{0:T(128)} %length_ref.1, bf16[8,16,64]{2,1,0:T(8,128)(2,1)} %reshape.320.coeff_ref, bf16[8,16,16384]{2,1,0:T(8,128)(2,1)} %convert_element_type.64.table_ref, bf16[64,128,128]{2,1,0:T(8,128)(2,1)} %bitcast.84), custom_call_target="tpu_custom_call" | custom-call | tf_op jit(solution)/shard_map/pallas_call | solution.py:151
  80.2 0.9 reshape.321
  81.1 0.7 broadcast_in_dim.25
  81.9 10.2 %all-to-all-start.1 = ((bf16[128,8,128]{2,1,0:T(8,128)(2,1)}), bf16[128,8,128]{2,1,0:T(8,128)(2,1)S(1)}, u32[]{:S(2)}, u32[]{:S(2)}) async-start(bf16[128,8,128]{2,1,0:T(8,128)(2,1)} %bitcast.20), calls=%async_computation.1 | async-start | bytes 524288 | tf_op jit(solution)/shard_map/all_to_all | solution.py:39
  92.3 0.6 multiply_reduce_fusion.3
  92.8 10.5 %all-to-all-done.1 = bf16[128,8,128]{2,1,0:T(8,128)(2,1)S(1)} async-done(((bf16[128,8,128]{2,1,0:T(8,128)(2,1)}), bf16[128,8,128]{2,1,0:T(8,128)(2,1)S(1)}, u32[]{:S(2)}, u32[]{:S(2)}) %all-to-all-start.1) | async-done | bytes 262176 | tf_op jit(solution)/shard_map/all_to_all | solution.py:39
  103.4 0.2 bitcast_multiply_fusion
  103.6 0.1 copy.105
  103.8 0.5 multiply_reduce_fusion.2
  104.3 0.2 reshape.329
  104.6 14.2 %all_to_all.15 = f32[128,1,256]{2,1,0:T(1,128)S(1)} all-to-all(f32[128,1,256]{2,1,0:T(1,128)S(1)} %reshape.329), channel_id=1, replica_groups=mesh['mgrp'=8,'band'=16] {'mgrp','band'}, dimensions={0} | all-to-all | bytes 262144 | tf_op jit(solution)/shard_map/all_to_all | solution.py:23
  118.8 0.5 broadcast.220
  119.3 1.0 reduce
  120.2 0.2 reshape.330
  120.4 0.1 reduce_sum.59
  120.7 1.0 copy.113
  121.7 1.0 copy.114
  122.6 1.0 copy.115
  (36 shorter events, 0.9 us)
Async XLA Ops:
  0.6 2.0 %copy-start = (bf16[1,1024,512]{2,1,0:T(8,128)(2,1)S(1)}, bf16[1,1024,512]{2,1,0:T(8,128)(2,1)}, u32[]{:S(2)}) copy-start(bf16[1,1024,512]{2,1,0:T(8,128)(2,1)} %param.15) | copy-start | bytes 3145732
  0.6 15.2 %copy-start.6 = (s32[8]{0:T(128)S(1)}, s32[8]{0:T(128)}, u32[]{:S(2)}) copy-start(s32[8]{0:T(128)} %length_ref.1) | copy-start | bytes 100
  0.7 15.3 %copy-start.7 = (s32[8]{0:T(128)S(1)}, s32[8]{0:T(128)}, u32[]{:S(2)}) copy-start(s32[8]{0:T(128)} %param.20) | copy-start | bytes 100
  4.3 52.2 %all-to-all-start = ((f32[128,8,128]{2,1,0:T(8,128)}), f32[128,8,128]{2,1,0:T(8,128)S(1)}, u32[]{:S(2)}, u32[]{:S(2)}) async-start(f32[128,8,128]{2,1,0:T(8,128)} %bitcast.5), calls=%async_computation | async-start | bytes 1048576 | tf_op jit(solution)/shard_map/all_to_all | solution.py:29
  46.3 7.2 %copy-start.4 = (bf16[8,64,64]{2,1,0:T(8,128)(2,1)S(1)}, bf16[8,64,64]{2,1,0:T(8,128)(2,1)}, u32[]{:S(2)}) copy-start(bf16[8,64,64]{2,1,0:T(8,128)(2,1)} %param.17) | copy-start | bytes 196612
  56.5 35.8 %copy-start.2 = (f32[2,64,1,512]{3,2,1,0:T(1,128)S(1)}, f32[2,64,1,512]{3,2,1,0:T(1,128)}, u32[]{:S(2)}) copy-start(f32[2,64,1,512]{3,2,1,0:T(1,128)} %param.13) | copy-start | bytes 786436
  57.3 46.5 %copy-start.1 = (f32[2,64,1,512]{3,2,1,0:T(1,128)S(1)}, f32[2,64,1,512]{3,2,1,0:T(1,128)}, u32[]{:S(2)}) copy-start(f32[2,64,1,512]{3,2,1,0:T(1,128)} %param.14) | copy-start | bytes 786436
  57.3 46.5 %copy-start.5 = (f32[512]{0:T(512)S(1)}, f32[512]{0:T(512)}, u32[]{:S(2)}) copy-start(f32[512]{0:T(512)} %param.16) | copy-start | bytes 6148
  80.2 40.3 %copy-start.3 = (f32[2,64,1,512]{3,2,1,0:T(1,128)S(1)}, f32[2,64,1,512]{3,2,1,0:T(1,128)}, u32[]{:S(2)}) copy-start(f32[2,64,1,512]{3,2,1,0:T(1,128)} %param.12) | copy-start | bytes 786436
  81.9 21.5 %all-to-all-start.1 = ((bf16[128,8,128]{2,1,0:T(8,128)(2,1)}), bf16[128,8,128]{2,1,0:T(8,128)(2,1)S(1)}, u32[]{:S(2)}, u32[]{:S(2)}) async-start(bf16[128,8,128]{2,1,0:T(8,128)(2,1)} %bitcast.20), calls=%async_computation.1 | async-start | bytes 524288 | tf_op jit(solution)/shard_map/all_to_all | solution.py:39

commit v7 on v5

--- a/solution.py
+++ b/solution.py
@@ -195,13 +195,24 @@
     coeffs = gather_cycles(masked_products.reshape(cycle_total, columns), band_count).astype(jnp.bfloat16)
     cycle_local = coeffs.shape[0]
     mode_total = coeffs.shape[1]
-    outputs = cycle_transform(coeffs, cycle_lengths, noise_index, m_values, noise_mats, weight)
-    backward = outputs.reshape(cycle_local, mode_total, columns)
-    returned = spread_cycles(backward, band_count)
-    masked = returned * row_mask(jnp.int32(0), cycle_total).astype(jnp.bfloat16)
-    image_data = jnp.einsum(
-        "mrl,rn->nml", legendre, masked, preferred_element_type=jnp.float32
-    )
+    group_count = lax.axis_size("mgrp")
+    half = cycle_local // 2
+    keep_rows = row_mask(jnp.int32(0), cycle_total).astype(jnp.bfloat16)
+    keep_rows = keep_rows.reshape(band_count, group_count, cycle_local, 1)
+    rows = legendre[0].reshape(band_count, group_count, cycle_local, l_local)
+    image_data = None
+    for part in range(2):
+        chosen = slice(part * half, (part + 1) * half)
+        outputs = cycle_transform(
+            coeffs[chosen], cycle_lengths[chosen], noise_index[chosen], m_values, noise_mats, weight
+        )
+        returned = spread_cycles(outputs.reshape(half, mode_total, columns), band_count)
+        masked = returned * keep_rows[:, :, chosen].reshape(-1, 1)
+        partial = jnp.einsum(
+            "rl,rn->nl", rows[:, :, chosen].reshape(-1, l_local), masked,
+            preferred_element_type=jnp.float32,
+        )
+        image_data = partial if image_data is None else image_data + partial
     image_data = image_data.reshape(2, map_count, mode_local, l_local)
     image_field = prior_inv[None, None, None, :] * direction + image_data
     norm_now, curvature, cross, image_norm = total_over_mesh(

time: 92.8 us -> 114 us (1.23)
  starting transfers between devices: 19.7 us -> 32.3 us
  other arithmetic: 12.6 us -> 17.6 us
  waiting for transfers between devices: 14.6 us -> 10.5 us
  Pallas kernels: 20.5 us -> 24.3 us
  matrix products: 0.95 us -> 2.61 us
    all_to_all x1 -> x2, starting transfers between devices: 8.27 us -> 20.8 us  [spread_cycles(): received = lax.all_to_all(pieces, MESH_AXES, 0, 0, tiled=True)]
    pallas_call x1 -> x2, Pallas kernels: 20.5 us -> 24.3 us  [cycle_transform(): pl.pallas_call(noise_kernel, grid_spec=grid_spec, out_shape=jax.ShapeDtyp...]
    all_to_all x1, waiting for transfers between devices: 4.1 us -> 1.14 us  [gather_cycles(): received = lax.all_to_all(pieces, MESH_AXES, 0, 0, tiled=True)]
    unnamed x23 -> x26, local copies, waits for them, and re-layouts: 3.5 us -> 0.61 us
    another operation x1, other arithmetic: 2.81 us -> 4.87 us
    add x1, other arithmetic: 0.13 us -> 1.59 us  [shards(): new_direction = new_residual + growth[None, :, None, None] * direction]
    dot_general x1, matrix products: 0.47 us -> 1.71 us  [shards(): jnp.einsum('mrl,nml->rmn', section, rounded, preferred_element_type=jnp.f...]
    slice x0 -> x5, local copies, waits for them, and re-layouts: none -> 1.15 us  [the longest x1 0.6 us: shards(): noise_index[chosen]]
  transfers between devices with their start and end apart: 2 -> 3, of which waited for: 2 -> 2; matrix products, arithmetic and copies ran while one was open for 11% -> 15% of each run, Pallas kernels for 0% -> 11%
where the time goes in v7:
time: 114 us; the launch traced here: 113 us
  starting transfers between devices  32.3 us (28%)
  Pallas kernels  24.3 us (21%)
  other arithmetic  17.6 us (15%)
  blocking collectives  14.2 us (12%)
  waiting for transfers between devices  10.5 us (9%)
  local copies, waits for them, and re-layouts  10.3 us (9%)
  matrix products  2.61 us (2%)
    pallas_call x2, Pallas kernels, cycle_transform(): pl.pallas_call(noise_kernel, grid_spec=grid_spec, out_shape=jax.ShapeDtyp...  24.3 us
    all_to_all x2, starting transfers between devices, spread_cycles(): received = lax.all_to_all(pieces, MESH_AXES, 0, 0, tiled=True)  20.8 us
    all_to_all x1, blocking collectives, total_over_mesh(): return jnp.sum(lax.all_to_all(copies, MESH_AXES, 0, 0, tiled=True), axis=0)  14.2 us
    all_to_all x1, starting transfers between devices, gather_cycles(): received = lax.all_to_all(pieces, MESH_AXES, 0, 0, tiled=True)  11.5 us
    all_to_all x2, waiting for transfers between devices, spread_cycles(): received = lax.all_to_all(pieces, MESH_AXES, 0, 0, tiled=True)  9.39 us
    another operation x1, other arithmetic  4.87 us
    convert_element_type x2, other arithmetic, cycle_tables(): return jnp.stack([cosine, sine_part], axis=1).astype(jnp.bfloat16)  2.99 us
    mul x1, other arithmetic, cycle_transform(): jnp.swapaxes(pair_table(noise_mats), 1, 2)  2.32 us
  transfers between devices with their start and end apart: 3, of which 2 were waited for; matrix products, arithmetic and copies ran while one was open for 15% of the time, Pallas kernels for 11%

profile of v7, /device:TPU:1, one launch (start us, length us, event | category | flops | bytes accessed | tf_op | source)
XLA Modules:
  0.0 112.9 jit_solution(11806106214176209458)
XLA Ops:
  0.6 0.7 convert_bitcast_fusion.1
  1.5 1.1 %convert_element_type.81 = bf16[2,64,1,512]{3,2,1,0:T(2,128)(2,1)S(1)} convert(f32[2,64,1,512]{3,2,1,0:T(1,128)} %param.14) | non-fusion elementwise | flops 65536 | bytes 393216 | tf_op jit(solution)/shard_map/convert_element_type | solution.py:186
  2.7 1.7 %fusion.13 = f32[1024,1,128]{0,2,1:T(8,128)S(1)} fusion(bf16[128,512]{1,0:T(8,128)(2,1)S(1)} %bitcast.153, bf16[1,1024,512]{2,1,0:T(8,128)(2,1)} %param.15, f32[1024]{0:T(1024)S(1)} %convert_element_type.84), kind=kOutput, calls=%fused_computation.22 | convolution fusion | flops 134348800 | bytes 1708032 | tf_op jit(solution)/shard_map/mrl,nml->rmn/dot_general | solution.py:193
  4.6 0.8 copy.98
  5.5 11.5 %all-to-all-start = ((f32[128,8,128]{2,1,0:T(8,128)}), f32[128,8,128]{2,1,0:T(8,128)S(1)}, u32[]{:S(2)}, u32[]{:S(2)}) async-start(f32[128,8,128]{2,1,0:T(8,128)} %bitcast.7), calls=%async_computation | async-start | bytes 1048576 | tf_op jit(solution)/shard_map/all_to_all | solution.py:32
  17.3 1.0 fusion.47
  18.7 0.8 copy.115
  19.7 4.9 %fusion.7 = (bf16[4,1,8,16384]{3,2,1,0:T(8,128)(2,1)S(1)}, bf16[4,1,8,16384]{3,2,1,0:T(8,128)(2,1)S(1)}, bf16[4,1,8,16384]{3,2,1,0:T(8,128)(2,1)S(1)}, bf16[4,1,8,16384]{3,2,1,0:T(8,128)(2,1)S(1)}) fusion(f32[4,16384]{1,0:T(4,128)S(1)} %get-tuple-element.59, f32[4,8,128]{2,1,0:T(8,128)S(1)} %get-tuple-element.34, f32[4,8,128]{1,2,0:T(8,128)} %copy.115, ...), kind=kLoop, calls=%fused_computation.13 | loop fusion | flops 12582912 | bytes 4849728 | tf_op jit(solution)/shard_map/convert
  24.6 1.5 %maximum_bitcast_fusion.1.table_ref = bf16[4,16,16384]{2,1,0:T(8,128)(2,1)} fusion(bf16[4,1,8,16384]{3,2,1,0:T(8,128)(2,1)S(1)} %get-tuple-element.18, bf16[4,1,8,16384]{3,2,1,0:T(8,128)(2,1)S(1)} %get-tuple-element.17), kind=kLoop, calls=%fused_computation.7 | loop fusion | flops 1048576 | bytes 4194304 | tf_op jit(solution)/shard_map/convert_element_type | solution.py:69
  26.2 0.6 fusion.58
  27.3 2.3 %fusion.3 = bf16[8,8,128,128]{2,3,1,0:T(8,128)(2,1)} fusion(bf16[8,8,64,64]{2,3,1,0:T(8,128)(2,1)S(1)} %broadcast_in_dim.31, bf16[8,8,64,64]{2,3,1,0:T(8,128)(2,1)S(1)} %broadcast_in_dim.30), kind=kLoop, calls=%fused_computation.5 | loop fusion | flops 10485760 | bytes 3145728 | tf_op jit(solution)/shard_map/mul | solution.py:144
  29.7 1.1 %all-to-all-done = f32[128,8,128]{2,1,0:T(8,128)S(1)} async-done(((f32[128,8,128]{2,1,0:T(8,128)}), f32[128,8,128]{2,1,0:T(8,128)S(1)}, u32[]{:S(2)}, u32[]{:S(2)}) %all-to-all-start) | async-done | bytes 524320 | tf_op jit(solution)/shard_map/all_to_all | solution.py:32
  30.9 0.7 copy.116.coeff_ref
  31.7 11.7 %shard_map.122 = bf16[4,64,16]{2,1,0:T(8,128)(2,1)} custom-call(s32[4,256]{1,0:T(4,128)} %get-tuple-element.23.index_ref, s32[4]{0:T(128)} %copy-done.8, bf16[4,64,16]{2,1,0:T(8,128)(2,1)} %copy.116.coeff_ref, bf16[4,16,16384]{2,1,0:T(8,128)(2,1)} %maximum_bitcast_fusion.1.table_ref, bf16[64,128,128]{2,1,0:T(8,128)(2,1)} %bitcast.146), custom_call_target="tpu_custom_call" | custom-call | tf_op jit(solution)/shard_map/pallas_call | solution.py:156
  43.4 0.9 copy.117
  44.4 0.7 broadcast_in_dim.34
  45.1 10.2 %all-to-all-start.2 = ((bf16[128,4,128]{2,1,0:T(4,128)(2,1)}), bf16[128,4,128]{2,1,0:T(4,128)(2,1)S(1)}, u32[]{:S(2)}, u32[]{:S(2)}) async-start(bf16[128,4,128]{2,1,0:T(4,128)(2,1)} %bitcast.50), calls=%async_computation.2 | async-start | bytes 262144 | tf_op jit(solution)/shard_map/all_to_all | solution.py:42
  55.4 1.5 %maximum_bitcast_fusion.table_ref = bf16[4,16,16384]{2,1,0:T(8,128)(2,1)} fusion(bf16[4,1,8,16384]{3,2,1,0:T(8,128)(2,1)S(1)} %get-tuple-element.40, bf16[4,1,8,16384]{3,2,1,0:T(8,128)(2,1)S(1)} %get-tuple-element.41), kind=kLoop, calls=%fused_computation.6 | loop fusion | flops 1048576 | bytes 4194304 | tf_op jit(solution)/shard_map/convert_element_type | solution.py:69
  57.0 0.7 copy.105.coeff_ref
  57.7 12.6 %shard_map.121 = bf16[4,64,16]{2,1,0:T(8,128)(2,1)} custom-call(s32[4,256]{1,0:T(4,128)} %get-tuple-element.22.index_ref, s32[4]{0:T(128)} %copy-done.7, bf16[4,64,16]{2,1,0:T(8,128)(2,1)} %copy.105.coeff_ref, bf16[4,16,16384]{2,1,0:T(8,128)(2,1)} %maximum_bitcast_fusion.table_ref, bf16[64,128,128]{2,1,0:T(8,128)(2,1)} %bitcast.147), custom_call_target="tpu_custom_call" | custom-call | tf_op jit(solution)/shard_map/pallas_call | solution.py:156
  70.2 0.9 copy.106
  71.3 0.7 broadcast_in_dim.32
  72.0 10.6 %all-to-all-start.1 = ((bf16[128,4,128]{2,1,0:T(4,128)(2,1)}), bf16[128,4,128]{2,1,0:T(4,128)(2,1)S(1)}, u32[]{:S(2)}, u32[]{:S(2)}) async-start(bf16[128,4,128]{2,1,0:T(4,128)(2,1)} %bitcast.27), calls=%async_computation.1 | async-start | bytes 262144 | tf_op jit(solution)/shard_map/all_to_all | solution.py:42
  82.6 0.5 fusion.56
  83.2 9.4 %all-to-all-done.1 = bf16[128,4,128]{2,1,0:T(4,128)(2,1)S(1)} async-done(((bf16[128,4,128]{2,1,0:T(4,128)(2,1)}), bf16[128,4,128]{2,1,0:T(4,128)(2,1)S(1)}, u32[]{:S(2)}, u32[]{:S(2)}) %all-to-all-start.1) | async-done | bytes 131104 | tf_op jit(solution)/shard_map/all_to_all | solution.py:42
  92.7 0.5 convolution_bitcast_fusion.1
  93.2 0.5 fusion.14
  93.7 1.3 %multiply_reduce_fusion.3 = (f32[64]{0:T(128)S(1)}, f32[64]{0:T(128)S(1)}, f32[64]{0:T(128)S(1)}, f32[64]{0:T(128)S(1)}, f32[2,64,1,512]{3,2,1,0:T(1,128)S(1)}) fusion(f32[2,64,1,512]{3,2,1,0:T(1,128)S(1)} %copy-done.2, f32[2,64,1,512]{3,2,1,0:T(1,128)S(1)} %copy-done.1, f32[2,64,1,512]{3,1,0,2:T(8,128)S(1)} %bitcast.150, f32[512]{0:T(512)S(1)} %copy-done.9), kind=kLoop, calls=%fused_computation.39 | loop fusion | flops 655104 | bytes 1051648 | tf_op jit(solution)/shard_map/reduce_sum | solution.py:221
  95.3 14.2 %all_to_all.20 = f32[128,1,256]{2,1,0:T(1,128)S(1)} all-to-all(f32[128,1,256]{2,1,0:T(1,128)S(1)} %reshape.523), channel_id=1, replica_groups=mesh['mgrp'=8,'band'=16] {'mgrp','band'}, dimensions={0} | all-to-all | bytes 262144 | tf_op jit(solution)/shard_map/all_to_all | solution.py:23
  109.5 0.5 broadcast.337
  110.0 1.0 reduce
  111.3 1.6 %multiply_add_fusion = (f32[2,64,1,512]{3,2,1,0:T(1,128)}, f32[2,64,1,512]{3,2,1,0:T(1,128)}, f32[2,64,1,512]{3,2,1,0:T(1,128)}) fusion(f32[2,64,1,512]{3,2,1,0:T(1,128)S(1)} %copy-done.1, f32[64]{0:T(128)S(1)} %get-tuple-element.10, f32[2,64,1,512]{3,2,1,0:T(1,128)S(1)} %copy-done.2, f32[2,64,1,512]{3,2,1,0:T(1,128)S(1)} %get-tuple-element.12, ...), kind=kLoop, calls=%fused_computation.31 | loop fusion | flops 393216 | bytes 1835520 | tf_op jit(solution)/shard_map/add | solution.py:233
  (63 shorter events, 3.1 us)
Async XLA Ops:
  2.7 14.3 %copy-start.5 = (s32[8]{0:T(128)S(1)}, s32[8]{0:T(128)}, u32[]{:S(2)}) copy-start(s32[8]{0:T(128)} %param.19) | copy-start | bytes 100
  2.7 14.5 %copy-start.10 = (s32[8]{0:T(128)S(1)}, s32[8]{0:T(128)}, u32[]{:S(2)}) copy-start(s32[8]{0:T(128)} %param.20) | copy-start | bytes 100
  5.5 25.3 %all-to-all-start = ((f32[128,8,128]{2,1,0:T(8,128)}), f32[128,8,128]{2,1,0:T(8,128)S(1)}, u32[]{:S(2)}, u32[]{:S(2)}) async-start(f32[128,8,128]{2,1,0:T(8,128)} %bitcast.7), calls=%async_computation | async-start | bytes 1048576 | tf_op jit(solution)/shard_map/all_to_all | solution.py:32
  17.0 7.5 %copy-start.7 = (s32[4]{0:T(128)}, s32[4]{0:T(128)S(1)}, u32[]{:S(2)}) copy-start(s32[4]{0:T(128)S(1)} %get-tuple-element.51.length_ref) | copy-start | bytes 52
  17.0 7.5 %copy-start.8 = (s32[4]{0:T(128)}, s32[4]{0:T(128)S(1)}, u32[]{:S(2)}) copy-start(s32[4]{0:T(128)S(1)} %get-tuple-element.50.length_ref) | copy-start | bytes 52
  24.6 1.5 %copy-start.4 = (bf16[8,64,64]{2,1,0:T(8,128)(2,1)S(1)}, bf16[8,64,64]{2,1,0:T(8,128)(2,1)}, u32[]{:S(2)}) copy-start(bf16[8,64,64]{2,1,0:T(8,128)(2,1)} %param.17) | copy-start | bytes 196612
  24.6 1.6 %copy-start.6 = (s32[8,256]{1,0:T(8,128)S(1)}, s32[8,256]{1,0:T(8,128)}, u32[]{:S(2)}) copy-start(s32[8,256]{1,0:T(8,128)} %param.18) | copy-start | bytes 24580
  45.1 26.1 %all-to-all-start.2 = ((bf16[128,4,128]{2,1,0:T(4,128)(2,1)}), bf16[128,4,128]{2,1,0:T(4,128)(2,1)S(1)}, u32[]{:S(2)}, u32[]{:S(2)}) async-start(bf16[128,4,128]{2,1,0:T(4,128)(2,1)} %bitcast.50), calls=%async_computation.2 | async-start | bytes 262144 | tf_op jit(solution)/shard_map/all_to_all | solution.py:42
  57.7 24.9 %copy-start = (bf16[1,1024,512]{2,1,0:T(8,128)(2,1)S(1)}, bf16[1,1024,512]{2,1,0:T(8,128)(2,1)}, u32[]{:S(2)}) copy-start(bf16[1,1024,512]{2,1,0:T(8,128)(2,1)} %param.15) | copy-start | bytes 3145732
  72.0 20.6 %all-to-all-start.1 = ((bf16[128,4,128]{2,1,0:T(4,128)(2,1)}), bf16[128,4,128]{2,1,0:T(4,128)(2,1)S(1)}, u32[]{:S(2)}, u32[]{:S(2)}) async-start(bf16[128,4,128]{2,1,0:T(4,128)(2,1)} %bitcast.27), calls=%async_computation.1 | async-start | bytes 262144 | tf_op jit(solution)/shard_map/all_to_all | solution.py:42
  83.1 10.5 %copy-start.1 = (f32[2,64,1,512]{3,2,1,0:T(1,128)S(1)}, f32[2,64,1,512]{3,2,1,0:T(1,128)}, u32[]{:S(2)}) copy-start(f32[2,64,1,512]{3,2,1,0:T(1,128)} %param.14) | copy-start | bytes 786436
  83.2 10.5 %copy-start.2 = (f32[2,64,1,512]{3,2,1,0:T(1,128)S(1)}, f32[2,64,1,512]{3,2,1,0:T(1,128)}, u32[]{:S(2)}) copy-start(f32[2,64,1,512]{3,2,1,0:T(1,128)} %param.13) | copy-start | bytes 786436
  83.2 10.5 %copy-start.9 = (f32[512]{0:T(512)S(1)}, f32[512]{0:T(512)}, u32[]{:S(2)}) copy-start(f32[512]{0:T(512)} %param.16) | copy-start | bytes 6148
  93.2 18.1 %copy-start.3 = (f32[2,64,1,512]{3,2,1,0:T(1,128)S(1)}, f32[2,64,1,512]{3,2,1,0:T(1,128)}, u32[]{:S(2)}) copy-start(f32[2,64,1,512]{3,2,1,0:T(1,128)} %param.12) | copy-start | bytes 786436

commit v8 on v5

--- a/solution.py
+++ b/solution.py
@@ -104,13 +104,12 @@
 
 def noise_kernel(index_ref, length_ref, coeff_ref, table_ref, pair_ref, back_ref, noisy_ref):
     cycle = pl.program_id(0)
-    span = noisy_ref.shape[1]
+    wide = noisy_ref.shape[1]
     pair_width = 2 * BLK
     coeff = coeff_ref[0]
     side = int(round(pair_ref.shape[0] ** 0.5))
 
-    def chunk(step, total):
-        start = pl.multiple_of(step * span, span)
+    def chunk(start, span, total):
         table = table_ref[0, :, pl.ds(start, span)]
         sky = jnp.dot(coeff, table, preferred_element_type=jnp.float32).astype(jnp.bfloat16)
         for inner in range(span // pair_width):
@@ -123,11 +122,27 @@
             )
             noisy_ref[:, inner * pair_width:(inner + 1) * pair_width] = noisy.astype(jnp.bfloat16)
         return total + lax.dot_general(
-            noisy_ref[...], table, (((1,), (1,)), ((), ())), preferred_element_type=jnp.float32
+            noisy_ref[:, :span], table, (((1,), (1,)), ((), ())), preferred_element_type=jnp.float32
         )
 
-    used = (length_ref[cycle] + span - 1) // span
-    total = lax.fori_loop(0, used, chunk, jnp.zeros(back_ref.shape[1:], jnp.float32))
+    length = length_ref[cycle]
+    full = length // wide
+    rest = length - full * wide
+    narrow = wide // 2
+    wide_count = full + (rest > narrow).astype(jnp.int32)
+    narrow_count = ((rest > 0) & (rest <= narrow)).astype(jnp.int32)
+    total = lax.fori_loop(
+        0,
+        wide_count,
+        lambda step, acc: chunk(pl.multiple_of(step * wide, wide), wide, acc),
+        jnp.zeros(back_ref.shape[1:], jnp.float32),
+    )
+    total = lax.fori_loop(
+        0,
+        narrow_count,
+        lambda step, acc: chunk(pl.multiple_of(full * wide, wide), narrow, acc),
+        total,
+    )
     back_ref[0] = total.astype(back_ref.dtype)
 
 
@@ -199,8 +214,8 @@
     backward = outputs.reshape(cycle_local, mode_total, columns)
     returned = spread_cycles(backward, band_count)
     masked = returned * row_mask(jnp.int32(0), cycle_total).astype(jnp.bfloat16)
-    image_data = jnp.einsum(
-        "mrl,rn->nml", legendre, masked, preferred_element_type=jnp.float32
+    image_data = lax.optimization_barrier(
+        jnp.einsum("rl,rn->nl", legendre[0], masked, preferred_element_type=jnp.float32)
     )
     image_data = image_data.reshape(2, map_count, mode_local, l_local)
     image_field = prior_inv[None, None, None, :] * direction + image_data

time: 92.8 us -> 91.9 us (level); the launches traced: 92.8 us -> 90.6 us
  blocking collectives: 14.2 us -> 34.3 us
  waiting for transfers between devices: 14.6 us -> 4.1 us
  starting transfers between devices: 19.7 us -> 11.5 us
  local copies, waits for them, and re-layouts: 9.25 us -> 5.33 us
  other arithmetic: 12.6 us -> 14.6 us
  Pallas kernels: 20.5 us -> 19 us
    all_to_all x0 -> x1, blocking collectives: none -> 20.1 us  [spread_cycles(): received = lax.all_to_all(pieces, MESH_AXES, 0, 0, tiled=True)]
    all_to_all x1 -> x0, waiting for transfers between devices: 10.5 us -> none  [spread_cycles(): received = lax.all_to_all(pieces, MESH_AXES, 0, 0, tiled=True)]
    all_to_all x1 -> x0, starting transfers between devices: 8.27 us -> none  [spread_cycles(): received = lax.all_to_all(pieces, MESH_AXES, 0, 0, tiled=True)]
    unnamed x23 -> x20, local copies, waits for them, and re-layouts: 3.5 us -> 0.59 us
    pallas_call x1, Pallas kernels: 20.5 us -> 19 us  [cycle_transform(): pl.pallas_call(noise_kernel, grid_spec=grid_spec, out_shape=jax.ShapeDtyp...]
    add x1, other arithmetic: 0.13 us -> 1.59 us  [shards(): new_direction = new_residual + growth[None, :, None, None] * direction]
  transfers between devices with their start and end apart: 2 -> 1, of which waited for: 2 -> 1; matrix products, arithmetic and copies ran while one was open for 11% -> 11% of each run, Pallas kernels for 0% -> 0%
where the time goes in v8:
time: 91.9 us; the launch traced here: 90.6 us
  blocking collectives  34.3 us (37%)
  Pallas kernels  19 us (21%)
  other arithmetic  14.6 us (16%)
  starting transfers between devices  11.5 us (13%)
  local copies, waits for them, and re-layouts  5.33 us (6%)
  waiting for transfers between devices  4.1 us (4%)
  between operations  0.93 us (1%)
    all_to_all x1, blocking collectives, spread_cycles(): received = lax.all_to_all(pieces, MESH_AXES, 0, 0, tiled=True)  20.1 us
    pallas_call x1, Pallas kernels, cycle_transform(): pl.pallas_call(noise_kernel, grid_spec=grid_spec, out_shape=jax.ShapeDtyp...  19 us
    all_to_all x1, blocking collectives, total_over_mesh(): return jnp.sum(lax.all_to_all(copies, MESH_AXES, 0, 0, tiled=True), axis=0)  14.2 us
    all_to_all x1, starting transfers between devices, gather_cycles(): received = lax.all_to_all(pieces, MESH_AXES, 0, 0, tiled=True)  11.5 us
    all_to_all x1, waiting for transfers between devices, gather_cycles(): received = lax.all_to_all(pieces, MESH_AXES, 0, 0, tiled=True)  4.1 us
    another operation x1, other arithmetic  2.81 us
    mul x1, other arithmetic, cycle_transform(): jnp.swapaxes(pair_table(noise_mats), 1, 2)  2.32 us
    convert_element_type x1, other arithmetic, cycle_tables(): return jnp.stack([cosine, sine_part], axis=1).astype(jnp.bfloat16)  2.29 us
  transfers between devices with their start and end apart: 1, of which 1 were waited for; matrix products, arithmetic and copies ran while one was open for 11% of the time, Pallas kernels for 0%

profile of v8, /device:TPU:1, one launch (start us, length us, event | category | flops | bytes accessed | tf_op | source)
XLA Modules:
  0.0 90.6 jit_solution(7608702053354763845)
XLA Ops:
  0.7 0.8 convert_bitcast_fusion.1
  1.6 1.1 %convert_element_type.61 = bf16[2,64,1,512]{3,2,1,0:T(2,128)(2,1)S(1)} convert(f32[2,64,1,512]{3,2,1,0:T(1,128)} %param.14) | non-fusion elementwise | flops 65536 | bytes 393216 | tf_op jit(solution)/shard_map/convert_element_type | solution.py:201
  2.7 0.5 fusion.9
  3.2 0.2 copy.72
  3.4 0.8 copy.73
  4.3 11.5 %all-to-all-start = ((f32[128,8,128]{2,1,0:T(8,128)}), f32[128,8,128]{2,1,0:T(8,128)S(1)}, u32[]{:S(2)}, u32[]{:S(2)}) async-start(f32[128,8,128]{2,1,0:T(8,128)} %bitcast.7), calls=%async_computation | async-start | bytes 1048576 | tf_op jit(solution)/shard_map/all_to_all | solution.py:32
  15.8 0.1 fusion.13
  16.0 1.0 %fusion.27 = (f32[8,8,128]{2,1,0:T(8,128)S(1)}, f32[8,8,128]{2,1,0:T(8,128)S(1)}, f32[8,8,128]{2,1,0:T(8,128)S(1)}, f32[8,8,128]{2,1,0:T(8,128)S(1)}) fusion(f32[8]{0:T(128)S(1)} %convert_element_type.68, pred[8]{0:T(512)(128)(4,1)S(1)} %compare_bitcast_fusion, s32[8]{0:T(128)S(1)} %fusion.31, s32[8,128]{1,0:T(8,128)S(1)} %get-tuple-element.26, ...), kind=kLoop, calls=%fused_computation.54 | loop fusion | flops 163840 | bytes 139336 | tf_op jit(solution)/shard_map/cos | solution.py:56
  17.0 0.2 copy.76
  17.2 0.2 copy.77
  17.4 2.8 %fusion.3 = (bf16[8,1,8,16384]{3,2,1,0:T(8,128)(2,1)S(1)}, bf16[8,1,8,16384]{3,2,1,0:T(8,128)(2,1)S(1)}) fusion(f32[8,16384]{1,0:T(8,128)S(1)} %fusion.13, f32[8,8,128]{2,1,0:T(8,128)S(1)} %get-tuple-element.20, f32[8,8,128]{1,2,0:T(8,128)S(1)} %copy.77, f32[8,8,128]{2,1,0:T(8,128)S(1)} %get-tuple-element.21, f32[8,8,128]{1,2,0:T(8,128)S(1)} %copy.76, ...), kind=kLoop, calls=%fused_computation.8 | loop fusion | flops 12582912 | bytes 4849728 | tf_op jit(solution)/shard_map/convert
  20.3 2.3 %maximum_bitcast_fusion.table_ref = bf16[8,16,16384]{2,1,0:T(8,128)(2,1)} fusion(bf16[8,1,8,16384]{3,2,1,0:T(8,128)(2,1)S(1)} %get-tuple-element.14, bf16[8,1,8,16384]{3,2,1,0:T(8,128)(2,1)S(1)} %get-tuple-element.13), kind=kLoop, calls=%fused_computation.2 | loop fusion | flops 2097152 | bytes 8388608 | tf_op jit(solution)/shard_map/convert_element_type | solution.py:69
  22.5 0.1 copy.78
  22.7 0.2 broadcast_in_dim.24
  22.9 0.2 broadcast_in_dim.25
  23.2 2.3 %fusion.7 = bf16[8,8,128,128]{2,3,1,0:T(8,128)(2,1)} fusion(bf16[8,8,64,64]{2,3,1,0:T(8,128)(2,1)S(1)} %broadcast_in_dim.25, bf16[8,8,64,64]{2,3,1,0:T(8,128)(2,1)S(1)} %broadcast_in_dim.24), kind=kLoop, calls=%fused_computation.12 | loop fusion | flops 10485760 | bytes 3145728 | tf_op jit(solution)/shard_map/mul | solution.py:159
  25.5 4.1 %all-to-all-done = f32[128,8,128]{2,1,0:T(8,128)S(1)} async-done(((f32[128,8,128]{2,1,0:T(8,128)}), f32[128,8,128]{2,1,0:T(8,128)S(1)}, u32[]{:S(2)}, u32[]{:S(2)}) %all-to-all-start) | async-done | bytes 524320 | tf_op jit(solution)/shard_map/all_to_all | solution.py:32
  29.8 0.8 copy.80.coeff_ref
  30.5 19.0 %shard_map.121 = bf16[8,64,16]{2,1,0:T(8,128)(2,1)} custom-call(s32[8,256]{1,0:T(8,128)} %index_ref.1, s32[8]{0:T(128)} %length_ref.1, bf16[8,64,16]{2,1,0:T(8,128)(2,1)} %copy.80.coeff_ref, bf16[8,16,16384]{2,1,0:T(8,128)(2,1)} %maximum_bitcast_fusion.table_ref, bf16[64,128,128]{2,1,0:T(8,128)(2,1)} %bitcast.99), custom_call_target="tpu_custom_call" | custom-call | tf_op jit(solution)/shard_map/pallas_call | solution.py:171
  49.5 1.0 %copy.81 = bf16[8,64,16]{1,2,0:T(8,128)(2,1)S(1)} copy(bf16[8,64,16]{2,1,0:T(8,128)(2,1)} %shard_map.121) | data formatting | bytes 32768 | tf_op jit(solution)/shard_map/pallas_call | solution.py:171
  50.6 0.1 reshape.354
  50.8 20.1 %all_to_all.15 = bf16[128,8,128]{2,1,0:T(8,128)(2,1)S(1)} all-to-all(bf16[128,8,128]{2,1,0:T(8,128)(2,1)S(1)} %bitcast.102), channel_id=1, replica_groups=mesh['mgrp'=8,'band'=16] {'mgrp','band'}, dimensions={0} | all-to-all | bytes 524288 | tf_op jit(solution)/shard_map/all_to_all | solution.py:42
  70.8 0.1 multiply_bitcast_fusion
  71.0 0.3 fusion.10
  71.4 1.3 %multiply_reduce_fusion.3 = (f32[64]{0:T(128)S(1)}, f32[64]{0:T(128)S(1)}, f32[64]{0:T(128)S(1)}, f32[64]{0:T(128)S(1)}, f32[2,64,1,512]{3,2,1,0:T(1,128)S(1)}) fusion(f32[2,64,1,512]{3,2,1,0:T(1,128)S(1)} %copy-done.2, f32[2,64,1,512]{3,2,1,0:T(1,128)S(1)} %copy-done.1, f32[2,64,1,512]{3,1,0,2:T(8,128)S(1)} %bitcast.104, f32[512]{0:T(512)S(1)} %copy-done.5), kind=kLoop, calls=%fused_computation.30 | loop fusion | flops 655104 | bytes 1051648 | tf_op jit(solution)/shard_map/reduce_sum | solution.py:225
  72.7 0.2 reshape.358
  73.0 14.2 %all_to_all.16 = f32[128,1,256]{2,1,0:T(1,128)S(1)} all-to-all(f32[128,1,256]{2,1,0:T(1,128)S(1)} %reshape.358), channel_id=1, replica_groups=mesh['mgrp'=8,'band'=16] {'mgrp','band'}, dimensions={0} | all-to-all | bytes 262144 | tf_op jit(solution)/shard_map/all_to_all | solution.py:23
  87.2 0.5 broadcast.229
  87.7 1.0 %reduce = f32[128,256]{1,0:T(8,128)S(1)} reduce(f32[128,1,256]{2,1,0:T(1,128)S(1)} %all_to_all.16, f32[]{:T(128)} %broadcast.229), dimensions={1}, to_apply=%all_to_all.11.reduce_sub_computation | reduce | bytes 262148 | tf_op jit(solution)/shard_map/all_to_all | solution.py:23
  88.7 0.2 reshape.359
  88.8 0.1 reduce_sum.59
  89.0 1.6 %multiply_add_fusion = (f32[2,64,1,512]{3,2,1,0:T(1,128)}, f32[2,64,1,512]{3,2,1,0:T(1,128)}, f32[2,64,1,512]{3,2,1,0:T(1,128)}) fusion(f32[2,64,1,512]{3,2,1,0:T(1,128)S(1)} %copy-done.1, f32[64]{0:T(128)S(1)} %get-tuple-element.10, f32[2,64,1,512]{3,2,1,0:T(1,128)S(1)} %copy-done.2, f32[2,64,1,512]{3,2,1,0:T(1,128)S(1)} %get-tuple-element.12, ...), kind=kLoop, calls=%fused_computation.23 | loop fusion | flops 393216 | bytes 1835520 | tf_op jit(solution)/shard_map/add | solution.py:237
  (36 shorter events, 0.6 us)
Async XLA Ops:
  0.6 2.1 %copy-start = (bf16[1,1024,512]{2,1,0:T(8,128)(2,1)S(1)}, bf16[1,1024,512]{2,1,0:T(8,128)(2,1)}, u32[]{:S(2)}) copy-start(bf16[1,1024,512]{2,1,0:T(8,128)(2,1)} %param.15) | copy-start | bytes 3145732
  0.6 15.1 %copy-start.6 = (s32[8]{0:T(128)S(1)}, s32[8]{0:T(128)}, u32[]{:S(2)}) copy-start(s32[8]{0:T(128)} %length_ref.1) | copy-start | bytes 100
  0.7 15.3 %copy-start.7 = (s32[8]{0:T(128)S(1)}, s32[8]{0:T(128)}, u32[]{:S(2)}) copy-start(s32[8]{0:T(128)} %param.20) | copy-start | bytes 100
  4.3 25.3 %all-to-all-start = ((f32[128,8,128]{2,1,0:T(8,128)}), f32[128,8,128]{2,1,0:T(8,128)S(1)}, u32[]{:S(2)}, u32[]{:S(2)}) async-start(f32[128,8,128]{2,1,0:T(8,128)} %bitcast.7), calls=%async_computation | async-start | bytes 1048576 | tf_op jit(solution)/shard_map/all_to_all | solution.py:32
  20.2 2.3 %copy-start.4 = (bf16[8,64,64]{2,1,0:T(8,128)(2,1)S(1)}, bf16[8,64,64]{2,1,0:T(8,128)(2,1)}, u32[]{:S(2)}) copy-start(bf16[8,64,64]{2,1,0:T(8,128)(2,1)} %param.17) | copy-start | bytes 196612
  30.5 40.8 %copy-start.1 = (f32[2,64,1,512]{3,2,1,0:T(1,128)S(1)}, f32[2,64,1,512]{3,2,1,0:T(1,128)}, u32[]{:S(2)}) copy-start(f32[2,64,1,512]{3,2,1,0:T(1,128)} %param.14) | copy-start | bytes 786436
  30.5 40.8 %copy-start.2 = (f32[2,64,1,512]{3,2,1,0:T(1,128)S(1)}, f32[2,64,1,512]{3,2,1,0:T(1,128)}, u32[]{:S(2)}) copy-start(f32[2,64,1,512]{3,2,1,0:T(1,128)} %param.13) | copy-start | bytes 786436
  30.5 40.8 %copy-start.5 = (f32[512]{0:T(512)S(1)}, f32[512]{0:T(512)}, u32[]{:S(2)}) copy-start(f32[512]{0:T(512)} %param.16) | copy-start | bytes 6148
  49.5 39.5 %copy-start.3 = (f32[2,64,1,512]{3,2,1,0:T(1,128)S(1)}, f32[2,64,1,512]{3,2,1,0:T(1,128)}, u32[]{:S(2)}) copy-start(f32[2,64,1,512]{3,2,1,0:T(1,128)} %param.12) | copy-start | bytes 786436

commit v9 on v8

--- a/solution.py
+++ b/solution.py
@@ -126,11 +126,13 @@
         )
 
     length = length_ref[cycle]
+    mid = wide // 2
+    narrow = wide // 4
     full = length // wide
     rest = length - full * wide
-    narrow = wide // 2
-    wide_count = full + (rest > narrow).astype(jnp.int32)
-    narrow_count = ((rest > 0) & (rest <= narrow)).astype(jnp.int32)
+    wide_count = full + (rest > mid + narrow).astype(jnp.int32)
+    mid_count = ((rest > narrow) & (rest <= mid + narrow)).astype(jnp.int32)
+    narrow_count = (((rest > 0) & (rest <= narrow)) | ((rest > mid) & (rest <= mid + narrow))).astype(jnp.int32)
     total = lax.fori_loop(
         0,
         wide_count,
@@ -139,8 +141,14 @@
     )
     total = lax.fori_loop(
         0,
+        mid_count,
+        lambda step, acc: chunk(pl.multiple_of(full * wide, wide), mid, acc),
+        total,
+    )
+    total = lax.fori_loop(
+        0,
         narrow_count,
-        lambda step, acc: chunk(pl.multiple_of(full * wide, wide), narrow, acc),
+        lambda step, acc: chunk(pl.multiple_of(full * wide + mid_count * mid, mid), narrow, acc),
         total,
     )
     back_ref[0] = total.astype(back_ref.dtype)
@@ -166,7 +174,7 @@
             pl.BlockSpec(pairs_t.shape, lambda r, idx, n: (0, 0, 0)),
         ],
         out_specs=pl.BlockSpec((1, map_count, 2 * mode_count), lambda r, idx, n: (r, 0, 0)),
-        scratch_shapes=[pltpu.VMEM((map_count, 4096), jnp.bfloat16)],
+        scratch_shapes=[pltpu.VMEM((map_count, 8192), jnp.bfloat16)],
     )
     back = pl.pallas_call(
         noise_kernel,

time: 91.9 us -> 90.5 us (0.985)
  blocking collectives: 34.3 us -> 31.5 us
  Pallas kernels: 19 us -> 20.4 us
    all_to_all x1, blocking collectives: 20.1 us -> 17.3 us  [spread_cycles(): received = lax.all_to_all(pieces, MESH_AXES, 0, 0, tiled=True)]
    pallas_call x1, Pallas kernels: 19 us -> 20.4 us  [cycle_transform(): pl.pallas_call(noise_kernel, grid_spec=grid_spec, out_shape=jax.ShapeDtyp...]
where the time goes in v9:
time: 90.5 us; the launch traced here: 89.1 us
  blocking collectives  31.5 us (35%)
  Pallas kernels  20.4 us (23%)
  other arithmetic  14.6 us (16%)
  starting transfers between devices  11.5 us (13%)
  local copies, waits for them, and re-layouts  5.33 us (6%)
  waiting for transfers between devices  4.1 us (5%)
  between operations  0.93 us (1%)
    pallas_call x1, Pallas kernels, cycle_transform(): pl.pallas_call(noise_kernel, grid_spec=grid_spec, out_shape=jax.ShapeDtyp...  20.4 us
    all_to_all x1, blocking collectives, spread_cycles(): received = lax.all_to_all(pieces, MESH_AXES, 0, 0, tiled=True)  17.3 us
    all_to_all x1, blocking collectives, total_over_mesh(): return jnp.sum(lax.all_to_all(copies, MESH_AXES, 0, 0, tiled=True), axis=0)  14.2 us
    all_to_all x1, starting transfers between devices, gather_cycles(): received = lax.all_to_all(pieces, MESH_AXES, 0, 0, tiled=True)  11.5 us
    all_to_all x1, waiting for transfers between devices, gather_cycles(): received = lax.all_to_all(pieces, MESH_AXES, 0, 0, tiled=True)  4.1 us
    another operation x1, other arithmetic  2.81 us
    mul x1, other arithmetic, cycle_transform(): jnp.swapaxes(pair_table(noise_mats), 1, 2)  2.32 us
    convert_element_type x1, other arithmetic, cycle_tables(): return jnp.stack([cosine, sine_part], axis=1).astype(jnp.bfloat16)  2.29 us
  transfers between devices with their start and end apart: 1, of which 1 were waited for; matrix products, arithmetic and copies ran while one was open for 11% of the time, Pallas kernels for 0%

profile of v9, /device:TPU:1, one launch (start us, length us, event | category | flops | bytes accessed | tf_op | source)
XLA Modules:
  0.0 89.1 jit_solution(4476531390626814397)
XLA Ops:
  0.7 0.8 convert_bitcast_fusion.1
  1.6 1.1 %convert_element_type.61 = bf16[2,64,1,512]{3,2,1,0:T(2,128)(2,1)S(1)} convert(f32[2,64,1,512]{3,2,1,0:T(1,128)} %param.14) | non-fusion elementwise | flops 65536 | bytes 393216 | tf_op jit(solution)/shard_map/convert_element_type | solution.py:209
  2.7 0.5 fusion.9
  3.2 0.2 copy.72
  3.4 0.8 copy.73
  4.3 11.5 %all-to-all-start = ((f32[128,8,128]{2,1,0:T(8,128)}), f32[128,8,128]{2,1,0:T(8,128)S(1)}, u32[]{:S(2)}, u32[]{:S(2)}) async-start(f32[128,8,128]{2,1,0:T(8,128)} %bitcast.7), calls=%async_computation | async-start | bytes 1048576 | tf_op jit(solution)/shard_map/all_to_all | solution.py:32
  15.8 0.1 fusion.13
  16.0 1.0 %fusion.27 = (f32[8,8,128]{2,1,0:T(8,128)S(1)}, f32[8,8,128]{2,1,0:T(8,128)S(1)}, f32[8,8,128]{2,1,0:T(8,128)S(1)}, f32[8,8,128]{2,1,0:T(8,128)S(1)}) fusion(f32[8]{0:T(128)S(1)} %convert_element_type.68, pred[8]{0:T(512)(128)(4,1)S(1)} %compare_bitcast_fusion, s32[8]{0:T(128)S(1)} %fusion.31, s32[8,128]{1,0:T(8,128)S(1)} %get-tuple-element.26, ...), kind=kLoop, calls=%fused_computation.54 | loop fusion | flops 163840 | bytes 139336 | tf_op jit(solution)/shard_map/cos | solution.py:56
  17.0 0.2 copy.76
  17.2 0.2 copy.77
  17.4 2.8 %fusion.3 = (bf16[8,1,8,16384]{3,2,1,0:T(8,128)(2,1)S(1)}, bf16[8,1,8,16384]{3,2,1,0:T(8,128)(2,1)S(1)}) fusion(f32[8,16384]{1,0:T(8,128)S(1)} %fusion.13, f32[8,8,128]{2,1,0:T(8,128)S(1)} %get-tuple-element.20, f32[8,8,128]{1,2,0:T(8,128)S(1)} %copy.77, f32[8,8,128]{2,1,0:T(8,128)S(1)} %get-tuple-element.21, f32[8,8,128]{1,2,0:T(8,128)S(1)} %copy.76, ...), kind=kLoop, calls=%fused_computation.8 | loop fusion | flops 12582912 | bytes 4849728 | tf_op jit(solution)/shard_map/convert
  20.3 2.3 %maximum_bitcast_fusion.table_ref = bf16[8,16,16384]{2,1,0:T(8,128)(2,1)} fusion(bf16[8,1,8,16384]{3,2,1,0:T(8,128)(2,1)S(1)} %get-tuple-element.14, bf16[8,1,8,16384]{3,2,1,0:T(8,128)(2,1)S(1)} %get-tuple-element.13), kind=kLoop, calls=%fused_computation.2 | loop fusion | flops 2097152 | bytes 8388608 | tf_op jit(solution)/shard_map/convert_element_type | solution.py:69
  22.5 0.1 copy.78
  22.7 0.2 broadcast_in_dim.24
  22.9 0.2 broadcast_in_dim.25
  23.2 2.3 %fusion.7 = bf16[8,8,128,128]{2,3,1,0:T(8,128)(2,1)} fusion(bf16[8,8,64,64]{2,3,1,0:T(8,128)(2,1)S(1)} %broadcast_in_dim.25, bf16[8,8,64,64]{2,3,1,0:T(8,128)(2,1)S(1)} %broadcast_in_dim.24), kind=kLoop, calls=%fused_computation.12 | loop fusion | flops 10485760 | bytes 3145728 | tf_op jit(solution)/shard_map/mul | solution.py:167
  25.5 4.1 %all-to-all-done = f32[128,8,128]{2,1,0:T(8,128)S(1)} async-done(((f32[128,8,128]{2,1,0:T(8,128)}), f32[128,8,128]{2,1,0:T(8,128)S(1)}, u32[]{:S(2)}, u32[]{:S(2)}) %all-to-all-start) | async-done | bytes 524320 | tf_op jit(solution)/shard_map/all_to_all | solution.py:32
  29.8 0.8 copy.80.coeff_ref
  30.5 20.4 %shard_map.121 = bf16[8,64,16]{2,1,0:T(8,128)(2,1)} custom-call(s32[8,256]{1,0:T(8,128)} %index_ref.1, s32[8]{0:T(128)} %length_ref.1, bf16[8,64,16]{2,1,0:T(8,128)(2,1)} %copy.80.coeff_ref, bf16[8,16,16384]{2,1,0:T(8,128)(2,1)} %maximum_bitcast_fusion.table_ref, bf16[64,128,128]{2,1,0:T(8,128)(2,1)} %bitcast.99), custom_call_target="tpu_custom_call" | custom-call | tf_op jit(solution)/shard_map/pallas_call | solution.py:179
  50.9 1.0 %copy.81 = bf16[8,64,16]{1,2,0:T(8,128)(2,1)S(1)} copy(bf16[8,64,16]{2,1,0:T(8,128)(2,1)} %shard_map.121) | data formatting | bytes 32768 | tf_op jit(solution)/shard_map/pallas_call | solution.py:179
  52.0 0.1 reshape.354
  52.1 17.3 %all_to_all.15 = bf16[128,8,128]{2,1,0:T(8,128)(2,1)S(1)} all-to-all(bf16[128,8,128]{2,1,0:T(8,128)(2,1)S(1)} %bitcast.102), channel_id=1, replica_groups=mesh['mgrp'=8,'band'=16] {'mgrp','band'}, dimensions={0} | all-to-all | bytes 524288 | tf_op jit(solution)/shard_map/all_to_all | solution.py:42
  69.4 0.1 multiply_bitcast_fusion
  69.6 0.3 fusion.10
  70.0 1.3 %multiply_reduce_fusion.3 = (f32[64]{0:T(128)S(1)}, f32[64]{0:T(128)S(1)}, f32[64]{0:T(128)S(1)}, f32[64]{0:T(128)S(1)}, f32[2,64,1,512]{3,2,1,0:T(1,128)S(1)}) fusion(f32[2,64,1,512]{3,2,1,0:T(1,128)S(1)} %copy-done.2, f32[2,64,1,512]{3,2,1,0:T(1,128)S(1)} %copy-done.1, f32[2,64,1,512]{3,1,0,2:T(8,128)S(1)} %bitcast.104, f32[512]{0:T(512)S(1)} %copy-done.5), kind=kLoop, calls=%fused_computation.30 | loop fusion | flops 655104 | bytes 1051648 | tf_op jit(solution)/shard_map/reduce_sum | solution.py:233
  71.3 0.2 reshape.358
  71.6 14.2 %all_to_all.16 = f32[128,1,256]{2,1,0:T(1,128)S(1)} all-to-all(f32[128,1,256]{2,1,0:T(1,128)S(1)} %reshape.358), channel_id=1, replica_groups=mesh['mgrp'=8,'band'=16] {'mgrp','band'}, dimensions={0} | all-to-all | bytes 262144 | tf_op jit(solution)/shard_map/all_to_all | solution.py:23
  85.8 0.5 broadcast.229
  86.3 1.0 %reduce = f32[128,256]{1,0:T(8,128)S(1)} reduce(f32[128,1,256]{2,1,0:T(1,128)S(1)} %all_to_all.16, f32[]{:T(128)} %broadcast.229), dimensions={1}, to_apply=%all_to_all.11.reduce_sub_computation | reduce | bytes 262148 | tf_op jit(solution)/shard_map/all_to_all | solution.py:23
  87.2 0.2 reshape.359
  87.4 0.1 reduce_sum.59
  87.6 1.6 %multiply_add_fusion = (f32[2,64,1,512]{3,2,1,0:T(1,128)}, f32[2,64,1,512]{3,2,1,0:T(1,128)}, f32[2,64,1,512]{3,2,1,0:T(1,128)}) fusion(f32[2,64,1,512]{3,2,1,0:T(1,128)S(1)} %copy-done.1, f32[64]{0:T(128)S(1)} %get-tuple-element.10, f32[2,64,1,512]{3,2,1,0:T(1,128)S(1)} %copy-done.2, f32[2,64,1,512]{3,2,1,0:T(1,128)S(1)} %get-tuple-element.12, ...), kind=kLoop, calls=%fused_computation.23 | loop fusion | flops 393216 | bytes 1835520 | tf_op jit(solution)/shard_map/add | solution.py:245
  (36 shorter events, 0.6 us)
Async XLA Ops:
  0.6 2.1 %copy-start = (bf16[1,1024,512]{2,1,0:T(8,128)(2,1)S(1)}, bf16[1,1024,512]{2,1,0:T(8,128)(2,1)}, u32[]{:S(2)}) copy-start(bf16[1,1024,512]{2,1,0:T(8,128)(2,1)} %param.15) | copy-start | bytes 3145732
  0.6 15.1 %copy-start.6 = (s32[8]{0:T(128)S(1)}, s32[8]{0:T(128)}, u32[]{:S(2)}) copy-start(s32[8]{0:T(128)} %length_ref.1) | copy-start | bytes 100
  0.7 15.3 %copy-start.7 = (s32[8]{0:T(128)S(1)}, s32[8]{0:T(128)}, u32[]{:S(2)}) copy-start(s32[8]{0:T(128)} %param.20) | copy-start | bytes 100
  4.3 25.3 %all-to-all-start = ((f32[128,8,128]{2,1,0:T(8,128)}), f32[128,8,128]{2,1,0:T(8,128)S(1)}, u32[]{:S(2)}, u32[]{:S(2)}) async-start(f32[128,8,128]{2,1,0:T(8,128)} %bitcast.7), calls=%async_computation | async-start | bytes 1048576 | tf_op jit(solution)/shard_map/all_to_all | solution.py:32
  20.2 2.3 %copy-start.4 = (bf16[8,64,64]{2,1,0:T(8,128)(2,1)S(1)}, bf16[8,64,64]{2,1,0:T(8,128)(2,1)}, u32[]{:S(2)}) copy-start(bf16[8,64,64]{2,1,0:T(8,128)(2,1)} %param.17) | copy-start | bytes 196612
  30.5 39.4 %copy-start.1 = (f32[2,64,1,512]{3,2,1,0:T(1,128)S(1)}, f32[2,64,1,512]{3,2,1,0:T(1,128)}, u32[]{:S(2)}) copy-start(f32[2,64,1,512]{3,2,1,0:T(1,128)} %param.14) | copy-start | bytes 786436
  30.5 39.4 %copy-start.2 = (f32[2,64,1,512]{3,2,1,0:T(1,128)S(1)}, f32[2,64,1,512]{3,2,1,0:T(1,128)}, u32[]{:S(2)}) copy-start(f32[2,64,1,512]{3,2,1,0:T(1,128)} %param.13) | copy-start | bytes 786436
  30.5 39.4 %copy-start.5 = (f32[512]{0:T(512)S(1)}, f32[512]{0:T(512)}, u32[]{:S(2)}) copy-start(f32[512]{0:T(512)} %param.16) | copy-start | bytes 6148
  50.9 36.7 %copy-start.3 = (f32[2,64,1,512]{3,2,1,0:T(1,128)S(1)}, f32[2,64,1,512]{3,2,1,0:T(1,128)}, u32[]{:S(2)}) copy-start(f32[2,64,1,512]{3,2,1,0:T(1,128)} %param.12) | copy-start | bytes 786436

commit v10 on v9

--- a/solution.py
+++ b/solution.py
@@ -171,7 +171,7 @@
         in_specs=[
             pl.BlockSpec((1, map_count, 2 * mode_count), lambda r, idx, n: (r, 0, 0)),
             pl.BlockSpec((1, 2 * mode_count, RLEN), lambda r, idx, n: (r, 0, 0)),
-            pl.BlockSpec(pairs_t.shape, lambda r, idx, n: (0, 0, 0)),
+            pl.BlockSpec(memory_space=pltpu.MemorySpace.VMEM),
         ],
         out_specs=pl.BlockSpec((1, map_count, 2 * mode_count), lambda r, idx, n: (r, 0, 0)),
         scratch_shapes=[pltpu.VMEM((map_count, 8192), jnp.bfloat16)],

time: 90.5 us -> 89 us (0.983)
  Pallas kernels: 20.4 us -> 16.6 us
  blocking collectives: 31.5 us -> 34.6 us
    pallas_call x1, Pallas kernels: 20.4 us -> 16.6 us  [cycle_transform(): pl.pallas_call(noise_kernel, grid_spec=grid_spec, out_shape=jax.ShapeDtyp...]
    all_to_all x1, blocking collectives: 17.3 us -> 20.4 us  [spread_cycles(): received = lax.all_to_all(pieces, MESH_AXES, 0, 0, tiled=True)]
where the time goes in v10:
time: 89 us; the launch traced here: 88.5 us
  blocking collectives  34.6 us (39%)
  Pallas kernels  16.6 us (19%)
  other arithmetic  14.6 us (16%)
  starting transfers between devices  11.5 us (13%)
  local copies, waits for them, and re-layouts  5.33 us (6%)
  waiting for transfers between devices  4.1 us (5%)
  between operations  0.93 us (1%)
    all_to_all x1, blocking collectives, spread_cycles(): received = lax.all_to_all(pieces, MESH_AXES, 0, 0, tiled=True)  20.4 us
    pallas_call x1, Pallas kernels, cycle_transform(): pl.pallas_call(noise_kernel, grid_spec=grid_spec, out_shape=jax.ShapeDtyp...  16.6 us
    all_to_all x1, blocking collectives, total_over_mesh(): return jnp.sum(lax.all_to_all(copies, MESH_AXES, 0, 0, tiled=True), axis=0)  14.2 us
    all_to_all x1, starting transfers between devices, gather_cycles(): received = lax.all_to_all(pieces, MESH_AXES, 0, 0, tiled=True)  11.5 us
    all_to_all x1, waiting for transfers between devices, gather_cycles(): received = lax.all_to_all(pieces, MESH_AXES, 0, 0, tiled=True)  4.1 us
    another operation x1, other arithmetic  2.81 us
    mul x1, other arithmetic, cycle_transform(): jnp.swapaxes(pair_table(noise_mats), 1, 2)  2.32 us
    convert_element_type x1, other arithmetic, cycle_tables(): return jnp.stack([cosine, sine_part], axis=1).astype(jnp.bfloat16)  2.29 us
  transfers between devices with their start and end apart: 1, of which 1 were waited for; matrix products, arithmetic and copies ran while one was open for 11% of the time, Pallas kernels for 0%

profile of v10, /device:TPU:1, one launch (start us, length us, event | category | flops | bytes accessed | tf_op | source)
XLA Modules:
  0.0 88.5 jit_solution(4476531390626814397)
XLA Ops:
  0.7 0.8 convert_bitcast_fusion.1
  1.6 1.1 %convert_element_type.61 = bf16[2,64,1,512]{3,2,1,0:T(2,128)(2,1)S(1)} convert(f32[2,64,1,512]{3,2,1,0:T(1,128)} %param.14) | non-fusion elementwise | flops 65536 | bytes 393216 | tf_op jit(solution)/shard_map/convert_element_type | solution.py:209
  2.7 0.5 fusion.9
  3.2 0.2 copy.72
  3.4 0.8 copy.73
  4.3 11.5 %all-to-all-start = ((f32[128,8,128]{2,1,0:T(8,128)}), f32[128,8,128]{2,1,0:T(8,128)S(1)}, u32[]{:S(2)}, u32[]{:S(2)}) async-start(f32[128,8,128]{2,1,0:T(8,128)} %bitcast.7), calls=%async_computation | async-start | bytes 1048576 | tf_op jit(solution)/shard_map/all_to_all | solution.py:32
  15.8 0.1 fusion.13
  16.0 1.0 %fusion.27 = (f32[8,8,128]{2,1,0:T(8,128)S(1)}, f32[8,8,128]{2,1,0:T(8,128)S(1)}, f32[8,8,128]{2,1,0:T(8,128)S(1)}, f32[8,8,128]{2,1,0:T(8,128)S(1)}) fusion(f32[8]{0:T(128)S(1)} %convert_element_type.68, pred[8]{0:T(512)(128)(4,1)S(1)} %compare_bitcast_fusion, s32[8]{0:T(128)S(1)} %fusion.31, s32[8,128]{1,0:T(8,128)S(1)} %get-tuple-element.26, ...), kind=kLoop, calls=%fused_computation.54 | loop fusion | flops 163840 | bytes 139336 | tf_op jit(solution)/shard_map/cos | solution.py:56
  17.0 0.2 copy.76
  17.2 0.2 copy.77
  17.4 2.8 %fusion.3 = (bf16[8,1,8,16384]{3,2,1,0:T(8,128)(2,1)S(1)}, bf16[8,1,8,16384]{3,2,1,0:T(8,128)(2,1)S(1)}) fusion(f32[8,16384]{1,0:T(8,128)S(1)} %fusion.13, f32[8,8,128]{2,1,0:T(8,128)S(1)} %get-tuple-element.20, f32[8,8,128]{1,2,0:T(8,128)S(1)} %copy.77, f32[8,8,128]{2,1,0:T(8,128)S(1)} %get-tuple-element.21, f32[8,8,128]{1,2,0:T(8,128)S(1)} %copy.76, ...), kind=kLoop, calls=%fused_computation.8 | loop fusion | flops 12582912 | bytes 4849728 | tf_op jit(solution)/shard_map/convert
  20.3 2.3 %maximum_bitcast_fusion.table_ref = bf16[8,16,16384]{2,1,0:T(8,128)(2,1)} fusion(bf16[8,1,8,16384]{3,2,1,0:T(8,128)(2,1)S(1)} %get-tuple-element.14, bf16[8,1,8,16384]{3,2,1,0:T(8,128)(2,1)S(1)} %get-tuple-element.13), kind=kLoop, calls=%fused_computation.2 | loop fusion | flops 2097152 | bytes 8388608 | tf_op jit(solution)/shard_map/convert_element_type | solution.py:69
  22.5 0.1 copy.78
  22.7 0.2 broadcast_in_dim.24
  22.9 0.2 broadcast_in_dim.25
  23.2 2.3 %fusion.7 = bf16[8,8,128,128]{2,3,1,0:T(8,128)(2,1)} fusion(bf16[8,8,64,64]{2,3,1,0:T(8,128)(2,1)S(1)} %broadcast_in_dim.25, bf16[8,8,64,64]{2,3,1,0:T(8,128)(2,1)S(1)} %broadcast_in_dim.24), kind=kLoop, calls=%fused_computation.12 | loop fusion | flops 10485760 | bytes 3145728 | tf_op jit(solution)/shard_map/mul | solution.py:167
  25.5 4.1 %all-to-all-done = f32[128,8,128]{2,1,0:T(8,128)S(1)} async-done(((f32[128,8,128]{2,1,0:T(8,128)}), f32[128,8,128]{2,1,0:T(8,128)S(1)}, u32[]{:S(2)}, u32[]{:S(2)}) %all-to-all-start) | async-done | bytes 524320 | tf_op jit(solution)/shard_map/all_to_all | solution.py:32
  29.8 0.8 copy.80.coeff_ref
  30.5 16.6 %shard_map.121 = bf16[8,64,16]{2,1,0:T(8,128)(2,1)} custom-call(s32[8,256]{1,0:T(8,128)} %index_ref.1, s32[8]{0:T(128)} %length_ref.1, bf16[8,64,16]{2,1,0:T(8,128)(2,1)} %copy.80.coeff_ref, bf16[8,16,16384]{2,1,0:T(8,128)(2,1)} %maximum_bitcast_fusion.table_ref, bf16[64,128,128]{2,1,0:T(8,128)(2,1)} %bitcast.99), custom_call_target="tpu_custom_call" | custom-call | tf_op jit(solution)/shard_map/pallas_call | solution.py:179
  47.2 1.0 %copy.81 = bf16[8,64,16]{1,2,0:T(8,128)(2,1)S(1)} copy(bf16[8,64,16]{2,1,0:T(8,128)(2,1)} %shard_map.121) | data formatting | bytes 32768 | tf_op jit(solution)/shard_map/pallas_call | solution.py:179
  48.2 0.1 reshape.354
  48.4 20.4 %all_to_all.15 = bf16[128,8,128]{2,1,0:T(8,128)(2,1)S(1)} all-to-all(bf16[128,8,128]{2,1,0:T(8,128)(2,1)S(1)} %bitcast.102), channel_id=1, replica_groups=mesh['mgrp'=8,'band'=16] {'mgrp','band'}, dimensions={0} | all-to-all | bytes 524288 | tf_op jit(solution)/shard_map/all_to_all | solution.py:42
  68.7 0.1 multiply_bitcast_fusion
  68.9 0.3 fusion.10
  69.3 1.3 %multiply_reduce_fusion.3 = (f32[64]{0:T(128)S(1)}, f32[64]{0:T(128)S(1)}, f32[64]{0:T(128)S(1)}, f32[64]{0:T(128)S(1)}, f32[2,64,1,512]{3,2,1,0:T(1,128)S(1)}) fusion(f32[2,64,1,512]{3,2,1,0:T(1,128)S(1)} %copy-done.2, f32[2,64,1,512]{3,2,1,0:T(1,128)S(1)} %copy-done.1, f32[2,64,1,512]{3,1,0,2:T(8,128)S(1)} %bitcast.104, f32[512]{0:T(512)S(1)} %copy-done.5), kind=kLoop, calls=%fused_computation.30 | loop fusion | flops 655104 | bytes 1051648 | tf_op jit(solution)/shard_map/reduce_sum | solution.py:233
  70.6 0.2 reshape.358
  70.9 14.2 %all_to_all.16 = f32[128,1,256]{2,1,0:T(1,128)S(1)} all-to-all(f32[128,1,256]{2,1,0:T(1,128)S(1)} %reshape.358), channel_id=1, replica_groups=mesh['mgrp'=8,'band'=16] {'mgrp','band'}, dimensions={0} | all-to-all | bytes 262144 | tf_op jit(solution)/shard_map/all_to_all | solution.py:23
  85.1 0.5 broadcast.229
  85.6 1.0 %reduce = f32[128,256]{1,0:T(8,128)S(1)} reduce(f32[128,1,256]{2,1,0:T(1,128)S(1)} %all_to_all.16, f32[]{:T(128)} %broadcast.229), dimensions={1}, to_apply=%all_to_all.11.reduce_sub_computation | reduce | bytes 262148 | tf_op jit(solution)/shard_map/all_to_all | solution.py:23
  86.6 0.2 reshape.359
  86.7 0.1 reduce_sum.59
  86.9 1.6 %multiply_add_fusion = (f32[2,64,1,512]{3,2,1,0:T(1,128)}, f32[2,64,1,512]{3,2,1,0:T(1,128)}, f32[2,64,1,512]{3,2,1,0:T(1,128)}) fusion(f32[2,64,1,512]{3,2,1,0:T(1,128)S(1)} %copy-done.1, f32[64]{0:T(128)S(1)} %get-tuple-element.10, f32[2,64,1,512]{3,2,1,0:T(1,128)S(1)} %copy-done.2, f32[2,64,1,512]{3,2,1,0:T(1,128)S(1)} %get-tuple-element.12, ...), kind=kLoop, calls=%fused_computation.23 | loop fusion | flops 393216 | bytes 1835520 | tf_op jit(solution)/shard_map/add | solution.py:245
  (36 shorter events, 0.6 us)
Async XLA Ops:
  0.6 2.1 %copy-start = (bf16[1,1024,512]{2,1,0:T(8,128)(2,1)S(1)}, bf16[1,1024,512]{2,1,0:T(8,128)(2,1)}, u32[]{:S(2)}) copy-start(bf16[1,1024,512]{2,1,0:T(8,128)(2,1)} %param.15) | copy-start | bytes 3145732
  0.6 15.1 %copy-start.6 = (s32[8]{0:T(128)S(1)}, s32[8]{0:T(128)}, u32[]{:S(2)}) copy-start(s32[8]{0:T(128)} %length_ref.1) | copy-start | bytes 100
  0.7 15.3 %copy-start.7 = (s32[8]{0:T(128)S(1)}, s32[8]{0:T(128)}, u32[]{:S(2)}) copy-start(s32[8]{0:T(128)} %param.20) | copy-start | bytes 100
  4.3 25.3 %all-to-all-start = ((f32[128,8,128]{2,1,0:T(8,128)}), f32[128,8,128]{2,1,0:T(8,128)S(1)}, u32[]{:S(2)}, u32[]{:S(2)}) async-start(f32[128,8,128]{2,1,0:T(8,128)} %bitcast.7), calls=%async_computation | async-start | bytes 1048576 | tf_op jit(solution)/shard_map/all_to_all | solution.py:32
  20.2 2.3 %copy-start.4 = (bf16[8,64,64]{2,1,0:T(8,128)(2,1)S(1)}, bf16[8,64,64]{2,1,0:T(8,128)(2,1)}, u32[]{:S(2)}) copy-start(bf16[8,64,64]{2,1,0:T(8,128)(2,1)} %param.17) | copy-start | bytes 196612
  30.5 38.7 %copy-start.1 = (f32[2,64,1,512]{3,2,1,0:T(1,128)S(1)}, f32[2,64,1,512]{3,2,1,0:T(1,128)}, u32[]{:S(2)}) copy-start(f32[2,64,1,512]{3,2,1,0:T(1,128)} %param.14) | copy-start | bytes 786436
  30.5 38.7 %copy-start.2 = (f32[2,64,1,512]{3,2,1,0:T(1,128)S(1)}, f32[2,64,1,512]{3,2,1,0:T(1,128)}, u32[]{:S(2)}) copy-start(f32[2,64,1,512]{3,2,1,0:T(1,128)} %param.13) | copy-start | bytes 786436
  30.5 38.8 %copy-start.5 = (f32[512]{0:T(512)S(1)}, f32[512]{0:T(512)}, u32[]{:S(2)}) copy-start(f32[512]{0:T(512)} %param.16) | copy-start | bytes 6148
  47.2 39.7 %copy-start.3 = (f32[2,64,1,512]{3,2,1,0:T(1,128)S(1)}, f32[2,64,1,512]{3,2,1,0:T(1,128)}, u32[]{:S(2)}) copy-start(f32[2,64,1,512]{3,2,1,0:T(1,128)} %param.12) | copy-start | bytes 786436

commit v11 on v9

--- a/solution.py
+++ b/solution.py
@@ -27,11 +27,42 @@
     cycle_total, columns = partials.shape
     group_count = lax.axis_size("mgrp")
     own = cycle_total // (band_count * group_count)
-    pieces = partials.reshape(band_count, group_count, own, columns).transpose(1, 0, 2, 3)
-    pieces = pieces.reshape(group_count * band_count, own, columns)
+    pieces = partials.reshape(group_count * band_count, own, columns)
     received = lax.all_to_all(pieces, MESH_AXES, 0, 0, tiled=True)
     received = received.reshape(group_count, band_count, own, columns)
     return jnp.sum(received, axis=1).transpose(1, 0, 2)
+
+
+def forward_kernel(cut_ref, leg_ref, dir_ref, out_ref, *, band_count, group_count):
+    cycle_total = leg_ref.shape[0]
+    own = cycle_total // (band_count * group_count)
+    rounded = dir_ref[...].astype(jnp.bfloat16)
+    products = lax.dot_general(
+        leg_ref[...], rounded, (((1,), (1,)), ((), ())), preferred_element_type=jnp.float32
+    )
+    for band in range(band_count):
+        for group in range(group_count):
+            first = (band * group_count + group) * own
+            target = (group * band_count + band) * own
+            keep = cut_ref[0, first // RB] != 0
+            out_ref[target:target + own, :] = jnp.where(keep, products[first:first + own], 0.0)
+
+
+def forward_products(cut_pattern, legendre, direction, band_count):
+    cycle_total, l_local = legendre.shape[1], legendre.shape[2]
+    columns = direction.shape[0] * direction.shape[1]
+    return pl.pallas_call(
+        functools.partial(
+            forward_kernel, band_count=band_count, group_count=lax.axis_size("mgrp")
+        ),
+        in_specs=[
+            pl.BlockSpec(memory_space=pltpu.MemorySpace.SMEM),
+            pl.BlockSpec(memory_space=pltpu.MemorySpace.VMEM),
+            pl.BlockSpec(memory_space=pltpu.MemorySpace.VMEM),
+        ],
+        out_specs=pl.BlockSpec(memory_space=pltpu.MemorySpace.VMEM),
+        out_shape=jax.ShapeDtypeStruct((cycle_total, columns), jnp.float32),
+    )(cut_pattern, legendre[0], direction.reshape(columns, l_local))
 
 
 def spread_cycles(backward, band_count):
@@ -206,16 +237,13 @@
     columns = 2 * map_count
     band_rows = cycle_total // band_count
     weight = L / (cycle_total * RLEN)
-    rounded = direction.astype(jnp.bfloat16).reshape(columns, mode_local, l_local)
 
     def row_mask(first_row, row_count):
         block_flags = lax.dynamic_slice_in_dim(cut_pattern, first_row // RB, row_count // RB, 1)
         return jnp.repeat(block_flags, RB, axis=1).T
 
-    section = legendre
-    products = jnp.einsum("mrl,nml->rmn", section, rounded, preferred_element_type=jnp.float32)
-    masked_products = products * row_mask(jnp.int32(0), cycle_total).astype(jnp.float32)[:, :, None]
-    coeffs = gather_cycles(masked_products.reshape(cycle_total, columns), band_count).astype(jnp.bfloat16)
+    masked_products = forward_products(cut_pattern, legendre, direction, band_count)
+    coeffs = gather_cycles(masked_products, band_count).astype(jnp.bfloat16)
     cycle_local = coeffs.shape[0]
     mode_total = coeffs.shape[1]
     outputs = cycle_transform(coeffs, cycle_lengths, noise_index, m_values, noise_mats, weight)

time: 90.5 us -> 94.9 us (1.049); the launches traced: 89.1 us -> 94.8 us
  blocking collectives: 31.5 us -> 14.2 us
  starting transfers between devices: 11.5 us -> 22.4 us
  waiting for transfers between devices: 4.1 us -> 11.4 us
  other arithmetic: 14.6 us -> 16.7 us
  Pallas kernels: 20.4 us -> 22.4 us
  local copies, waits for them, and re-layouts: 5.33 us -> 6.49 us
    all_to_all x1 -> x0, blocking collectives: 17.3 us -> none  [spread_cycles(): received = lax.all_to_all(pieces, MESH_AXES, 0, 0, tiled=True)]
    all_to_all x0 -> x1, waiting for transfers between devices: none -> 11.2 us  [spread_cycles(): received = lax.all_to_all(pieces, MESH_AXES, 0, 0, tiled=True)]
    all_to_all x0 -> x1, starting transfers between devices: none -> 10.9 us  [spread_cycles(): received = lax.all_to_all(pieces, MESH_AXES, 0, 0, tiled=True)]
    all_to_all x1, waiting for transfers between devices: 4.1 us -> 0.22 us  [gather_cycles(): received = lax.all_to_all(pieces, MESH_AXES, 0, 0, tiled=True)]
    pallas_call x0 -> x1, Pallas kernels: none -> 2.51 us  [forward_products(): pl.pallas_call(functools.partial(forward_kernel, band_count=band_count, g...]
    unnamed x20 -> x18, local copies, waits for them, and re-layouts: 0.59 us -> 2.22 us
    rem x2, other arithmetic: 0.08 us -> 1.38 us  [cycle_tables(): m_values[None, :, None] * coarse[None, None, :] % lengths[:, None, None]]
    convert_element_type x1 -> x0, other arithmetic: 1.13 us -> none  [shards(): direction.astype(jnp.bfloat16).reshape(columns, mode_local, l_local)]
  transfers between devices with their start and end apart: 1 -> 2, of which waited for: 1 -> 2; matrix products, arithmetic and copies ran while one was open for 11% -> 14% of each run, Pallas kernels for 0% -> 0%
where the time goes in v11:
time: 94.9 us; the launch traced here: 94.8 us
  Pallas kernels  22.4 us (24%)
  starting transfers between devices  22.4 us (24%)
  other arithmetic  16.7 us (18%)
  blocking collectives  14.2 us (15%)
  waiting for transfers between devices  11.4 us (12%)
  local copies, waits for them, and re-layouts  6.49 us (7%)
    pallas_call x1, Pallas kernels, cycle_transform(): pl.pallas_call(noise_kernel, grid_spec=grid_spec, out_shape=jax.ShapeDtyp...  19.9 us
    all_to_all x1, blocking collectives, total_over_mesh(): return jnp.sum(lax.all_to_all(copies, MESH_AXES, 0, 0, tiled=True), axis=0)  14.2 us
    all_to_all x1, starting transfers between devices, gather_cycles(): received = lax.all_to_all(pieces, MESH_AXES, 0, 0, tiled=True)  11.5 us
    all_to_all x1, waiting for transfers between devices, spread_cycles(): received = lax.all_to_all(pieces, MESH_AXES, 0, 0, tiled=True)  11.2 us
    all_to_all x1, starting transfers between devices, spread_cycles(): received = lax.all_to_all(pieces, MESH_AXES, 0, 0, tiled=True)  10.9 us
    another operation x1, other arithmetic  2.81 us
    pallas_call x1, Pallas kernels, forward_products(): pl.pallas_call(functools.partial(forward_kernel, band_count=band_count, g...  2.51 us
    mul x1, other arithmetic, cycle_transform(): jnp.swapaxes(pair_table(noise_mats), 1, 2)  2.32 us
  transfers between devices with their start and end apart: 2, of which 2 were waited for; matrix products, arithmetic and copies ran while one was open for 14% of the time, Pallas kernels for 0%

profile of v11, /device:TPU:1, one launch (start us, length us, event | category | flops | bytes accessed | tf_op | source)
XLA Modules:
  0.0 94.8 jit_solution(15888709206636030101)
XLA Ops:
  0.6 1.7 %copy.77 = f32[2,64,1,512]{3,1,2,0:T(8,128)} copy(f32[2,64,1,512]{3,2,1,0:T(1,128)} %param.14) | data formatting | bytes 524288
  2.3 2.5 %shard_map.121 = f32[1024,128]{1,0:T(8,128)} custom-call(s32[1,16]{1,0:T(1,128)} %cut_ref.1, bf16[1024,512]{1,0:T(8,128)(2,1)} %bitcast.84, f32[128,512]{1,0:T(8,128)} %bitcast.88), custom_call_target="tpu_custom_call" | custom-call | tf_op jit(solution)/shard_map/pallas_call | solution.py:54
  4.8 11.5 %all-to-all-start = ((f32[128,8,128]{2,1,0:T(8,128)}), f32[128,8,128]{2,1,0:T(8,128)S(1)}, u32[]{:S(2)}, u32[]{:S(2)}) async-start(f32[128,8,128]{2,1,0:T(8,128)} %bitcast.85), calls=%async_computation | async-start | bytes 1048576 | tf_op jit(solution)/shard_map/all_to_all | solution.py:31
  16.3 0.7 compare_bitcast_fusion
  17.0 0.7 convert_element_type.45
  17.6 0.7 fusion.26
  18.3 0.8 fusion.8
  19.1 0.7 compare_select_fusion.1
  19.7 0.7 multiply_bitcast_fusion.2
  20.5 1.0 %fusion.22 = (f32[8,8,128]{2,1,0:T(8,128)S(1)}, f32[8,8,128]{2,1,0:T(8,128)S(1)}, f32[8,8,128]{2,1,0:T(8,128)S(1)}, f32[8,8,128]{2,1,0:T(8,128)S(1)}) fusion(f32[8]{0:T(128)S(1)} %convert_element_type.45, pred[8]{0:T(512)(128)(4,1)S(1)} %compare_bitcast_fusion, s32[8]{0:T(128)S(1)} %fusion.26, s32[8,128]{1,0:T(8,128)S(1)} %get-tuple-element.24, ...), kind=kLoop, calls=%fused_computation.48 | loop fusion | flops 163840 | bytes 139336 | tf_op jit(solution)/shard_map/cos | solution.py:87
  21.4 0.2 copy.66
  21.6 0.2 copy.67
  21.8 2.8 %fusion.3 = (bf16[8,1,8,16384]{3,2,1,0:T(8,128)(2,1)S(1)}, bf16[8,1,8,16384]{3,2,1,0:T(8,128)(2,1)S(1)}) fusion(f32[8,16384]{1,0:T(8,128)S(1)} %fusion.8, f32[8,8,128]{2,1,0:T(8,128)S(1)} %get-tuple-element.20, f32[8,8,128]{1,2,0:T(8,128)S(1)} %copy.67, f32[8,8,128]{2,1,0:T(8,128)S(1)} %get-tuple-element.21, f32[8,8,128]{1,2,0:T(8,128)S(1)} %copy.66, ...), kind=kLoop, calls=%fused_computation.8 | loop fusion | flops 12582912 | bytes 4849728 | tf_op jit(solution)/shard_map/convert
  24.7 2.3 %maximum_bitcast_fusion.table_ref = bf16[8,16,16384]{2,1,0:T(8,128)(2,1)} fusion(bf16[8,1,8,16384]{3,2,1,0:T(8,128)(2,1)S(1)} %get-tuple-element.14, bf16[8,1,8,16384]{3,2,1,0:T(8,128)(2,1)S(1)} %get-tuple-element.13), kind=kLoop, calls=%fused_computation.2 | loop fusion | flops 2097152 | bytes 8388608 | tf_op jit(solution)/shard_map/convert_element_type | solution.py:100
  27.1 0.2 broadcast_in_dim.21
  27.4 0.2 broadcast_in_dim.22
  27.6 2.3 %fusion.7 = bf16[8,8,128,128]{2,3,1,0:T(8,128)(2,1)} fusion(bf16[8,8,64,64]{2,3,1,0:T(8,128)(2,1)S(1)} %broadcast_in_dim.22, bf16[8,8,64,64]{2,3,1,0:T(8,128)(2,1)S(1)} %broadcast_in_dim.21), kind=kLoop, calls=%fused_computation.12 | loop fusion | flops 10485760 | bytes 3145728 | tf_op jit(solution)/shard_map/mul | solution.py:198
  29.9 0.2 all-to-all-done
  30.3 0.8 copy.70.coeff_ref
  31.1 19.9 %shard_map.122 = bf16[8,64,16]{2,1,0:T(8,128)(2,1)} custom-call(s32[8,256]{1,0:T(8,128)} %index_ref.1, s32[8]{0:T(128)} %length_ref.1, bf16[8,64,16]{2,1,0:T(8,128)(2,1)} %copy.70.coeff_ref, bf16[8,16,16384]{2,1,0:T(8,128)(2,1)} %maximum_bitcast_fusion.table_ref, bf16[64,128,128]{2,1,0:T(8,128)(2,1)} %bitcast.83), custom_call_target="tpu_custom_call" | custom-call | tf_op jit(solution)/shard_map/pallas_call | solution.py:210
  51.0 1.0 %copy.71 = bf16[8,64,16]{1,2,0:T(8,128)(2,1)S(1)} copy(bf16[8,64,16]{2,1,0:T(8,128)(2,1)} %shard_map.122) | data formatting | bytes 32768 | tf_op jit(solution)/shard_map/pallas_call | solution.py:210
  52.1 0.7 broadcast_in_dim.23
  52.9 10.9 %all-to-all-start.1 = ((bf16[128,8,128]{2,1,0:T(8,128)(2,1)}), bf16[128,8,128]{2,1,0:T(8,128)(2,1)S(1)}, u32[]{:S(2)}, u32[]{:S(2)}) async-start(bf16[128,8,128]{2,1,0:T(8,128)(2,1)} %bitcast.22), calls=%async_computation.1 | async-start | bytes 524288 | tf_op jit(solution)/shard_map/all_to_all | solution.py:73
  63.8 11.2 %all-to-all-done.1 = bf16[128,8,128]{2,1,0:T(8,128)(2,1)S(1)} async-done(((bf16[128,8,128]{2,1,0:T(8,128)(2,1)}), bf16[128,8,128]{2,1,0:T(8,128)(2,1)S(1)}, u32[]{:S(2)}, u32[]{:S(2)}) %all-to-all-start.1) | async-done | bytes 262176 | tf_op jit(solution)/shard_map/all_to_all | solution.py:73
  75.2 0.3 fusion.27
  75.6 1.3 %multiply_reduce_fusion.3 = (f32[64]{0:T(128)S(1)}, f32[64]{0:T(128)S(1)}, f32[64]{0:T(128)S(1)}, f32[64]{0:T(128)S(1)}, f32[2,64,1,512]{3,2,1,0:T(1,128)S(1)}) fusion(f32[2,64,1,512]{3,2,1,0:T(1,128)S(1)} %copy-done.2, f32[2,64,1,512]{3,2,1,0:T(1,128)S(1)} %copy-done.1, f32[2,64,1,512]{3,1,0,2:T(8,128)S(1)} %bitcast.89, f32[512]{0:T(512)S(1)} %copy-done.5), kind=kLoop, calls=%fused_computation.24 | loop fusion | flops 655104 | bytes 1051648 | tf_op jit(solution)/shard_map/reduce_sum | solution.py:261
  76.9 0.2 reshape.336
  77.2 14.2 %all_to_all.15 = f32[128,1,256]{2,1,0:T(1,128)S(1)} all-to-all(f32[128,1,256]{2,1,0:T(1,128)S(1)} %reshape.336), channel_id=1, replica_groups=mesh['mgrp'=8,'band'=16] {'mgrp','band'}, dimensions={0} | all-to-all | bytes 262144 | tf_op jit(solution)/shard_map/all_to_all | solution.py:23
  91.4 0.5 broadcast.224
  91.9 1.0 %reduce = f32[128,256]{1,0:T(8,128)S(1)} reduce(f32[128,1,256]{2,1,0:T(1,128)S(1)} %all_to_all.15, f32[]{:T(128)} %broadcast.224), dimensions={1}, to_apply=%all_to_all.11.reduce_sub_computation | reduce | bytes 262148 | tf_op jit(solution)/shard_map/all_to_all | solution.py:23
  92.8 0.2 reshape.337
  93.2 1.6 %multiply_add_fusion = (f32[2,64,1,512]{3,2,1,0:T(1,128)}, f32[2,64,1,512]{3,2,1,0:T(1,128)}, f32[2,64,1,512]{3,2,1,0:T(1,128)}) fusion(f32[2,64,1,512]{3,2,1,0:T(1,128)S(1)} %copy-done.1, f32[64]{0:T(128)S(1)} %get-tuple-element.10, f32[2,64,1,512]{3,2,1,0:T(1,128)S(1)} %copy-done.2, f32[2,64,1,512]{3,2,1,0:T(1,128)S(1)} %get-tuple-element.12, ...), kind=kLoop, calls=%fused_computation.17 | loop fusion | flops 393216 | bytes 1835520 | tf_op jit(solution)/shard_map/add | solution.py:273
  (30 shorter events, 0.8 us)
Async XLA Ops:
  4.8 25.3 %all-to-all-start = ((f32[128,8,128]{2,1,0:T(8,128)}), f32[128,8,128]{2,1,0:T(8,128)S(1)}, u32[]{:S(2)}, u32[]{:S(2)}) async-start(f32[128,8,128]{2,1,0:T(8,128)} %bitcast.85), calls=%async_computation | async-start | bytes 1048576 | tf_op jit(solution)/shard_map/all_to_all | solution.py:31
  24.7 2.3 %copy-start.4 = (bf16[8,64,64]{2,1,0:T(8,128)(2,1)S(1)}, bf16[8,64,64]{2,1,0:T(8,128)(2,1)}, u32[]{:S(2)}) copy-start(bf16[8,64,64]{2,1,0:T(8,128)(2,1)} %param.17) | copy-start | bytes 196612
  29.9 33.9 %copy-start.6 = (s32[1,16]{1,0:T(1,128)S(1)}, s32[1,16]{1,0:T(1,128)}, u32[]{:S(2)}) copy-start(s32[1,16]{1,0:T(1,128)} %cut_ref.1) | copy-start | bytes 196
  31.1 44.1 %copy-start = (bf16[1,1024,512]{2,1,0:T(8,128)(2,1)S(1)}, bf16[1,1024,512]{2,1,0:T(8,128)(2,1)}, u32[]{:S(2)}) copy-start(bf16[1,1024,512]{2,1,0:T(8,128)(2,1)} %param.15) | copy-start | bytes 3145732
  31.1 44.5 %copy-start.1 = (f32[2,64,1,512]{3,2,1,0:T(1,128)S(1)}, f32[2,64,1,512]{3,2,1,0:T(1,128)}, u32[]{:S(2)}) copy-start(f32[2,64,1,512]{3,2,1,0:T(1,128)} %param.14) | copy-start | bytes 786436
  31.1 44.5 %copy-start.2 = (f32[2,64,1,512]{3,2,1,0:T(1,128)S(1)}, f32[2,64,1,512]{3,2,1,0:T(1,128)}, u32[]{:S(2)}) copy-start(f32[2,64,1,512]{3,2,1,0:T(1,128)} %param.13) | copy-start | bytes 786436
  31.1 44.5 %copy-start.5 = (f32[512]{0:T(512)S(1)}, f32[512]{0:T(512)}, u32[]{:S(2)}) copy-start(f32[512]{0:T(512)} %param.16) | copy-start | bytes 6148
  51.0 42.2 %copy-start.3 = (f32[2,64,1,512]{3,2,1,0:T(1,128)S(1)}, f32[2,64,1,512]{3,2,1,0:T(1,128)}, u32[]{:S(2)}) copy-start(f32[2,64,1,512]{3,2,1,0:T(1,128)} %param.12) | copy-start | bytes 786436
  52.9 22.1 %all-to-all-start.1 = ((bf16[128,8,128]{2,1,0:T(8,128)(2,1)}), bf16[128,8,128]{2,1,0:T(8,128)(2,1)S(1)}, u32[]{:S(2)}, u32[]{:S(2)}) async-start(bf16[128,8,128]{2,1,0:T(8,128)(2,1)} %bitcast.22), calls=%async_computation.1 | async-start | bytes 524288 | tf_op jit(solution)/shard_map/all_to_all | solution.py:73

commit v12 on v9

--- a/solution.py
+++ b/solution.py
@@ -102,25 +102,36 @@
     return backward.reshape(cycle_count, mode_count, columns).astype(jnp.bfloat16)
 
 
-def noise_kernel(index_ref, length_ref, coeff_ref, table_ref, pair_ref, back_ref, noisy_ref):
+def noise_kernel(index_ref, length_ref, coeff_ref, table_ref, pair_ref, back_ref, noisy_ref, quad_ref):
     cycle = pl.program_id(0)
     wide = noisy_ref.shape[1]
     pair_width = 2 * BLK
     coeff = coeff_ref[0]
     side = int(round(pair_ref.shape[0] ** 0.5))
 
+    quad_width = 2 * pair_width
+    slots = quad_ref.shape[0]
+    zero = jnp.zeros((pair_width, pair_width), quad_ref.dtype)
+    for slot in range(slots):
+        quad_ref[slot, 0:pair_width, pair_width:quad_width] = zero
+        quad_ref[slot, pair_width:quad_width, 0:pair_width] = zero
+
     def chunk(start, span, total):
         table = table_ref[0, :, pl.ds(start, span)]
         sky = jnp.dot(coeff, table, preferred_element_type=jnp.float32).astype(jnp.bfloat16)
-        for inner in range(span // pair_width):
-            block = (start + inner * pair_width) // BLK
-            pick = index_ref[cycle, block] * side + index_ref[cycle, block + 1]
+        for inner in range(span // quad_width):
+            block = (start + inner * quad_width) // BLK
+            first = index_ref[cycle, block] * side + index_ref[cycle, block + 1]
+            second = index_ref[cycle, block + 2] * side + index_ref[cycle, block + 3]
+            slot = inner % slots
+            quad_ref[slot, 0:pair_width, 0:pair_width] = pair_ref[first]
+            quad_ref[slot, pair_width:quad_width, pair_width:quad_width] = pair_ref[second]
             noisy = jnp.dot(
-                sky[:, inner * pair_width:(inner + 1) * pair_width],
-                pair_ref[pick],
+                sky[:, inner * quad_width:(inner + 1) * quad_width],
+                quad_ref[slot],
                 preferred_element_type=jnp.float32,
             )
-            noisy_ref[:, inner * pair_width:(inner + 1) * pair_width] = noisy.astype(jnp.bfloat16)
+            noisy_ref[:, inner * quad_width:(inner + 1) * quad_width] = noisy.astype(jnp.bfloat16)
         return total + lax.dot_general(
             noisy_ref[:, :span], table, (((1,), (1,)), ((), ())), preferred_element_type=jnp.float32
         )
@@ -174,7 +185,10 @@
             pl.BlockSpec(pairs_t.shape, lambda r, idx, n: (0, 0, 0)),
         ],
         out_specs=pl.BlockSpec((1, map_count, 2 * mode_count), lambda r, idx, n: (r, 0, 0)),
-        scratch_shapes=[pltpu.VMEM((map_count, 8192), jnp.bfloat16)],
+        scratch_shapes=[
+            pltpu.VMEM((map_count, 8192), jnp.bfloat16),
+            pltpu.VMEM((4, 8 * BLK // 2, 8 * BLK // 2), jnp.bfloat16),
+        ],
     )
     back = pl.pallas_call(
         noise_kernel,

time: 90.5 us -> 93.6 us (1.034); the launches traced: 89.1 us -> 93.4 us
  blocking collectives: 31.5 us -> 33.7 us
  Pallas kernels: 20.4 us -> 22.4 us
    all_to_all x1, blocking collectives: 17.3 us -> 19.5 us  [spread_cycles(): received = lax.all_to_all(pieces, MESH_AXES, 0, 0, tiled=True)]
    pallas_call x1, Pallas kernels: 20.4 us -> 22.4 us  [cycle_transform(): pl.pallas_call(noise_kernel, grid_spec=grid_spec, out_shape=jax.ShapeDtyp...]
  transfers between devices with their start and end apart: 1 -> 1, of which waited for: 1 -> 1; matrix products, arithmetic and copies ran while one was open for 11% -> 10% of each run, Pallas kernels for 0% -> 0%
where the time goes in v12:
time: 93.6 us; the launch traced here: 93.4 us
  blocking collectives  33.7 us (36%)
  Pallas kernels  22.4 us (24%)
  other arithmetic  14.6 us (16%)
  starting transfers between devices  11.5 us (12%)
  local copies, waits for them, and re-layouts  5.33 us (6%)
  waiting for transfers between devices  4.1 us (4%)
    pallas_call x1, Pallas kernels, cycle_transform(): pl.pallas_call(noise_kernel, grid_spec=grid_spec, out_shape=jax.ShapeDtyp...  22.4 us
    all_to_all x1, blocking collectives, spread_cycles(): received = lax.all_to_all(pieces, MESH_AXES, 0, 0, tiled=True)  19.5 us
    all_to_all x1, blocking collectives, total_over_mesh(): return jnp.sum(lax.all_to_all(copies, MESH_AXES, 0, 0, tiled=True), axis=0)  14.2 us
    all_to_all x1, starting transfers between devices, gather_cycles(): received = lax.all_to_all(pieces, MESH_AXES, 0, 0, tiled=True)  11.5 us
    all_to_all x1, waiting for transfers between devices, gather_cycles(): received = lax.all_to_all(pieces, MESH_AXES, 0, 0, tiled=True)  4.1 us
    another operation x1, other arithmetic  2.81 us
    mul x1, other arithmetic, cycle_transform(): jnp.swapaxes(pair_table(noise_mats), 1, 2)  2.32 us
    convert_element_type x1, other arithmetic, cycle_tables(): return jnp.stack([cosine, sine_part], axis=1).astype(jnp.bfloat16)  2.29 us
  transfers between devices with their start and end apart: 1, of which 1 were waited for; matrix products, arithmetic and copies ran while one was open for 10% of the time, Pallas kernels for 0%

profile of v12, /device:TPU:1, one launch (start us, length us, event | category | flops | bytes accessed | tf_op | source)
XLA Modules:
  0.0 93.4 jit_solution(6198606011080318311)
XLA Ops:
  0.7 0.8 convert_bitcast_fusion.1
  1.6 1.1 %convert_element_type.61 = bf16[2,64,1,512]{3,2,1,0:T(2,128)(2,1)S(1)} convert(f32[2,64,1,512]{3,2,1,0:T(1,128)} %param.14) | non-fusion elementwise | flops 65536 | bytes 393216 | tf_op jit(solution)/shard_map/convert_element_type | solution.py:223
  2.7 0.5 fusion.9
  3.2 0.2 copy.72
  3.4 0.8 copy.73
  4.3 11.5 %all-to-all-start = ((f32[128,8,128]{2,1,0:T(8,128)}), f32[128,8,128]{2,1,0:T(8,128)S(1)}, u32[]{:S(2)}, u32[]{:S(2)}) async-start(f32[128,8,128]{2,1,0:T(8,128)} %bitcast.7), calls=%async_computation | async-start | bytes 1048576 | tf_op jit(solution)/shard_map/all_to_all | solution.py:32
  15.8 0.1 fusion.13
  16.0 1.0 %fusion.27 = (f32[8,8,128]{2,1,0:T(8,128)S(1)}, f32[8,8,128]{2,1,0:T(8,128)S(1)}, f32[8,8,128]{2,1,0:T(8,128)S(1)}, f32[8,8,128]{2,1,0:T(8,128)S(1)}) fusion(f32[8]{0:T(128)S(1)} %convert_element_type.68, pred[8]{0:T(512)(128)(4,1)S(1)} %compare_bitcast_fusion, s32[8]{0:T(128)S(1)} %fusion.31, s32[8,128]{1,0:T(8,128)S(1)} %get-tuple-element.26, ...), kind=kLoop, calls=%fused_computation.54 | loop fusion | flops 163840 | bytes 139336 | tf_op jit(solution)/shard_map/cos | solution.py:56
  17.0 0.2 copy.76
  17.2 0.2 copy.77
  17.4 2.8 %fusion.3 = (bf16[8,1,8,16384]{3,2,1,0:T(8,128)(2,1)S(1)}, bf16[8,1,8,16384]{3,2,1,0:T(8,128)(2,1)S(1)}) fusion(f32[8,16384]{1,0:T(8,128)S(1)} %fusion.13, f32[8,8,128]{2,1,0:T(8,128)S(1)} %get-tuple-element.20, f32[8,8,128]{1,2,0:T(8,128)S(1)} %copy.77, f32[8,8,128]{2,1,0:T(8,128)S(1)} %get-tuple-element.21, f32[8,8,128]{1,2,0:T(8,128)S(1)} %copy.76, ...), kind=kLoop, calls=%fused_computation.8 | loop fusion | flops 12582912 | bytes 4849728 | tf_op jit(solution)/shard_map/convert
  20.3 2.3 %maximum_bitcast_fusion.table_ref = bf16[8,16,16384]{2,1,0:T(8,128)(2,1)} fusion(bf16[8,1,8,16384]{3,2,1,0:T(8,128)(2,1)S(1)} %get-tuple-element.14, bf16[8,1,8,16384]{3,2,1,0:T(8,128)(2,1)S(1)} %get-tuple-element.13), kind=kLoop, calls=%fused_computation.2 | loop fusion | flops 2097152 | bytes 8388608 | tf_op jit(solution)/shard_map/convert_element_type | solution.py:69
  22.5 0.1 copy.78
  22.7 0.2 broadcast_in_dim.24
  22.9 0.2 broadcast_in_dim.25
  23.2 2.3 %fusion.7 = bf16[8,8,128,128]{2,3,1,0:T(8,128)(2,1)} fusion(bf16[8,8,64,64]{2,3,1,0:T(8,128)(2,1)S(1)} %broadcast_in_dim.25, bf16[8,8,64,64]{2,3,1,0:T(8,128)(2,1)S(1)} %broadcast_in_dim.24), kind=kLoop, calls=%fused_computation.12 | loop fusion | flops 10485760 | bytes 3145728 | tf_op jit(solution)/shard_map/mul | solution.py:178
  25.5 4.1 %all-to-all-done = f32[128,8,128]{2,1,0:T(8,128)S(1)} async-done(((f32[128,8,128]{2,1,0:T(8,128)}), f32[128,8,128]{2,1,0:T(8,128)S(1)}, u32[]{:S(2)}, u32[]{:S(2)}) %all-to-all-start) | async-done | bytes 524320 | tf_op jit(solution)/shard_map/all_to_all | solution.py:32
  29.8 0.8 copy.80.coeff_ref
  30.5 22.4 %shard_map.121 = bf16[8,64,16]{2,1,0:T(8,128)(2,1)} custom-call(s32[8,256]{1,0:T(8,128)} %index_ref.1, s32[8]{0:T(128)} %length_ref.1, bf16[8,64,16]{2,1,0:T(8,128)(2,1)} %copy.80.coeff_ref, bf16[8,16,16384]{2,1,0:T(8,128)(2,1)} %maximum_bitcast_fusion.table_ref, bf16[64,128,128]{2,1,0:T(8,128)(2,1)} %bitcast.99), custom_call_target="tpu_custom_call" | custom-call | tf_op jit(solution)/shard_map/pallas_call | solution.py:193
  52.9 1.0 %copy.81 = bf16[8,64,16]{1,2,0:T(8,128)(2,1)S(1)} copy(bf16[8,64,16]{2,1,0:T(8,128)(2,1)} %shard_map.121) | data formatting | bytes 32768 | tf_op jit(solution)/shard_map/pallas_call | solution.py:193
  54.0 0.1 reshape.354
  54.2 19.5 %all_to_all.15 = bf16[128,8,128]{2,1,0:T(8,128)(2,1)S(1)} all-to-all(bf16[128,8,128]{2,1,0:T(8,128)(2,1)S(1)} %bitcast.102), channel_id=1, replica_groups=mesh['mgrp'=8,'band'=16] {'mgrp','band'}, dimensions={0} | all-to-all | bytes 524288 | tf_op jit(solution)/shard_map/all_to_all | solution.py:42
  73.7 0.1 multiply_bitcast_fusion
  73.9 0.3 fusion.10
  74.3 1.3 %multiply_reduce_fusion.3 = (f32[64]{0:T(128)S(1)}, f32[64]{0:T(128)S(1)}, f32[64]{0:T(128)S(1)}, f32[64]{0:T(128)S(1)}, f32[2,64,1,512]{3,2,1,0:T(1,128)S(1)}) fusion(f32[2,64,1,512]{3,2,1,0:T(1,128)S(1)} %copy-done.2, f32[2,64,1,512]{3,2,1,0:T(1,128)S(1)} %copy-done.1, f32[2,64,1,512]{3,1,0,2:T(8,128)S(1)} %bitcast.104, f32[512]{0:T(512)S(1)} %copy-done.5), kind=kLoop, calls=%fused_computation.30 | loop fusion | flops 655104 | bytes 1051648 | tf_op jit(solution)/shard_map/reduce_sum | solution.py:247
  75.6 0.2 reshape.358
  75.9 14.2 %all_to_all.16 = f32[128,1,256]{2,1,0:T(1,128)S(1)} all-to-all(f32[128,1,256]{2,1,0:T(1,128)S(1)} %reshape.358), channel_id=1, replica_groups=mesh['mgrp'=8,'band'=16] {'mgrp','band'}, dimensions={0} | all-to-all | bytes 262144 | tf_op jit(solution)/shard_map/all_to_all | solution.py:23
  90.1 0.5 broadcast.229
  90.6 1.0 %reduce = f32[128,256]{1,0:T(8,128)S(1)} reduce(f32[128,1,256]{2,1,0:T(1,128)S(1)} %all_to_all.16, f32[]{:T(128)} %broadcast.229), dimensions={1}, to_apply=%all_to_all.11.reduce_sub_computation | reduce | bytes 262148 | tf_op jit(solution)/shard_map/all_to_all | solution.py:23
  91.5 0.2 reshape.359
  91.7 0.1 reduce_sum.59
  91.9 1.6 %multiply_add_fusion = (f32[2,64,1,512]{3,2,1,0:T(1,128)}, f32[2,64,1,512]{3,2,1,0:T(1,128)}, f32[2,64,1,512]{3,2,1,0:T(1,128)}) fusion(f32[2,64,1,512]{3,2,1,0:T(1,128)S(1)} %copy-done.1, f32[64]{0:T(128)S(1)} %get-tuple-element.10, f32[2,64,1,512]{3,2,1,0:T(1,128)S(1)} %copy-done.2, f32[2,64,1,512]{3,2,1,0:T(1,128)S(1)} %get-tuple-element.12, ...), kind=kLoop, calls=%fused_computation.23 | loop fusion | flops 393216 | bytes 1835520 | tf_op jit(solution)/shard_map/add | solution.py:259
  (36 shorter events, 0.6 us)
Async XLA Ops:
  0.6 2.1 %copy-start = (bf16[1,1024,512]{2,1,0:T(8,128)(2,1)S(1)}, bf16[1,1024,512]{2,1,0:T(8,128)(2,1)}, u32[]{:S(2)}) copy-start(bf16[1,1024,512]{2,1,0:T(8,128)(2,1)} %param.15) | copy-start | bytes 3145732
  0.6 15.1 %copy-start.6 = (s32[8]{0:T(128)S(1)}, s32[8]{0:T(128)}, u32[]{:S(2)}) copy-start(s32[8]{0:T(128)} %length_ref.1) | copy-start | bytes 100
  0.7 15.3 %copy-start.7 = (s32[8]{0:T(128)S(1)}, s32[8]{0:T(128)}, u32[]{:S(2)}) copy-start(s32[8]{0:T(128)} %param.20) | copy-start | bytes 100
  4.3 25.3 %all-to-all-start = ((f32[128,8,128]{2,1,0:T(8,128)}), f32[128,8,128]{2,1,0:T(8,128)S(1)}, u32[]{:S(2)}, u32[]{:S(2)}) async-start(f32[128,8,128]{2,1,0:T(8,128)} %bitcast.7), calls=%async_computation | async-start | bytes 1048576 | tf_op jit(solution)/shard_map/all_to_all | solution.py:32
  20.2 2.3 %copy-start.4 = (bf16[8,64,64]{2,1,0:T(8,128)(2,1)S(1)}, bf16[8,64,64]{2,1,0:T(8,128)(2,1)}, u32[]{:S(2)}) copy-start(bf16[8,64,64]{2,1,0:T(8,128)(2,1)} %param.17) | copy-start | bytes 196612
  30.5 43.7 %copy-start.1 = (f32[2,64,1,512]{3,2,1,0:T(1,128)S(1)}, f32[2,64,1,512]{3,2,1,0:T(1,128)}, u32[]{:S(2)}) copy-start(f32[2,64,1,512]{3,2,1,0:T(1,128)} %param.14) | copy-start | bytes 786436
  30.5 43.7 %copy-start.2 = (f32[2,64,1,512]{3,2,1,0:T(1,128)S(1)}, f32[2,64,1,512]{3,2,1,0:T(1,128)}, u32[]{:S(2)}) copy-start(f32[2,64,1,512]{3,2,1,0:T(1,128)} %param.13) | copy-start | bytes 786436
  30.5 43.7 %copy-start.5 = (f32[512]{0:T(512)S(1)}, f32[512]{0:T(512)}, u32[]{:S(2)}) copy-start(f32[512]{0:T(512)} %param.16) | copy-start | bytes 6148
  52.9 38.9 %copy-start.3 = (f32[2,64,1,512]{3,2,1,0:T(1,128)S(1)}, f32[2,64,1,512]{3,2,1,0:T(1,128)}, u32[]{:S(2)}) copy-start(f32[2,64,1,512]{3,2,1,0:T(1,128)} %param.12) | copy-start | bytes 786436

commit v13 on v9

--- a/solution.py
+++ b/solution.py
@@ -35,9 +35,9 @@
 
 
 def spread_cycles(backward, band_count):
-    own, group_count, columns = backward.shape
+    group_count, own, columns = backward.shape
     pieces = jnp.broadcast_to(
-        backward.transpose(1, 0, 2)[:, None], (group_count, band_count, own, columns)
+        backward[:, None], (group_count, band_count, own, columns)
     ).reshape(group_count * band_count, own, columns)
     received = lax.all_to_all(pieces, MESH_AXES, 0, 0, tiled=True)
     received = received.reshape(group_count, band_count, own, columns).transpose(1, 0, 2, 3)
@@ -122,7 +122,7 @@
             )
             noisy_ref[:, inner * pair_width:(inner + 1) * pair_width] = noisy.astype(jnp.bfloat16)
         return total + lax.dot_general(
-            noisy_ref[:, :span], table, (((1,), (1,)), ((), ())), preferred_element_type=jnp.float32
+            table, noisy_ref[:, :span], (((1,), (1,)), ((), ())), preferred_element_type=jnp.float32
         )
 
     length = length_ref[cycle]
@@ -137,7 +137,7 @@
         0,
         wide_count,
         lambda step, acc: chunk(pl.multiple_of(step * wide, wide), wide, acc),
-        jnp.zeros(back_ref.shape[1:], jnp.float32),
+        jnp.zeros((table_ref.shape[1], noisy_ref.shape[0]), jnp.float32),
     )
     total = lax.fori_loop(
         0,
@@ -151,7 +151,12 @@
         lambda step, acc: chunk(pl.multiple_of(full * wide + mid_count * mid, mid), narrow, acc),
         total,
     )
-    back_ref[0] = total.astype(back_ref.dtype)
+    modes = back_ref.shape[0]
+    maps = noisy_ref.shape[0]
+    for part in range(table_ref.shape[1] // modes):
+        for mode in range(modes):
+            row = part * modes + mode
+            back_ref[mode, pl.ds(cycle, 1), part * maps:(part + 1) * maps] = total[row:row + 1, :]
 
 
 def cycle_transform(coeffs, lengths, indices, m_values, noise_mats, weight):
@@ -173,19 +178,15 @@
             pl.BlockSpec((1, 2 * mode_count, RLEN), lambda r, idx, n: (r, 0, 0)),
             pl.BlockSpec(pairs_t.shape, lambda r, idx, n: (0, 0, 0)),
         ],
-        out_specs=pl.BlockSpec((1, map_count, 2 * mode_count), lambda r, idx, n: (r, 0, 0)),
+        out_specs=pl.BlockSpec((mode_count, cycle_count, columns), lambda r, idx, n: (0, 0, 0)),
         scratch_shapes=[pltpu.VMEM((map_count, 8192), jnp.bfloat16)],
     )
     back = pl.pallas_call(
         noise_kernel,
         grid_spec=grid_spec,
-        out_shape=jax.ShapeDtypeStruct((cycle_count, map_count, 2 * mode_count), jnp.bfloat16),
+        out_shape=jax.ShapeDtypeStruct((mode_count, cycle_count, columns), jnp.float32),
     )(indices, lengths, coeff_t, tables, pairs_t)
-    return (
-        back.reshape(cycle_count, map_count, 2, mode_count)
-        .transpose(0, 3, 2, 1)
-        .reshape(cycle_count, mode_count, columns)
-    )
+    return back.astype(jnp.bfloat16)
 
 
 def shards(
@@ -219,8 +220,7 @@
     cycle_local = coeffs.shape[0]
     mode_total = coeffs.shape[1]
     outputs = cycle_transform(coeffs, cycle_lengths, noise_index, m_values, noise_mats, weight)
-    backward = outputs.reshape(cycle_local, mode_total, columns)
-    returned = spread_cycles(backward, band_count)
+    returned = spread_cycles(outputs, band_count)
     masked = returned * row_mask(jnp.int32(0), cycle_total).astype(jnp.bfloat16)
     image_data = lax.optimization_barrier(
         jnp.einsum("rl,rn->nl", legendre[0], masked, preferred_element_type=jnp.float32)

time: 90.5 us -> 89.6 us (0.990); the launches traced: 89.1 us -> 90.4 us
  blocking collectives: 31.5 us -> 32.9 us
  local copies, waits for them, and re-layouts: 5.33 us -> 4.17 us
    all_to_all x1, blocking collectives: 17.3 us -> 18.7 us  [spread_cycles(): received = lax.all_to_all(pieces, MESH_AXES, 0, 0, tiled=True)]
    pallas_call x1 -> x0, local copies, waits for them, and re-layouts: 1.04 us -> none  [cycle_transform(): pl.pallas_call(noise_kernel, grid_spec=grid_spec, out_shape=jax.ShapeDtyp...]
where the time goes in v13:
time: 89.6 us; the launch traced here: 90.4 us
  blocking collectives  32.9 us (37%)
  Pallas kernels  20.6 us (23%)
  other arithmetic  15.4 us (17%)
  starting transfers between devices  11.5 us (13%)
  local copies, waits for them, and re-layouts  4.17 us (5%)
  waiting for transfers between devices  4.1 us (5%)
  between operations  0.91 us (1%)
    pallas_call x1, Pallas kernels, cycle_transform(): pl.pallas_call(noise_kernel, grid_spec=grid_spec, out_shape=jax.ShapeDtyp...  20.6 us
    all_to_all x1, blocking collectives, spread_cycles(): received = lax.all_to_all(pieces, MESH_AXES, 0, 0, tiled=True)  18.7 us
    all_to_all x1, blocking collectives, total_over_mesh(): return jnp.sum(lax.all_to_all(copies, MESH_AXES, 0, 0, tiled=True), axis=0)  14.2 us
    all_to_all x1, starting transfers between devices, gather_cycles(): received = lax.all_to_all(pieces, MESH_AXES, 0, 0, tiled=True)  11.5 us
    all_to_all x1, waiting for transfers between devices, gather_cycles(): received = lax.all_to_all(pieces, MESH_AXES, 0, 0, tiled=True)  4.1 us
    another operation x1, other arithmetic  2.81 us
    mul x1, other arithmetic, cycle_transform(): jnp.swapaxes(pair_table(noise_mats), 1, 2)  2.32 us
    convert_element_type x1, other arithmetic, cycle_tables(): return jnp.stack([cosine, sine_part], axis=1).astype(jnp.bfloat16)  2.29 us
  transfers between devices with their start and end apart: 1, of which 1 were waited for; matrix products, arithmetic and copies ran while one was open for 11% of the time, Pallas kernels for 0%

profile of v13, /device:TPU:1, one launch (start us, length us, event | category | flops | bytes accessed | tf_op | source)
XLA Modules:
  0.0 90.4 jit_solution(6507530745027736833)
XLA Ops:
  0.7 0.8 convert_bitcast_fusion.1
  1.6 1.1 %convert_element_type.64 = bf16[2,64,1,512]{3,2,1,0:T(2,128)(2,1)S(1)} convert(f32[2,64,1,512]{3,2,1,0:T(1,128)} %param.14) | non-fusion elementwise | flops 65536 | bytes 393216 | tf_op jit(solution)/shard_map/convert_element_type | solution.py:210
  2.7 0.5 fusion.9
  3.2 0.2 copy.59
  3.4 0.8 copy.60
  4.3 11.5 %all-to-all-start = ((f32[128,8,128]{2,1,0:T(8,128)}), f32[128,8,128]{2,1,0:T(8,128)S(1)}, u32[]{:S(2)}, u32[]{:S(2)}) async-start(f32[128,8,128]{2,1,0:T(8,128)} %bitcast.7), calls=%async_computation | async-start | bytes 1048576 | tf_op jit(solution)/shard_map/all_to_all | solution.py:32
  15.8 0.1 fusion.13
  16.0 1.0 %fusion.27 = (f32[8,8,128]{2,1,0:T(8,128)S(1)}, f32[8,8,128]{2,1,0:T(8,128)S(1)}, f32[8,8,128]{2,1,0:T(8,128)S(1)}, f32[8,8,128]{2,1,0:T(8,128)S(1)}) fusion(f32[8]{0:T(128)S(1)} %convert_element_type.71, pred[8]{0:T(512)(128)(4,1)S(1)} %compare_bitcast_fusion, s32[8]{0:T(128)S(1)} %fusion.31, s32[8,128]{1,0:T(8,128)S(1)} %get-tuple-element.26, ...), kind=kLoop, calls=%fused_computation.54 | loop fusion | flops 163840 | bytes 139336 | tf_op jit(solution)/shard_map/cos | solution.py:56
  17.0 0.2 copy.63
  17.2 0.2 copy.64
  17.4 2.8 %fusion.3 = (bf16[8,1,8,16384]{3,2,1,0:T(8,128)(2,1)S(1)}, bf16[8,1,8,16384]{3,2,1,0:T(8,128)(2,1)S(1)}) fusion(f32[8,16384]{1,0:T(8,128)S(1)} %fusion.13, f32[8,8,128]{2,1,0:T(8,128)S(1)} %get-tuple-element.20, f32[8,8,128]{1,2,0:T(8,128)S(1)} %copy.64, f32[8,8,128]{2,1,0:T(8,128)S(1)} %get-tuple-element.21, f32[8,8,128]{1,2,0:T(8,128)S(1)} %copy.63, ...), kind=kLoop, calls=%fused_computation.8 | loop fusion | flops 12582912 | bytes 4849728 | tf_op jit(solution)/shard_map/convert
  20.3 2.3 %maximum_bitcast_fusion.table_ref = bf16[8,16,16384]{2,1,0:T(8,128)(2,1)} fusion(bf16[8,1,8,16384]{3,2,1,0:T(8,128)(2,1)S(1)} %get-tuple-element.14, bf16[8,1,8,16384]{3,2,1,0:T(8,128)(2,1)S(1)} %get-tuple-element.13), kind=kLoop, calls=%fused_computation.2 | loop fusion | flops 2097152 | bytes 8388608 | tf_op jit(solution)/shard_map/convert_element_type | solution.py:69
  22.5 0.1 copy.65
  22.7 0.2 broadcast_in_dim.24
  22.9 0.2 broadcast_in_dim.25
  23.2 2.3 %fusion.7 = bf16[8,8,128,128]{2,3,1,0:T(8,128)(2,1)} fusion(bf16[8,8,64,64]{2,3,1,0:T(8,128)(2,1)S(1)} %broadcast_in_dim.25, bf16[8,8,64,64]{2,3,1,0:T(8,128)(2,1)S(1)} %broadcast_in_dim.24), kind=kLoop, calls=%fused_computation.12 | loop fusion | flops 10485760 | bytes 3145728 | tf_op jit(solution)/shard_map/mul | solution.py:172
  25.5 4.1 %all-to-all-done = f32[128,8,128]{2,1,0:T(8,128)S(1)} async-done(((f32[128,8,128]{2,1,0:T(8,128)}), f32[128,8,128]{2,1,0:T(8,128)S(1)}, u32[]{:S(2)}, u32[]{:S(2)}) %all-to-all-start) | async-done | bytes 524320 | tf_op jit(solution)/shard_map/all_to_all | solution.py:32
  29.7 0.1 reshape.345
  29.8 0.8 copy.67.coeff_ref
  30.5 20.6 %shard_map.121 = f32[8,8,128]{2,1,0:T(8,128)} custom-call(s32[8,256]{1,0:T(8,128)} %index_ref.1, s32[8]{0:T(128)} %length_ref.1, bf16[8,64,16]{2,1,0:T(8,128)(2,1)} %copy.67.coeff_ref, bf16[8,16,16384]{2,1,0:T(8,128)(2,1)} %maximum_bitcast_fusion.table_ref, bf16[64,128,128]{2,1,0:T(8,128)(2,1)} %bitcast.95), custom_call_target="tpu_custom_call" | custom-call | tf_op jit(solution)/shard_map/pallas_call | solution.py:184
  51.1 0.8 convert_element_type.75
  52.0 18.7 %all_to_all.15 = bf16[128,8,128]{2,1,0:T(8,128)(2,1)S(1)} all-to-all(bf16[128,8,128]{2,1,0:T(8,128)(2,1)S(1)} %bitcast.98), channel_id=1, replica_groups=mesh['mgrp'=8,'band'=16] {'mgrp','band'}, dimensions={0} | all-to-all | bytes 524288 | tf_op jit(solution)/shard_map/all_to_all | solution.py:42
  70.7 0.1 multiply_bitcast_fusion
  70.8 0.3 fusion.10
  71.2 1.3 %multiply_reduce_fusion.3 = (f32[64]{0:T(128)S(1)}, f32[64]{0:T(128)S(1)}, f32[64]{0:T(128)S(1)}, f32[64]{0:T(128)S(1)}, f32[2,64,1,512]{3,2,1,0:T(1,128)S(1)}) fusion(f32[2,64,1,512]{3,2,1,0:T(1,128)S(1)} %copy-done.2, f32[2,64,1,512]{3,2,1,0:T(1,128)S(1)} %copy-done.1, f32[2,64,1,512]{3,1,0,2:T(8,128)S(1)} %bitcast.100, f32[512]{0:T(512)S(1)} %copy-done.5), kind=kLoop, calls=%fused_computation.30 | loop fusion | flops 655104 | bytes 1051648 | tf_op jit(solution)/shard_map/reduce_sum | solution.py:233
  72.6 0.2 reshape.350
  72.8 14.2 %all_to_all.16 = f32[128,1,256]{2,1,0:T(1,128)S(1)} all-to-all(f32[128,1,256]{2,1,0:T(1,128)S(1)} %reshape.350), channel_id=1, replica_groups=mesh['mgrp'=8,'band'=16] {'mgrp','band'}, dimensions={0} | all-to-all | bytes 262144 | tf_op jit(solution)/shard_map/all_to_all | solution.py:23
  87.0 0.5 broadcast.229
  87.5 1.0 %reduce = f32[128,256]{1,0:T(8,128)S(1)} reduce(f32[128,1,256]{2,1,0:T(1,128)S(1)} %all_to_all.16, f32[]{:T(128)} %broadcast.229), dimensions={1}, to_apply=%all_to_all.11.reduce_sub_computation | reduce | bytes 262148 | tf_op jit(solution)/shard_map/all_to_all | solution.py:23
  88.5 0.2 reshape.351
  88.7 0.1 reduce_sum.59
  88.8 1.6 %multiply_add_fusion = (f32[2,64,1,512]{3,2,1,0:T(1,128)}, f32[2,64,1,512]{3,2,1,0:T(1,128)}, f32[2,64,1,512]{3,2,1,0:T(1,128)}) fusion(f32[2,64,1,512]{3,2,1,0:T(1,128)S(1)} %copy-done.1, f32[64]{0:T(128)S(1)} %get-tuple-element.10, f32[2,64,1,512]{3,2,1,0:T(1,128)S(1)} %copy-done.2, f32[2,64,1,512]{3,2,1,0:T(1,128)S(1)} %get-tuple-element.12, ...), kind=kLoop, calls=%fused_computation.23 | loop fusion | flops 393216 | bytes 1835520 | tf_op jit(solution)/shard_map/add | solution.py:245
  (33 shorter events, 0.5 us)
Async XLA Ops:
  0.6 2.1 %copy-start = (bf16[1,1024,512]{2,1,0:T(8,128)(2,1)S(1)}, bf16[1,1024,512]{2,1,0:T(8,128)(2,1)}, u32[]{:S(2)}) copy-start(bf16[1,1024,512]{2,1,0:T(8,128)(2,1)} %param.15) | copy-start | bytes 3145732
  0.6 15.1 %copy-start.6 = (s32[8]{0:T(128)S(1)}, s32[8]{0:T(128)}, u32[]{:S(2)}) copy-start(s32[8]{0:T(128)} %length_ref.1) | copy-start | bytes 100
  0.7 15.3 %copy-start.7 = (s32[8]{0:T(128)S(1)}, s32[8]{0:T(128)}, u32[]{:S(2)}) copy-start(s32[8]{0:T(128)} %param.20) | copy-start | bytes 100
  4.3 25.3 %all-to-all-start = ((f32[128,8,128]{2,1,0:T(8,128)}), f32[128,8,128]{2,1,0:T(8,128)S(1)}, u32[]{:S(2)}, u32[]{:S(2)}) async-start(f32[128,8,128]{2,1,0:T(8,128)} %bitcast.7), calls=%async_computation | async-start | bytes 1048576 | tf_op jit(solution)/shard_map/all_to_all | solution.py:32
  20.2 2.3 %copy-start.4 = (bf16[8,64,64]{2,1,0:T(8,128)(2,1)S(1)}, bf16[8,64,64]{2,1,0:T(8,128)(2,1)}, u32[]{:S(2)}) copy-start(bf16[8,64,64]{2,1,0:T(8,128)(2,1)} %param.17) | copy-start | bytes 196612
  30.5 40.7 %copy-start.1 = (f32[2,64,1,512]{3,2,1,0:T(1,128)S(1)}, f32[2,64,1,512]{3,2,1,0:T(1,128)}, u32[]{:S(2)}) copy-start(f32[2,64,1,512]{3,2,1,0:T(1,128)} %param.14) | copy-start | bytes 786436
  30.5 40.7 %copy-start.2 = (f32[2,64,1,512]{3,2,1,0:T(1,128)S(1)}, f32[2,64,1,512]{3,2,1,0:T(1,128)}, u32[]{:S(2)}) copy-start(f32[2,64,1,512]{3,2,1,0:T(1,128)} %param.13) | copy-start | bytes 786436
  30.5 40.7 %copy-start.5 = (f32[512]{0:T(512)S(1)}, f32[512]{0:T(512)}, u32[]{:S(2)}) copy-start(f32[512]{0:T(512)} %param.16) | copy-start | bytes 6148
  51.1 37.7 %copy-start.3 = (f32[2,64,1,512]{3,2,1,0:T(1,128)S(1)}, f32[2,64,1,512]{3,2,1,0:T(1,128)}, u32[]{:S(2)}) copy-start(f32[2,64,1,512]{3,2,1,0:T(1,128)} %param.12) | copy-start | bytes 786436

commit v14 on v13

--- a/solution.py
+++ b/solution.py
@@ -207,14 +207,19 @@
     columns = 2 * map_count
     band_rows = cycle_total // band_count
     weight = L / (cycle_total * RLEN)
-    rounded = direction.astype(jnp.bfloat16).reshape(columns, mode_local, l_local)
 
     def row_mask(first_row, row_count):
         block_flags = lax.dynamic_slice_in_dim(cut_pattern, first_row // RB, row_count // RB, 1)
         return jnp.repeat(block_flags, RB, axis=1).T
 
     section = legendre
-    products = jnp.einsum("mrl,nml->rmn", section, rounded, preferred_element_type=jnp.float32)
+    products = jnp.einsum(
+        "mrl,nml->rmn",
+        section,
+        direction.reshape(columns, mode_local, l_local),
+        precision=lax.Precision.DEFAULT,
+        preferred_element_type=jnp.float32,
+    )
     masked_products = products * row_mask(jnp.int32(0), cycle_total).astype(jnp.float32)[:, :, None]
     coeffs = gather_cycles(masked_products.reshape(cycle_total, columns), band_count).astype(jnp.bfloat16)
     cycle_local = coeffs.shape[0]

time: 89.6 us -> 89.3 us (level); the launches traced: 90.4 us -> 88.8 us
  blocking collectives: 32.9 us -> 30 us
  Pallas kernels: 20.6 us -> 22.1 us
  other arithmetic: 15.4 us -> 14.3 us
  local copies, waits for them, and re-layouts: 4.17 us -> 5.12 us
    all_to_all x1, blocking collectives: 18.7 us -> 15.8 us  [spread_cycles(): received = lax.all_to_all(pieces, MESH_AXES, 0, 0, tiled=True)]
    pallas_call x1, Pallas kernels: 20.6 us -> 22.1 us  [cycle_transform(): pl.pallas_call(noise_kernel, grid_spec=grid_spec, out_shape=jax.ShapeDtyp...]
    convert_element_type x1 -> x0, other arithmetic: 1.13 us -> none  [shards(): direction.astype(jnp.bfloat16).reshape(columns, mode_local, l_local)]
    unnamed x20, local copies, waits for them, and re-layouts: 0.59 us -> 1.54 us
where the time goes in v14:
time: 89.3 us; the launch traced here: 88.8 us
  blocking collectives  30 us (34%)
  Pallas kernels  22.1 us (25%)
  other arithmetic  14.3 us (16%)
  starting transfers between devices  11.5 us (13%)
  local copies, waits for them, and re-layouts  5.12 us (6%)
  waiting for transfers between devices  4.1 us (5%)
  between operations  0.9 us (1%)
    pallas_call x1, Pallas kernels, cycle_transform(): pl.pallas_call(noise_kernel, grid_spec=grid_spec, out_shape=jax.ShapeDtyp...  22.1 us
    all_to_all x1, blocking collectives, spread_cycles(): received = lax.all_to_all(pieces, MESH_AXES, 0, 0, tiled=True)  15.8 us
    all_to_all x1, blocking collectives, total_over_mesh(): return jnp.sum(lax.all_to_all(copies, MESH_AXES, 0, 0, tiled=True), axis=0)  14.2 us
    all_to_all x1, starting transfers between devices, gather_cycles(): received = lax.all_to_all(pieces, MESH_AXES, 0, 0, tiled=True)  11.5 us
    all_to_all x1, waiting for transfers between devices, gather_cycles(): received = lax.all_to_all(pieces, MESH_AXES, 0, 0, tiled=True)  4.1 us
    another operation x1, other arithmetic  2.81 us
    mul x1, other arithmetic, cycle_transform(): jnp.swapaxes(pair_table(noise_mats), 1, 2)  2.32 us
    convert_element_type x1, other arithmetic, cycle_tables(): return jnp.stack([cosine, sine_part], axis=1).astype(jnp.bfloat16)  2.29 us
  transfers between devices with their start and end apart: 1, of which 1 were waited for; matrix products, arithmetic and copies ran while one was open for 11% of the time, Pallas kernels for 0%

profile of v14, /device:TPU:1, one launch (start us, length us, event | category | flops | bytes accessed | tf_op | source)
XLA Modules:
  0.0 88.8 jit_solution(15786390610110531686)
XLA Ops:
  0.7 0.8 convert_bitcast_fusion.1
  1.6 1.0 %copy.71 = bf16[2,64,1,512]{3,1,2,0:T(8,128)(2,1)S(1)} copy(f32[2,64,1,512]{3,2,1,0:T(1,128)} %param.14) | data formatting | bytes 393216
  2.6 0.5 fusion.9
  3.0 0.2 copy.59
  3.2 0.8 copy.60
  4.1 11.5 %all-to-all-start = ((f32[128,8,128]{2,1,0:T(8,128)}), f32[128,8,128]{2,1,0:T(8,128)S(1)}, u32[]{:S(2)}, u32[]{:S(2)}) async-start(f32[128,8,128]{2,1,0:T(8,128)} %bitcast.7), calls=%async_computation | async-start | bytes 1048576 | tf_op jit(solution)/shard_map/all_to_all | solution.py:32
  15.6 0.1 fusion.13
  15.8 1.0 %fusion.27 = (f32[8,8,128]{2,1,0:T(8,128)S(1)}, f32[8,8,128]{2,1,0:T(8,128)S(1)}, f32[8,8,128]{2,1,0:T(8,128)S(1)}, f32[8,8,128]{2,1,0:T(8,128)S(1)}) fusion(f32[8]{0:T(128)S(1)} %convert_element_type.67, pred[8]{0:T(512)(128)(4,1)S(1)} %compare_bitcast_fusion, s32[8]{0:T(128)S(1)} %fusion.31, s32[8,128]{1,0:T(8,128)S(1)} %get-tuple-element.26, ...), kind=kLoop, calls=%fused_computation.54 | loop fusion | flops 163840 | bytes 139336 | tf_op jit(solution)/shard_map/cos | solution.py:56
  16.8 0.2 copy.63
  17.0 0.2 copy.64
  17.2 2.8 %fusion.3 = (bf16[8,1,8,16384]{3,2,1,0:T(8,128)(2,1)S(1)}, bf16[8,1,8,16384]{3,2,1,0:T(8,128)(2,1)S(1)}) fusion(f32[8,16384]{1,0:T(8,128)S(1)} %fusion.13, f32[8,8,128]{2,1,0:T(8,128)S(1)} %get-tuple-element.20, f32[8,8,128]{1,2,0:T(8,128)S(1)} %copy.64, f32[8,8,128]{2,1,0:T(8,128)S(1)} %get-tuple-element.21, f32[8,8,128]{1,2,0:T(8,128)S(1)} %copy.63, ...), kind=kLoop, calls=%fused_computation.8 | loop fusion | flops 12582912 | bytes 4849728 | tf_op jit(solution)/shard_map/convert
  20.1 2.3 %maximum_bitcast_fusion.table_ref = bf16[8,16,16384]{2,1,0:T(8,128)(2,1)} fusion(bf16[8,1,8,16384]{3,2,1,0:T(8,128)(2,1)S(1)} %get-tuple-element.14, bf16[8,1,8,16384]{3,2,1,0:T(8,128)(2,1)S(1)} %get-tuple-element.13), kind=kLoop, calls=%fused_computation.2 | loop fusion | flops 2097152 | bytes 8388608 | tf_op jit(solution)/shard_map/convert_element_type | solution.py:69
  22.4 0.1 copy.65
  22.5 0.2 broadcast_in_dim.24
  22.7 0.2 broadcast_in_dim.25
  23.0 2.3 %fusion.7 = bf16[8,8,128,128]{2,3,1,0:T(8,128)(2,1)} fusion(bf16[8,8,64,64]{2,3,1,0:T(8,128)(2,1)S(1)} %broadcast_in_dim.25, bf16[8,8,64,64]{2,3,1,0:T(8,128)(2,1)S(1)} %broadcast_in_dim.24), kind=kLoop, calls=%fused_computation.12 | loop fusion | flops 10485760 | bytes 3145728 | tf_op jit(solution)/shard_map/mul | solution.py:172
  25.3 4.1 %all-to-all-done = f32[128,8,128]{2,1,0:T(8,128)S(1)} async-done(((f32[128,8,128]{2,1,0:T(8,128)}), f32[128,8,128]{2,1,0:T(8,128)S(1)}, u32[]{:S(2)}, u32[]{:S(2)}) %all-to-all-start) | async-done | bytes 524320 | tf_op jit(solution)/shard_map/all_to_all | solution.py:32
  29.5 0.1 reshape.345
  29.6 0.8 copy.67.coeff_ref
  30.3 22.1 %shard_map.121 = f32[8,8,128]{2,1,0:T(8,128)} custom-call(s32[8,256]{1,0:T(8,128)} %index_ref.1, s32[8]{0:T(128)} %length_ref.1, bf16[8,64,16]{2,1,0:T(8,128)(2,1)} %copy.67.coeff_ref, bf16[8,16,16384]{2,1,0:T(8,128)(2,1)} %maximum_bitcast_fusion.table_ref, bf16[64,128,128]{2,1,0:T(8,128)(2,1)} %bitcast.95), custom_call_target="tpu_custom_call" | custom-call | tf_op jit(solution)/shard_map/pallas_call | solution.py:184
  52.5 0.8 convert_element_type.71
  53.3 15.8 %all_to_all.15 = bf16[128,8,128]{2,1,0:T(8,128)(2,1)S(1)} all-to-all(bf16[128,8,128]{2,1,0:T(8,128)(2,1)S(1)} %bitcast.98), channel_id=1, replica_groups=mesh['mgrp'=8,'band'=16] {'mgrp','band'}, dimensions={0} | all-to-all | bytes 524288 | tf_op jit(solution)/shard_map/all_to_all | solution.py:42
  69.1 0.1 multiply_bitcast_fusion
  69.3 0.3 fusion.10
  69.6 1.3 %multiply_reduce_fusion.3 = (f32[64]{0:T(128)S(1)}, f32[64]{0:T(128)S(1)}, f32[64]{0:T(128)S(1)}, f32[64]{0:T(128)S(1)}, f32[2,64,1,512]{3,2,1,0:T(1,128)S(1)}) fusion(f32[2,64,1,512]{3,2,1,0:T(1,128)S(1)} %copy-done.2, f32[2,64,1,512]{3,2,1,0:T(1,128)S(1)} %copy-done.1, f32[2,64,1,512]{3,1,0,2:T(8,128)S(1)} %bitcast.100, f32[512]{0:T(512)S(1)} %copy-done.5), kind=kLoop, calls=%fused_computation.30 | loop fusion | flops 655104 | bytes 1051648 | tf_op jit(solution)/shard_map/reduce_sum | solution.py:238
  71.0 0.2 reshape.350
  71.2 14.2 %all_to_all.16 = f32[128,1,256]{2,1,0:T(1,128)S(1)} all-to-all(f32[128,1,256]{2,1,0:T(1,128)S(1)} %reshape.350), channel_id=1, replica_groups=mesh['mgrp'=8,'band'=16] {'mgrp','band'}, dimensions={0} | all-to-all | bytes 262144 | tf_op jit(solution)/shard_map/all_to_all | solution.py:23
  85.5 0.5 broadcast.229
  86.0 1.0 %reduce = f32[128,256]{1,0:T(8,128)S(1)} reduce(f32[128,1,256]{2,1,0:T(1,128)S(1)} %all_to_all.16, f32[]{:T(128)} %broadcast.229), dimensions={1}, to_apply=%all_to_all.11.reduce_sub_computation | reduce | bytes 262148 | tf_op jit(solution)/shard_map/all_to_all | solution.py:23
  86.9 0.2 reshape.351
  87.1 0.1 reduce_sum.59
  87.2 1.6 %multiply_add_fusion = (f32[2,64,1,512]{3,2,1,0:T(1,128)}, f32[2,64,1,512]{3,2,1,0:T(1,128)}, f32[2,64,1,512]{3,2,1,0:T(1,128)}) fusion(f32[2,64,1,512]{3,2,1,0:T(1,128)S(1)} %copy-done.1, f32[64]{0:T(128)S(1)} %get-tuple-element.10, f32[2,64,1,512]{3,2,1,0:T(1,128)S(1)} %copy-done.2, f32[2,64,1,512]{3,2,1,0:T(1,128)S(1)} %get-tuple-element.12, ...), kind=kLoop, calls=%fused_computation.23 | loop fusion | flops 393216 | bytes 1835520 | tf_op jit(solution)/shard_map/add | solution.py:250
  (32 shorter events, 0.5 us)
Async XLA Ops:
  0.6 1.9 %copy-start = (bf16[1,1024,512]{2,1,0:T(8,128)(2,1)S(1)}, bf16[1,1024,512]{2,1,0:T(8,128)(2,1)}, u32[]{:S(2)}) copy-start(bf16[1,1024,512]{2,1,0:T(8,128)(2,1)} %param.15) | copy-start | bytes 3145732
  0.6 14.9 %copy-start.6 = (s32[8]{0:T(128)S(1)}, s32[8]{0:T(128)}, u32[]{:S(2)}) copy-start(s32[8]{0:T(128)} %length_ref.1) | copy-start | bytes 100
  0.7 15.1 %copy-start.7 = (s32[8]{0:T(128)S(1)}, s32[8]{0:T(128)}, u32[]{:S(2)}) copy-start(s32[8]{0:T(128)} %param.20) | copy-start | bytes 100
  4.1 25.3 %all-to-all-start = ((f32[128,8,128]{2,1,0:T(8,128)}), f32[128,8,128]{2,1,0:T(8,128)S(1)}, u32[]{:S(2)}, u32[]{:S(2)}) async-start(f32[128,8,128]{2,1,0:T(8,128)} %bitcast.7), calls=%async_computation | async-start | bytes 1048576 | tf_op jit(solution)/shard_map/all_to_all | solution.py:32
  20.1 2.3 %copy-start.4 = (bf16[8,64,64]{2,1,0:T(8,128)(2,1)S(1)}, bf16[8,64,64]{2,1,0:T(8,128)(2,1)}, u32[]{:S(2)}) copy-start(bf16[8,64,64]{2,1,0:T(8,128)(2,1)} %param.17) | copy-start | bytes 196612
  30.3 39.3 %copy-start.1 = (f32[2,64,1,512]{3,2,1,0:T(1,128)S(1)}, f32[2,64,1,512]{3,2,1,0:T(1,128)}, u32[]{:S(2)}) copy-start(f32[2,64,1,512]{3,2,1,0:T(1,128)} %param.14) | copy-start | bytes 786436
  30.3 39.3 %copy-start.2 = (f32[2,64,1,512]{3,2,1,0:T(1,128)S(1)}, f32[2,64,1,512]{3,2,1,0:T(1,128)}, u32[]{:S(2)}) copy-start(f32[2,64,1,512]{3,2,1,0:T(1,128)} %param.13) | copy-start | bytes 786436
  30.3 39.3 %copy-start.5 = (f32[512]{0:T(512)S(1)}, f32[512]{0:T(512)}, u32[]{:S(2)}) copy-start(f32[512]{0:T(512)} %param.16) | copy-start | bytes 6148
  52.5 34.8 %copy-start.3 = (f32[2,64,1,512]{3,2,1,0:T(1,128)S(1)}, f32[2,64,1,512]{3,2,1,0:T(1,128)}, u32[]{:S(2)}) copy-start(f32[2,64,1,512]{3,2,1,0:T(1,128)} %param.12) | copy-start | bytes 786436

commit v15 on v14

--- a/solution.py
+++ b/solution.py
@@ -212,7 +212,7 @@
         block_flags = lax.dynamic_slice_in_dim(cut_pattern, first_row // RB, row_count // RB, 1)
         return jnp.repeat(block_flags, RB, axis=1).T
 
-    section = legendre
+    section = legendre * row_mask(jnp.int32(0), cycle_total).astype(legendre.dtype)[None]
     products = jnp.einsum(
         "mrl,nml->rmn",
         section,
@@ -220,15 +220,15 @@
         precision=lax.Precision.DEFAULT,
         preferred_element_type=jnp.float32,
     )
-    masked_products = products * row_mask(jnp.int32(0), cycle_total).astype(jnp.float32)[:, :, None]
+    masked_products = products
     coeffs = gather_cycles(masked_products.reshape(cycle_total, columns), band_count).astype(jnp.bfloat16)
     cycle_local = coeffs.shape[0]
     mode_total = coeffs.shape[1]
     outputs = cycle_transform(coeffs, cycle_lengths, noise_index, m_values, noise_mats, weight)
     returned = spread_cycles(outputs, band_count)
-    masked = returned * row_mask(jnp.int32(0), cycle_total).astype(jnp.bfloat16)
+    masked = returned
     image_data = lax.optimization_barrier(
-        jnp.einsum("rl,rn->nl", legendre[0], masked, preferred_element_type=jnp.float32)
+        jnp.einsum("rl,rn->nl", section[0], masked, preferred_element_type=jnp.float32)
     )
     image_data = image_data.reshape(2, map_count, mode_local, l_local)
     image_field = prior_inv[None, None, None, :] * direction + image_data

time: 89.3 us -> 90 us (level)
  Pallas kernels: 22.1 us -> 20.6 us
  matrix products: 0.82 us -> 2.15 us
    pallas_call x1, Pallas kernels: 22.1 us -> 20.6 us  [cycle_transform(): pl.pallas_call(noise_kernel, grid_spec=grid_spec, out_shape=jax.ShapeDtyp...]
    dot_general x1, matrix products: 0.47 us -> 1.71 us  [shards(): jnp.einsum('mrl,nml->rmn', section, direction.reshape(columns, mode_local...]
where the time goes in v15:
time: 90 us; the launch traced here: 88.6 us
  blocking collectives  30.3 us (34%)
  Pallas kernels  20.6 us (23%)
  other arithmetic  14.1 us (16%)
  starting transfers between devices  11.5 us (13%)
  local copies, waits for them, and re-layouts  4.94 us (5%)
  waiting for transfers between devices  4.1 us (5%)
  matrix products  2.15 us (2%)
    pallas_call x1, Pallas kernels, cycle_transform(): pl.pallas_call(noise_kernel, grid_spec=grid_spec, out_shape=jax.ShapeDtyp...  20.6 us
    all_to_all x1, blocking collectives, spread_cycles(): received = lax.all_to_all(pieces, MESH_AXES, 0, 0, tiled=True)  16.1 us
    all_to_all x1, blocking collectives, total_over_mesh(): return jnp.sum(lax.all_to_all(copies, MESH_AXES, 0, 0, tiled=True), axis=0)  14.2 us
    all_to_all x1, starting transfers between devices, gather_cycles(): received = lax.all_to_all(pieces, MESH_AXES, 0, 0, tiled=True)  11.5 us
    all_to_all x1, waiting for transfers between devices, gather_cycles(): received = lax.all_to_all(pieces, MESH_AXES, 0, 0, tiled=True)  4.1 us
    another operation x1, other arithmetic  2.81 us
    mul x1, other arithmetic, cycle_transform(): jnp.swapaxes(pair_table(noise_mats), 1, 2)  2.32 us
    convert_element_type x1, other arithmetic, cycle_tables(): return jnp.stack([cosine, sine_part], axis=1).astype(jnp.bfloat16)  2.29 us
  transfers between devices with their start and end apart: 1, of which 1 were waited for; matrix products, arithmetic and copies ran while one was open for 11% of the time, Pallas kernels for 0%

profile of v15, /device:TPU:1, one launch (start us, length us, event | category | flops | bytes accessed | tf_op | source)
XLA Modules:
  0.0 88.6 jit_solution(4996212896435785830)
XLA Ops:
  0.7 0.7 convert_bitcast_fusion.1
  1.3 0.1 broadcast_in_dim.20
  1.4 0.1 convert_element_type.50
  1.5 1.0 %copy.66 = bf16[2,64,1,512]{3,1,2,0:T(8,128)(2,1)S(1)} copy(f32[2,64,1,512]{3,2,1,0:T(1,128)} %param.14) | data formatting | bytes 393216
  2.5 1.7 %fusion.10 = f32[1024,128]{1,0:T(8,128)S(1)} fusion(bf16[128,512]{1,0:T(8,128)(2,1)S(1)} %bitcast.97, bf16[1,1024,512]{2,1,0:T(8,128)(2,1)} %param.15, bf16[1024]{0:T(1024)(128)(2,1)S(1)} %convert_element_type.50), kind=kOutput, calls=%fused_computation.15 | convolution fusion | flops 134742016 | bytes 1705984 | tf_op jit(solution)/shard_map/mrl,nml->rmn/dot_general | solution.py:216
  4.2 0.8 copy.55
  5.0 11.5 %all-to-all-start = ((f32[128,8,128]{2,1,0:T(8,128)}), f32[128,8,128]{2,1,0:T(8,128)S(1)}, u32[]{:S(2)}, u32[]{:S(2)}) async-start(f32[128,8,128]{2,1,0:T(8,128)} %bitcast.8), calls=%async_computation | async-start | bytes 1048576 | tf_op jit(solution)/shard_map/all_to_all | solution.py:32
  16.6 0.1 fusion.16
  16.8 1.0 %fusion.30 = (f32[8,8,128]{2,1,0:T(8,128)S(1)}, f32[8,8,128]{2,1,0:T(8,128)S(1)}, f32[8,8,128]{2,1,0:T(8,128)S(1)}, f32[8,8,128]{2,1,0:T(8,128)S(1)}) fusion(f32[8]{0:T(128)S(1)} %convert_element_type.54, pred[8]{0:T(512)(128)(4,1)S(1)} %compare_bitcast_fusion, s32[8]{0:T(128)S(1)} %fusion.34, s32[8,128]{1,0:T(8,128)S(1)} %get-tuple-element.24, ...), kind=kLoop, calls=%fused_computation.55 | loop fusion | flops 163840 | bytes 139336 | tf_op jit(solution)/shard_map/cos | solution.py:56
  17.8 0.2 copy.58
  18.0 0.2 copy.59
  18.2 2.8 %fusion.3 = (bf16[8,1,8,16384]{3,2,1,0:T(8,128)(2,1)S(1)}, bf16[8,1,8,16384]{3,2,1,0:T(8,128)(2,1)S(1)}) fusion(f32[8,16384]{1,0:T(8,128)S(1)} %fusion.16, f32[8,8,128]{2,1,0:T(8,128)S(1)} %get-tuple-element.20, f32[8,8,128]{1,2,0:T(8,128)S(1)} %copy.59, f32[8,8,128]{2,1,0:T(8,128)S(1)} %get-tuple-element.21, f32[8,8,128]{1,2,0:T(8,128)S(1)} %copy.58, ...), kind=kLoop, calls=%fused_computation.8 | loop fusion | flops 12582912 | bytes 4849728 | tf_op jit(solution)/shard_map/convert
  21.0 2.3 %maximum_bitcast_fusion.table_ref = bf16[8,16,16384]{2,1,0:T(8,128)(2,1)} fusion(bf16[8,1,8,16384]{3,2,1,0:T(8,128)(2,1)S(1)} %get-tuple-element.14, bf16[8,1,8,16384]{3,2,1,0:T(8,128)(2,1)S(1)} %get-tuple-element.13), kind=kLoop, calls=%fused_computation.2 | loop fusion | flops 2097152 | bytes 8388608 | tf_op jit(solution)/shard_map/convert_element_type | solution.py:69
  23.3 0.1 copy.60
  23.4 0.2 broadcast_in_dim.24
  23.7 0.2 broadcast_in_dim.25
  23.9 2.3 %fusion.7 = bf16[8,8,128,128]{2,3,1,0:T(8,128)(2,1)} fusion(bf16[8,8,64,64]{2,3,1,0:T(8,128)(2,1)S(1)} %broadcast_in_dim.25, bf16[8,8,64,64]{2,3,1,0:T(8,128)(2,1)S(1)} %broadcast_in_dim.24), kind=kLoop, calls=%fused_computation.12 | loop fusion | flops 10485760 | bytes 3145728 | tf_op jit(solution)/shard_map/mul | solution.py:172
  26.3 4.1 %all-to-all-done = f32[128,8,128]{2,1,0:T(8,128)S(1)} async-done(((f32[128,8,128]{2,1,0:T(8,128)}), f32[128,8,128]{2,1,0:T(8,128)S(1)}, u32[]{:S(2)}, u32[]{:S(2)}) %all-to-all-start) | async-done | bytes 524320 | tf_op jit(solution)/shard_map/all_to_all | solution.py:32
  30.4 0.1 reshape.325
  30.5 0.8 copy.62.coeff_ref
  31.3 20.6 %shard_map.121 = f32[8,8,128]{2,1,0:T(8,128)} custom-call(s32[8,256]{1,0:T(8,128)} %index_ref.1, s32[8]{0:T(128)} %length_ref.1, bf16[8,64,16]{2,1,0:T(8,128)(2,1)} %copy.62.coeff_ref, bf16[8,16,16384]{2,1,0:T(8,128)(2,1)} %maximum_bitcast_fusion.table_ref, bf16[64,128,128]{2,1,0:T(8,128)(2,1)} %bitcast.91), custom_call_target="tpu_custom_call" | custom-call | tf_op jit(solution)/shard_map/pallas_call | solution.py:184
  51.9 0.8 convert_element_type.58
  52.8 16.1 %all_to_all.15 = bf16[128,8,128]{2,1,0:T(8,128)(2,1)S(1)} all-to-all(bf16[128,8,128]{2,1,0:T(8,128)(2,1)S(1)} %bitcast.92), channel_id=1, replica_groups=mesh['mgrp'=8,'band'=16] {'mgrp','band'}, dimensions={0} | all-to-all | bytes 524288 | tf_op jit(solution)/shard_map/all_to_all | solution.py:42
  69.0 0.4 fusion.8
  69.4 1.3 %multiply_reduce_fusion.3 = (f32[64]{0:T(128)S(1)}, f32[64]{0:T(128)S(1)}, f32[64]{0:T(128)S(1)}, f32[64]{0:T(128)S(1)}, f32[2,64,1,512]{3,2,1,0:T(1,128)S(1)}) fusion(f32[2,64,1,512]{3,2,1,0:T(1,128)S(1)} %copy-done.2, f32[2,64,1,512]{3,2,1,0:T(1,128)S(1)} %copy-done, f32[2,64,1,512]{3,1,0,2:T(8,128)S(1)} %bitcast.95, f32[512]{0:T(512)S(1)} %copy-done.5), kind=kLoop, calls=%fused_computation.31 | loop fusion | flops 655104 | bytes 1051648 | tf_op jit(solution)/shard_map/reduce_sum | solution.py:238
  70.8 0.2 reshape.331
  71.0 14.2 %all_to_all.16 = f32[128,1,256]{2,1,0:T(1,128)S(1)} all-to-all(f32[128,1,256]{2,1,0:T(1,128)S(1)} %reshape.331), channel_id=1, replica_groups=mesh['mgrp'=8,'band'=16] {'mgrp','band'}, dimensions={0} | all-to-all | bytes 262144 | tf_op jit(solution)/shard_map/all_to_all | solution.py:23
  85.3 0.5 broadcast.214
  85.8 1.0 %reduce = f32[128,256]{1,0:T(8,128)S(1)} reduce(f32[128,1,256]{2,1,0:T(1,128)S(1)} %all_to_all.16, f32[]{:T(128)} %broadcast.214), dimensions={1}, to_apply=%all_to_all.11.reduce_sub_computation | reduce | bytes 262148 | tf_op jit(solution)/shard_map/all_to_all | solution.py:23
  86.7 0.2 reshape.332
  86.9 0.1 reduce_sum.59
  87.1 1.6 %multiply_add_fusion = (f32[2,64,1,512]{3,2,1,0:T(1,128)}, f32[2,64,1,512]{3,2,1,0:T(1,128)}, f32[2,64,1,512]{3,2,1,0:T(1,128)}) fusion(f32[2,64,1,512]{3,2,1,0:T(1,128)S(1)} %copy-done, f32[64]{0:T(128)S(1)} %get-tuple-element.10, f32[2,64,1,512]{3,2,1,0:T(1,128)S(1)} %copy-done.2, f32[2,64,1,512]{3,2,1,0:T(1,128)S(1)} %get-tuple-element.12, ...), kind=kLoop, calls=%fused_computation.25 | loop fusion | flops 393216 | bytes 1835520 | tf_op jit(solution)/shard_map/add | solution.py:250
  (30 shorter events, 0.3 us)
Async XLA Ops:
  0.6 15.9 %copy-start.6 = (s32[8]{0:T(128)S(1)}, s32[8]{0:T(128)}, u32[]{:S(2)}) copy-start(s32[8]{0:T(128)} %length_ref.1) | copy-start | bytes 100
  0.6 16.0 %copy-start.7 = (s32[8]{0:T(128)S(1)}, s32[8]{0:T(128)}, u32[]{:S(2)}) copy-start(s32[8]{0:T(128)} %param.20) | copy-start | bytes 100
  5.0 25.3 %all-to-all-start = ((f32[128,8,128]{2,1,0:T(8,128)}), f32[128,8,128]{2,1,0:T(8,128)S(1)}, u32[]{:S(2)}, u32[]{:S(2)}) async-start(f32[128,8,128]{2,1,0:T(8,128)} %bitcast.8), calls=%async_computation | async-start | bytes 1048576 | tf_op jit(solution)/shard_map/all_to_all | solution.py:32
  21.0 2.3 %copy-start.4 = (bf16[8,64,64]{2,1,0:T(8,128)(2,1)S(1)}, bf16[8,64,64]{2,1,0:T(8,128)(2,1)}, u32[]{:S(2)}) copy-start(bf16[8,64,64]{2,1,0:T(8,128)(2,1)} %param.17) | copy-start | bytes 196612
  30.4 38.6 %copy-start.1 = (bf16[1,1024,512]{2,1,0:T(8,128)(2,1)S(1)}, bf16[1,1024,512]{2,1,0:T(8,128)(2,1)}, u32[]{:S(2)}) copy-start(bf16[1,1024,512]{2,1,0:T(8,128)(2,1)} %param.15) | copy-start | bytes 3145732
  31.3 38.1 %copy-start = (f32[2,64,1,512]{3,2,1,0:T(1,128)S(1)}, f32[2,64,1,512]{3,2,1,0:T(1,128)}, u32[]{:S(2)}) copy-start(f32[2,64,1,512]{3,2,1,0:T(1,128)} %param.14) | copy-start | bytes 786436
  31.3 38.1 %copy-start.2 = (f32[2,64,1,512]{3,2,1,0:T(1,128)S(1)}, f32[2,64,1,512]{3,2,1,0:T(1,128)}, u32[]{:S(2)}) copy-start(f32[2,64,1,512]{3,2,1,0:T(1,128)} %param.13) | copy-start | bytes 786436
  31.3 38.2 %copy-start.5 = (f32[512]{0:T(512)S(1)}, f32[512]{0:T(512)}, u32[]{:S(2)}) copy-start(f32[512]{0:T(512)} %param.16) | copy-start | bytes 6148
  51.9 35.1 %copy-start.3 = (f32[2,64,1,512]{3,2,1,0:T(1,128)S(1)}, f32[2,64,1,512]{3,2,1,0:T(1,128)}, u32[]{:S(2)}) copy-start(f32[2,64,1,512]{3,2,1,0:T(1,128)} %param.12) | copy-start | bytes 786436

commit v16 on v14

--- a/solution.py
+++ b/solution.py
@@ -19,8 +19,9 @@
 
 def total_over_mesh(values):
     count = lax.axis_size(MESH_AXES)
-    copies = jnp.broadcast_to(values[None], (count,) + values.shape)
-    return jnp.sum(lax.all_to_all(copies, MESH_AXES, 0, 0, tiled=True), axis=0)
+    flat = values.reshape(-1, 128)
+    copies = jnp.broadcast_to(flat[None], (count,) + flat.shape)
+    return jnp.sum(lax.all_to_all(copies, MESH_AXES, 0, 0, tiled=True), axis=0).reshape(values.shape)
 
 
 def gather_cycles(partials, band_count):

time: 89.3 us -> 88 us (0.985)
  blocking collectives: 30 us -> 34.6 us
  Pallas kernels: 22.1 us -> 18.1 us
  other arithmetic: 14.3 us -> 13.3 us
    all_to_all x1, blocking collectives: 15.8 us -> 20.4 us  [spread_cycles(): received = lax.all_to_all(pieces, MESH_AXES, 0, 0, tiled=True)]
    pallas_call x1, Pallas kernels: 22.1 us -> 18.1 us  [cycle_transform(): pl.pallas_call(noise_kernel, grid_spec=grid_spec, out_shape=jax.ShapeDtyp...]
    all_to_all x1 -> x0, other arithmetic: 0.95 us -> none  [total_over_mesh(): return jnp.sum(lax.all_to_all(copies, MESH_AXES, 0, 0, tiled=True), axis=0)]
where the time goes in v16:
time: 88 us; the launch traced here: 87.6 us
  blocking collectives  34.6 us (39%)
  Pallas kernels  18.1 us (21%)
  other arithmetic  13.3 us (15%)
  starting transfers between devices  11.5 us (13%)
  local copies, waits for them, and re-layouts  4.37 us (5%)
  waiting for transfers between devices  4.09 us (5%)
  between operations  0.88 us (1%)
    all_to_all x1, blocking collectives, spread_cycles(): received = lax.all_to_all(pieces, MESH_AXES, 0, 0, tiled=True)  20.4 us
    pallas_call x1, Pallas kernels, cycle_transform(): pl.pallas_call(noise_kernel, grid_spec=grid_spec, out_shape=jax.ShapeDtyp...  18.1 us
    all_to_all x1, blocking collectives, total_over_mesh(): lax.all_to_all(copies, MESH_AXES, 0, 0, tiled=True)  14.2 us
    all_to_all x1, starting transfers between devices, gather_cycles(): received = lax.all_to_all(pieces, MESH_AXES, 0, 0, tiled=True)  11.5 us
    all_to_all x1, waiting for transfers between devices, gather_cycles(): received = lax.all_to_all(pieces, MESH_AXES, 0, 0, tiled=True)  4.09 us
    another operation x1, other arithmetic  2.81 us
    mul x1, other arithmetic, cycle_transform(): jnp.swapaxes(pair_table(noise_mats), 1, 2)  2.32 us
    convert_element_type x1, other arithmetic, cycle_tables(): return jnp.stack([cosine, sine_part], axis=1).astype(jnp.bfloat16)  2.3 us
  transfers between devices with their start and end apart: 1, of which 1 were waited for; matrix products, arithmetic and copies ran while one was open for 11% of the time, Pallas kernels for 0%

profile of v16, /device:TPU:1, one launch (start us, length us, event | category | flops | bytes accessed | tf_op | source)
XLA Modules:
  0.0 87.6 jit_solution(13997126212564960129)
XLA Ops:
  0.7 0.8 convert_bitcast_fusion.1
  1.5 0.1 convert_element_type.63
  1.6 1.0 %copy.71 = bf16[2,64,1,512]{3,1,2,0:T(8,128)(2,1)S(1)} copy(f32[2,64,1,512]{3,2,1,0:T(1,128)} %param.14) | data formatting | bytes 393216
  2.6 0.5 fusion.9
  3.0 0.2 copy.59
  3.2 0.8 copy.60
  4.1 11.5 %all-to-all-start = ((f32[128,8,128]{2,1,0:T(8,128)}), f32[128,8,128]{2,1,0:T(8,128)S(1)}, u32[]{:S(2)}, u32[]{:S(2)}) async-start(f32[128,8,128]{2,1,0:T(8,128)} %bitcast.7), calls=%async_computation | async-start | bytes 1048576 | tf_op jit(solution)/shard_map/all_to_all | solution.py:33
  15.6 0.1 fusion.13
  15.8 0.1 multiply_bitcast_fusion.2
  15.8 1.0 %fusion.27 = (f32[8,8,128]{2,1,0:T(8,128)S(1)}, f32[8,8,128]{2,1,0:T(8,128)S(1)}, f32[8,8,128]{2,1,0:T(8,128)S(1)}, f32[8,8,128]{2,1,0:T(8,128)S(1)}) fusion(f32[8]{0:T(128)S(1)} %convert_element_type.67, pred[8]{0:T(512)(128)(4,1)S(1)} %compare_bitcast_fusion, s32[8]{0:T(128)S(1)} %fusion.31, s32[8,128]{1,0:T(8,128)S(1)} %get-tuple-element.26, ...), kind=kLoop, calls=%fused_computation.54 | loop fusion | flops 163840 | bytes 139336 | tf_op jit(solution)/shard_map/cos | solution.py:57
  16.8 0.2 copy.63
  17.0 0.2 copy.64
  17.2 2.8 %fusion.3 = (bf16[8,1,8,16384]{3,2,1,0:T(8,128)(2,1)S(1)}, bf16[8,1,8,16384]{3,2,1,0:T(8,128)(2,1)S(1)}) fusion(f32[8,16384]{1,0:T(8,128)S(1)} %fusion.13, f32[8,8,128]{2,1,0:T(8,128)S(1)} %get-tuple-element.20, f32[8,8,128]{1,2,0:T(8,128)S(1)} %copy.64, f32[8,8,128]{2,1,0:T(8,128)S(1)} %get-tuple-element.21, f32[8,8,128]{1,2,0:T(8,128)S(1)} %copy.63, ...), kind=kLoop, calls=%fused_computation.8 | loop fusion | flops 12582912 | bytes 4849728 | tf_op jit(solution)/shard_map/convert
  20.1 2.3 %maximum_bitcast_fusion.table_ref = bf16[8,16,16384]{2,1,0:T(8,128)(2,1)} fusion(bf16[8,1,8,16384]{3,2,1,0:T(8,128)(2,1)S(1)} %get-tuple-element.14, bf16[8,1,8,16384]{3,2,1,0:T(8,128)(2,1)S(1)} %get-tuple-element.13), kind=kLoop, calls=%fused_computation.2 | loop fusion | flops 2097152 | bytes 8388608 | tf_op jit(solution)/shard_map/convert_element_type | solution.py:70
  22.4 0.1 copy.65
  22.5 0.2 broadcast_in_dim.26
  22.7 0.2 broadcast_in_dim.27
  23.0 2.3 %fusion.7 = bf16[8,8,128,128]{2,3,1,0:T(8,128)(2,1)} fusion(bf16[8,8,64,64]{2,3,1,0:T(8,128)(2,1)S(1)} %broadcast_in_dim.27, bf16[8,8,64,64]{2,3,1,0:T(8,128)(2,1)S(1)} %broadcast_in_dim.26), kind=kLoop, calls=%fused_computation.12 | loop fusion | flops 10485760 | bytes 3145728 | tf_op jit(solution)/shard_map/mul | solution.py:173
  25.3 4.1 %all-to-all-done = f32[128,8,128]{2,1,0:T(8,128)S(1)} async-done(((f32[128,8,128]{2,1,0:T(8,128)}), f32[128,8,128]{2,1,0:T(8,128)S(1)}, u32[]{:S(2)}, u32[]{:S(2)}) %all-to-all-start) | async-done | bytes 524320 | tf_op jit(solution)/shard_map/all_to_all | solution.py:33
  29.5 0.1 reshape.348
  29.6 0.8 copy.67.coeff_ref
  30.3 18.1 %shard_map.121 = f32[8,8,128]{2,1,0:T(8,128)} custom-call(s32[8,256]{1,0:T(8,128)} %index_ref.1, s32[8]{0:T(128)} %length_ref.1, bf16[8,64,16]{2,1,0:T(8,128)(2,1)} %copy.67.coeff_ref, bf16[8,16,16384]{2,1,0:T(8,128)(2,1)} %maximum_bitcast_fusion.table_ref, bf16[64,128,128]{2,1,0:T(8,128)(2,1)} %bitcast.95), custom_call_target="tpu_custom_call" | custom-call | tf_op jit(solution)/shard_map/pallas_call | solution.py:185
  48.4 0.8 convert_element_type.71
  49.2 20.4 %all_to_all.15 = bf16[128,8,128]{2,1,0:T(8,128)(2,1)S(1)} all-to-all(bf16[128,8,128]{2,1,0:T(8,128)(2,1)S(1)} %bitcast.98), channel_id=1, replica_groups=mesh['mgrp'=8,'band'=16] {'mgrp','band'}, dimensions={0} | all-to-all | bytes 524288 | tf_op jit(solution)/shard_map/all_to_all | solution.py:43
  69.6 0.1 multiply_bitcast_fusion
  69.8 0.3 fusion.10
  70.1 1.3 %multiply_reduce_fusion.3 = (f32[64]{0:T(128)S(1)}, f32[64]{0:T(128)S(1)}, f32[64]{0:T(128)S(1)}, f32[64]{0:T(128)S(1)}, f32[2,64,1,512]{3,2,1,0:T(1,128)S(1)}) fusion(f32[2,64,1,512]{3,2,1,0:T(1,128)S(1)} %copy-done.2, f32[2,64,1,512]{3,2,1,0:T(1,128)S(1)} %copy-done.1, f32[2,64,1,512]{3,1,0,2:T(8,128)S(1)} %bitcast.100, f32[512]{0:T(512)S(1)} %copy-done.5), kind=kLoop, calls=%fused_computation.30 | loop fusion | flops 655104 | bytes 1051648 | tf_op jit(solution)/shard_map/reduce_sum | solution.py:239
  71.5 0.1 broadcast_in_dim.29
  71.6 14.2 %all_to_all.16 = f32[128,2,128]{2,1,0:T(2,128)S(1)} all-to-all(f32[128,2,128]{2,1,0:T(2,128)S(1)} %broadcast_in_dim.30), channel_id=1, replica_groups=mesh['mgrp'=8,'band'=16] {'mgrp','band'}, dimensions={0} | all-to-all | bytes 262144 | tf_op jit(solution)/shard_map/all_to_all | solution.py:24
  85.8 0.1 reduce_sum.59
  85.9 0.1 reshape.353
  86.0 1.6 %multiply_add_fusion = (f32[2,64,1,512]{3,2,1,0:T(1,128)}, f32[2,64,1,512]{3,2,1,0:T(1,128)}, f32[2,64,1,512]{3,2,1,0:T(1,128)}) fusion(f32[2,64,1,512]{3,2,1,0:T(1,128)S(1)} %copy-done.1, f32[64]{0:T(128)S(1)} %get-tuple-element.10, f32[2,64,1,512]{3,2,1,0:T(1,128)S(1)} %copy-done.2, f32[2,64,1,512]{3,2,1,0:T(1,128)S(1)} %get-tuple-element.12, ...), kind=kLoop, calls=%fused_computation.23 | loop fusion | flops 393216 | bytes 1835520 | tf_op jit(solution)/shard_map/add | solution.py:251
  (30 shorter events, 0.3 us)
Async XLA Ops:
  0.6 1.9 %copy-start = (bf16[1,1024,512]{2,1,0:T(8,128)(2,1)S(1)}, bf16[1,1024,512]{2,1,0:T(8,128)(2,1)}, u32[]{:S(2)}) copy-start(bf16[1,1024,512]{2,1,0:T(8,128)(2,1)} %param.15) | copy-start | bytes 3145732
  0.6 14.9 %copy-start.6 = (s32[8]{0:T(128)S(1)}, s32[8]{0:T(128)}, u32[]{:S(2)}) copy-start(s32[8]{0:T(128)} %length_ref.1) | copy-start | bytes 100
  0.7 15.1 %copy-start.7 = (s32[8]{0:T(128)S(1)}, s32[8]{0:T(128)}, u32[]{:S(2)}) copy-start(s32[8]{0:T(128)} %param.20) | copy-start | bytes 100
  4.1 25.3 %all-to-all-start = ((f32[128,8,128]{2,1,0:T(8,128)}), f32[128,8,128]{2,1,0:T(8,128)S(1)}, u32[]{:S(2)}, u32[]{:S(2)}) async-start(f32[128,8,128]{2,1,0:T(8,128)} %bitcast.7), calls=%async_computation | async-start | bytes 1048576 | tf_op jit(solution)/shard_map/all_to_all | solution.py:33
  20.0 2.3 %copy-start.4 = (bf16[8,64,64]{2,1,0:T(8,128)(2,1)S(1)}, bf16[8,64,64]{2,1,0:T(8,128)(2,1)}, u32[]{:S(2)}) copy-start(bf16[8,64,64]{2,1,0:T(8,128)(2,1)} %param.17) | copy-start | bytes 196612
  30.3 39.8 %copy-start.1 = (f32[2,64,1,512]{3,2,1,0:T(1,128)S(1)}, f32[2,64,1,512]{3,2,1,0:T(1,128)}, u32[]{:S(2)}) copy-start(f32[2,64,1,512]{3,2,1,0:T(1,128)} %param.14) | copy-start | bytes 786436
  30.3 39.8 %copy-start.2 = (f32[2,64,1,512]{3,2,1,0:T(1,128)S(1)}, f32[2,64,1,512]{3,2,1,0:T(1,128)}, u32[]{:S(2)}) copy-start(f32[2,64,1,512]{3,2,1,0:T(1,128)} %param.13) | copy-start | bytes 786436
  30.3 39.8 %copy-start.5 = (f32[512]{0:T(512)S(1)}, f32[512]{0:T(512)}, u32[]{:S(2)}) copy-start(f32[512]{0:T(512)} %param.16) | copy-start | bytes 6148
  30.3 55.7 %copy-start.3 = (f32[2,64,1,512]{3,2,1,0:T(1,128)S(1)}, f32[2,64,1,512]{3,2,1,0:T(1,128)}, u32[]{:S(2)}) copy-start(f32[2,64,1,512]{3,2,1,0:T(1,128)} %param.12) | copy-start | bytes 786436

commit v17 on v16

--- a/solution.py
+++ b/solution.py
@@ -103,7 +103,7 @@
     return backward.reshape(cycle_count, mode_count, columns).astype(jnp.bfloat16)
 
 
-def noise_kernel(index_ref, length_ref, coeff_ref, table_ref, pair_ref, back_ref, noisy_ref):
+def noise_kernel(index_ref, length_ref, coeff_ref, table_ref, pair_ref, back_ref, noisy_ref, sums_ref):
     cycle = pl.program_id(0)
     wide = noisy_ref.shape[1]
     pair_width = 2 * BLK
@@ -157,7 +157,11 @@
     for part in range(table_ref.shape[1] // modes):
         for mode in range(modes):
             row = part * modes + mode
-            back_ref[mode, pl.ds(cycle, 1), part * maps:(part + 1) * maps] = total[row:row + 1, :]
+            sums_ref[mode, pl.ds(cycle, 1), part * maps:(part + 1) * maps] = total[row:row + 1, :]
+
+    @pl.when(cycle == pl.num_programs(0) - 1)
+    def _():
+        back_ref[...] = sums_ref[...].astype(back_ref.dtype)
 
 
 def cycle_transform(coeffs, lengths, indices, m_values, noise_mats, weight):
@@ -180,14 +184,17 @@
             pl.BlockSpec(pairs_t.shape, lambda r, idx, n: (0, 0, 0)),
         ],
         out_specs=pl.BlockSpec((mode_count, cycle_count, columns), lambda r, idx, n: (0, 0, 0)),
-        scratch_shapes=[pltpu.VMEM((map_count, 8192), jnp.bfloat16)],
+        scratch_shapes=[
+            pltpu.VMEM((map_count, 8192), jnp.bfloat16),
+            pltpu.VMEM((mode_count, cycle_count, columns), jnp.float32),
+        ],
     )
     back = pl.pallas_call(
         noise_kernel,
         grid_spec=grid_spec,
-        out_shape=jax.ShapeDtypeStruct((mode_count, cycle_count, columns), jnp.float32),
+        out_shape=jax.ShapeDtypeStruct((mode_count, cycle_count, columns), jnp.bfloat16),
     )(indices, lengths, coeff_t, tables, pairs_t)
-    return back.astype(jnp.bfloat16)
+    return back
 
 
 def shards(

time: 88 us -> 87.1 us (0.990)
  blocking collectives: 34.6 us -> 31.6 us
  Pallas kernels: 18.1 us -> 20.7 us
    all_to_all x1, blocking collectives: 20.4 us -> 17.4 us  [spread_cycles(): received = lax.all_to_all(pieces, MESH_AXES, 0, 0, tiled=True)]
    pallas_call x1, Pallas kernels: 18.1 us -> 20.7 us  [cycle_transform(): pl.pallas_call(noise_kernel, grid_spec=grid_spec, out_shape=jax.ShapeDtyp...]
where the time goes in v17:
time: 87.1 us; the launch traced here: 87.2 us
  blocking collectives  31.6 us (36%)
  Pallas kernels  20.7 us (24%)
  other arithmetic  12.5 us (14%)
  starting transfers between devices  11.5 us (13%)
  local copies, waits for them, and re-layouts  5.08 us (6%)
  waiting for transfers between devices  4.09 us (5%)
  between operations  0.88 us (1%)
    pallas_call x1, Pallas kernels, cycle_transform(): pl.pallas_call(noise_kernel, grid_spec=grid_spec, out_shape=jax.ShapeDtyp...  20.7 us
    all_to_all x1, blocking collectives, spread_cycles(): received = lax.all_to_all(pieces, MESH_AXES, 0, 0, tiled=True)  17.4 us
    all_to_all x1, blocking collectives, total_over_mesh(): lax.all_to_all(copies, MESH_AXES, 0, 0, tiled=True)  14.2 us
    all_to_all x1, starting transfers between devices, gather_cycles(): received = lax.all_to_all(pieces, MESH_AXES, 0, 0, tiled=True)  11.5 us
    all_to_all x1, waiting for transfers between devices, gather_cycles(): received = lax.all_to_all(pieces, MESH_AXES, 0, 0, tiled=True)  4.09 us
    another operation x1, other arithmetic  2.81 us
    mul x1, other arithmetic, cycle_transform(): jnp.swapaxes(pair_table(noise_mats), 1, 2)  2.32 us
    convert_element_type x1, other arithmetic, cycle_tables(): return jnp.stack([cosine, sine_part], axis=1).astype(jnp.bfloat16)  2.3 us
  transfers between devices with their start and end apart: 1, of which 1 were waited for; matrix products, arithmetic and copies ran while one was open for 11% of the time, Pallas kernels for 0%

profile of v17, /device:TPU:1, one launch (start us, length us, event | category | flops | bytes accessed | tf_op | source)
XLA Modules:
  0.0 87.2 jit_solution(1826056706744932551)
XLA Ops:
  0.7 0.8 convert_bitcast_fusion.1
  1.5 0.1 convert_element_type.60
  1.6 1.0 %copy.71 = bf16[2,64,1,512]{3,1,2,0:T(8,128)(2,1)S(1)} copy(f32[2,64,1,512]{3,2,1,0:T(1,128)} %param.14) | data formatting | bytes 393216
  2.6 0.5 fusion.9
  3.0 0.2 copy.59
  3.2 0.8 copy.60
  4.1 11.5 %all-to-all-start = ((f32[128,8,128]{2,1,0:T(8,128)}), f32[128,8,128]{2,1,0:T(8,128)S(1)}, u32[]{:S(2)}, u32[]{:S(2)}) async-start(f32[128,8,128]{2,1,0:T(8,128)} %bitcast.7), calls=%async_computation | async-start | bytes 1048576 | tf_op jit(solution)/shard_map/all_to_all | solution.py:33
  15.6 0.1 fusion.13
  15.8 0.1 multiply_bitcast_fusion.2
  15.8 1.0 %fusion.27 = (f32[8,8,128]{2,1,0:T(8,128)S(1)}, f32[8,8,128]{2,1,0:T(8,128)S(1)}, f32[8,8,128]{2,1,0:T(8,128)S(1)}, f32[8,8,128]{2,1,0:T(8,128)S(1)}) fusion(f32[8]{0:T(128)S(1)} %convert_element_type.64, pred[8]{0:T(512)(128)(4,1)S(1)} %compare_bitcast_fusion, s32[8]{0:T(128)S(1)} %fusion.31, s32[8,128]{1,0:T(8,128)S(1)} %get-tuple-element.26, ...), kind=kLoop, calls=%fused_computation.54 | loop fusion | flops 163840 | bytes 139336 | tf_op jit(solution)/shard_map/cos | solution.py:57
  16.8 0.2 copy.63
  17.0 0.2 copy.64
  17.2 2.8 %fusion.3 = (bf16[8,1,8,16384]{3,2,1,0:T(8,128)(2,1)S(1)}, bf16[8,1,8,16384]{3,2,1,0:T(8,128)(2,1)S(1)}) fusion(f32[8,16384]{1,0:T(8,128)S(1)} %fusion.13, f32[8,8,128]{2,1,0:T(8,128)S(1)} %get-tuple-element.20, f32[8,8,128]{1,2,0:T(8,128)S(1)} %copy.64, f32[8,8,128]{2,1,0:T(8,128)S(1)} %get-tuple-element.21, f32[8,8,128]{1,2,0:T(8,128)S(1)} %copy.63, ...), kind=kLoop, calls=%fused_computation.8 | loop fusion | flops 12582912 | bytes 4849728 | tf_op jit(solution)/shard_map/convert
  20.1 2.3 %maximum_bitcast_fusion.table_ref = bf16[8,16,16384]{2,1,0:T(8,128)(2,1)} fusion(bf16[8,1,8,16384]{3,2,1,0:T(8,128)(2,1)S(1)} %get-tuple-element.14, bf16[8,1,8,16384]{3,2,1,0:T(8,128)(2,1)S(1)} %get-tuple-element.13), kind=kLoop, calls=%fused_computation.2 | loop fusion | flops 2097152 | bytes 8388608 | tf_op jit(solution)/shard_map/convert_element_type | solution.py:70
  22.4 0.1 copy.65
  22.5 0.2 broadcast_in_dim.26
  22.7 0.2 broadcast_in_dim.27
  23.0 2.3 %fusion.7 = bf16[8,8,128,128]{2,3,1,0:T(8,128)(2,1)} fusion(bf16[8,8,64,64]{2,3,1,0:T(8,128)(2,1)S(1)} %broadcast_in_dim.27, bf16[8,8,64,64]{2,3,1,0:T(8,128)(2,1)S(1)} %broadcast_in_dim.26), kind=kLoop, calls=%fused_computation.12 | loop fusion | flops 10485760 | bytes 3145728 | tf_op jit(solution)/shard_map/mul | solution.py:177
  25.3 4.1 %all-to-all-done = f32[128,8,128]{2,1,0:T(8,128)S(1)} async-done(((f32[128,8,128]{2,1,0:T(8,128)}), f32[128,8,128]{2,1,0:T(8,128)S(1)}, u32[]{:S(2)}, u32[]{:S(2)}) %all-to-all-start) | async-done | bytes 524320 | tf_op jit(solution)/shard_map/all_to_all | solution.py:33
  29.5 0.1 reshape.348
  29.6 0.8 copy.67.coeff_ref
  30.3 20.7 %shard_map.121 = bf16[8,8,128]{2,1,0:T(8,128)(2,1)} custom-call(s32[8,256]{1,0:T(8,128)} %index_ref.1, s32[8]{0:T(128)} %length_ref.1, bf16[8,64,16]{2,1,0:T(8,128)(2,1)} %copy.67.coeff_ref, bf16[8,16,16384]{2,1,0:T(8,128)(2,1)} %maximum_bitcast_fusion.table_ref, bf16[64,128,128]{2,1,0:T(8,128)(2,1)} %bitcast.95), custom_call_target="tpu_custom_call" | custom-call | tf_op jit(solution)/shard_map/pallas_call | solution.py:192
  51.0 0.8 broadcast_in_dim.28
  51.8 17.4 %all_to_all.15 = bf16[128,8,128]{2,1,0:T(8,128)(2,1)S(1)} all-to-all(bf16[128,8,128]{2,1,0:T(8,128)(2,1)S(1)} %bitcast.98), channel_id=1, replica_groups=mesh['mgrp'=8,'band'=16] {'mgrp','band'}, dimensions={0} | all-to-all | bytes 524288 | tf_op jit(solution)/shard_map/all_to_all | solution.py:43
  69.2 0.1 multiply_bitcast_fusion
  69.3 0.3 fusion.10
  69.7 1.3 %multiply_reduce_fusion.3 = (f32[64]{0:T(128)S(1)}, f32[64]{0:T(128)S(1)}, f32[64]{0:T(128)S(1)}, f32[64]{0:T(128)S(1)}, f32[2,64,1,512]{3,2,1,0:T(1,128)S(1)}) fusion(f32[2,64,1,512]{3,2,1,0:T(1,128)S(1)} %copy-done.2, f32[2,64,1,512]{3,2,1,0:T(1,128)S(1)} %copy-done.1, f32[2,64,1,512]{3,1,0,2:T(8,128)S(1)} %bitcast.100, f32[512]{0:T(512)S(1)} %copy-done.5), kind=kLoop, calls=%fused_computation.30 | loop fusion | flops 655104 | bytes 1051648 | tf_op jit(solution)/shard_map/reduce_sum | solution.py:246
  71.0 0.1 broadcast_in_dim.29
  71.1 14.2 %all_to_all.16 = f32[128,2,128]{2,1,0:T(2,128)S(1)} all-to-all(f32[128,2,128]{2,1,0:T(2,128)S(1)} %broadcast_in_dim.30), channel_id=1, replica_groups=mesh['mgrp'=8,'band'=16] {'mgrp','band'}, dimensions={0} | all-to-all | bytes 262144 | tf_op jit(solution)/shard_map/all_to_all | solution.py:24
  85.3 0.1 reduce_sum.59
  85.5 0.1 reshape.353
  85.6 1.6 %multiply_add_fusion = (f32[2,64,1,512]{3,2,1,0:T(1,128)}, f32[2,64,1,512]{3,2,1,0:T(1,128)}, f32[2,64,1,512]{3,2,1,0:T(1,128)}) fusion(f32[2,64,1,512]{3,2,1,0:T(1,128)S(1)} %copy-done.1, f32[64]{0:T(128)S(1)} %get-tuple-element.10, f32[2,64,1,512]{3,2,1,0:T(1,128)S(1)} %copy-done.2, f32[2,64,1,512]{3,2,1,0:T(1,128)S(1)} %get-tuple-element.12, ...), kind=kLoop, calls=%fused_computation.23 | loop fusion | flops 393216 | bytes 1835520 | tf_op jit(solution)/shard_map/add | solution.py:258
  (29 shorter events, 0.3 us)
Async XLA Ops:
  0.6 1.9 %copy-start = (bf16[1,1024,512]{2,1,0:T(8,128)(2,1)S(1)}, bf16[1,1024,512]{2,1,0:T(8,128)(2,1)}, u32[]{:S(2)}) copy-start(bf16[1,1024,512]{2,1,0:T(8,128)(2,1)} %param.15) | copy-start | bytes 3145732
  0.6 14.9 %copy-start.6 = (s32[8]{0:T(128)S(1)}, s32[8]{0:T(128)}, u32[]{:S(2)}) copy-start(s32[8]{0:T(128)} %length_ref.1) | copy-start | bytes 100
  0.7 15.1 %copy-start.7 = (s32[8]{0:T(128)S(1)}, s32[8]{0:T(128)}, u32[]{:S(2)}) copy-start(s32[8]{0:T(128)} %param.20) | copy-start | bytes 100
  4.1 25.3 %all-to-all-start = ((f32[128,8,128]{2,1,0:T(8,128)}), f32[128,8,128]{2,1,0:T(8,128)S(1)}, u32[]{:S(2)}, u32[]{:S(2)}) async-start(f32[128,8,128]{2,1,0:T(8,128)} %bitcast.7), calls=%async_computation | async-start | bytes 1048576 | tf_op jit(solution)/shard_map/all_to_all | solution.py:33
  20.0 2.3 %copy-start.4 = (bf16[8,64,64]{2,1,0:T(8,128)(2,1)S(1)}, bf16[8,64,64]{2,1,0:T(8,128)(2,1)}, u32[]{:S(2)}) copy-start(bf16[8,64,64]{2,1,0:T(8,128)(2,1)} %param.17) | copy-start | bytes 196612
  30.3 39.3 %copy-start.1 = (f32[2,64,1,512]{3,2,1,0:T(1,128)S(1)}, f32[2,64,1,512]{3,2,1,0:T(1,128)}, u32[]{:S(2)}) copy-start(f32[2,64,1,512]{3,2,1,0:T(1,128)} %param.14) | copy-start | bytes 786436
  30.3 39.4 %copy-start.2 = (f32[2,64,1,512]{3,2,1,0:T(1,128)S(1)}, f32[2,64,1,512]{3,2,1,0:T(1,128)}, u32[]{:S(2)}) copy-start(f32[2,64,1,512]{3,2,1,0:T(1,128)} %param.13) | copy-start | bytes 786436
  30.3 39.4 %copy-start.5 = (f32[512]{0:T(512)S(1)}, f32[512]{0:T(512)}, u32[]{:S(2)}) copy-start(f32[512]{0:T(512)} %param.16) | copy-start | bytes 6148
  30.3 55.3 %copy-start.3 = (f32[2,64,1,512]{3,2,1,0:T(1,128)S(1)}, f32[2,64,1,512]{3,2,1,0:T(1,128)}, u32[]{:S(2)}) copy-start(f32[2,64,1,512]{3,2,1,0:T(1,128)} %param.12) | copy-start | bytes 786436

commit v18 on v17

--- a/solution.py
+++ b/solution.py
@@ -133,7 +133,9 @@
     rest = length - full * wide
     wide_count = full + (rest > mid + narrow).astype(jnp.int32)
     mid_count = ((rest > narrow) & (rest <= mid + narrow)).astype(jnp.int32)
-    narrow_count = (((rest > 0) & (rest <= narrow)) | ((rest > mid) & (rest <= mid + narrow))).astype(jnp.int32)
+    left = jnp.where(rest > mid + narrow, 0, rest - mid_count * mid)
+    narrow_count = (left > narrow // 2).astype(jnp.int32)
+    tiny_count = ((left > 0) & (left <= narrow // 2)).astype(jnp.int32)
     total = lax.fori_loop(
         0,
         wide_count,
@@ -150,6 +152,12 @@
         0,
         narrow_count,
         lambda step, acc: chunk(pl.multiple_of(full * wide + mid_count * mid, mid), narrow, acc),
+        total,
+    )
+    total = lax.fori_loop(
+        0,
+        tiny_count,
+        lambda step, acc: chunk(pl.multiple_of(full * wide + mid_count * mid, mid), narrow // 2, acc),
         total,
     )
     modes = back_ref.shape[0]

time: 87.1 us -> 87.4 us (level); the launches traced: 87.2 us -> 86.4 us
  Pallas kernels: 20.7 us -> 19 us
  blocking collectives: 31.6 us -> 32.5 us
    pallas_call x1, Pallas kernels: 20.7 us -> 19 us  [cycle_transform(): pl.pallas_call(noise_kernel, grid_spec=grid_spec, out_shape=jax.ShapeDtyp...]
    all_to_all x1, blocking collectives: 17.4 us -> 18.3 us  [spread_cycles(): received = lax.all_to_all(pieces, MESH_AXES, 0, 0, tiled=True)]
where the time goes in v18:
time: 87.4 us; the launch traced here: 86.4 us
  blocking collectives  32.5 us (37%)
  Pallas kernels  19 us (22%)
  other arithmetic  12.5 us (14%)
  starting transfers between devices  11.5 us (13%)
  local copies, waits for them, and re-layouts  5.08 us (6%)
  waiting for transfers between devices  4.09 us (5%)
  between operations  0.88 us (1%)
    pallas_call x1, Pallas kernels, cycle_transform(): pl.pallas_call(noise_kernel, grid_spec=grid_spec, out_shape=jax.ShapeDtyp...  19 us
    all_to_all x1, blocking collectives, spread_cycles(): received = lax.all_to_all(pieces, MESH_AXES, 0, 0, tiled=True)  18.3 us
    all_to_all x1, blocking collectives, total_over_mesh(): lax.all_to_all(copies, MESH_AXES, 0, 0, tiled=True)  14.2 us
    all_to_all x1, starting transfers between devices, gather_cycles(): received = lax.all_to_all(pieces, MESH_AXES, 0, 0, tiled=True)  11.5 us
    all_to_all x1, waiting for transfers between devices, gather_cycles(): received = lax.all_to_all(pieces, MESH_AXES, 0, 0, tiled=True)  4.09 us
    another operation x1, other arithmetic  2.81 us
    mul x1, other arithmetic, cycle_transform(): jnp.swapaxes(pair_table(noise_mats), 1, 2)  2.32 us
    convert_element_type x1, other arithmetic, cycle_tables(): return jnp.stack([cosine, sine_part], axis=1).astype(jnp.bfloat16)  2.3 us
  transfers between devices with their start and end apart: 1, of which 1 were waited for; matrix products, arithmetic and copies ran while one was open for 11% of the time, Pallas kernels for 0%

profile of v18, /device:TPU:1, one launch (start us, length us, event | category | flops | bytes accessed | tf_op | source)
XLA Modules:
  0.0 86.4 jit_solution(8688753163239417880)
XLA Ops:
  0.7 0.8 convert_bitcast_fusion.1
  1.5 0.1 convert_element_type.60
  1.6 1.0 %copy.71 = bf16[2,64,1,512]{3,1,2,0:T(8,128)(2,1)S(1)} copy(f32[2,64,1,512]{3,2,1,0:T(1,128)} %param.14) | data formatting | bytes 393216
  2.6 0.5 fusion.9
  3.0 0.2 copy.59
  3.2 0.8 copy.60
  4.1 11.5 %all-to-all-start = ((f32[128,8,128]{2,1,0:T(8,128)}), f32[128,8,128]{2,1,0:T(8,128)S(1)}, u32[]{:S(2)}, u32[]{:S(2)}) async-start(f32[128,8,128]{2,1,0:T(8,128)} %bitcast.7), calls=%async_computation | async-start | bytes 1048576 | tf_op jit(solution)/shard_map/all_to_all | solution.py:33
  15.6 0.1 fusion.13
  15.8 0.1 multiply_bitcast_fusion.2
  15.8 1.0 %fusion.27 = (f32[8,8,128]{2,1,0:T(8,128)S(1)}, f32[8,8,128]{2,1,0:T(8,128)S(1)}, f32[8,8,128]{2,1,0:T(8,128)S(1)}, f32[8,8,128]{2,1,0:T(8,128)S(1)}) fusion(f32[8]{0:T(128)S(1)} %convert_element_type.64, pred[8]{0:T(512)(128)(4,1)S(1)} %compare_bitcast_fusion, s32[8]{0:T(128)S(1)} %fusion.31, s32[8,128]{1,0:T(8,128)S(1)} %get-tuple-element.26, ...), kind=kLoop, calls=%fused_computation.54 | loop fusion | flops 163840 | bytes 139336 | tf_op jit(solution)/shard_map/cos | solution.py:57
  16.8 0.2 copy.63
  17.0 0.2 copy.64
  17.2 2.8 %fusion.3 = (bf16[8,1,8,16384]{3,2,1,0:T(8,128)(2,1)S(1)}, bf16[8,1,8,16384]{3,2,1,0:T(8,128)(2,1)S(1)}) fusion(f32[8,16384]{1,0:T(8,128)S(1)} %fusion.13, f32[8,8,128]{2,1,0:T(8,128)S(1)} %get-tuple-element.20, f32[8,8,128]{1,2,0:T(8,128)S(1)} %copy.64, f32[8,8,128]{2,1,0:T(8,128)S(1)} %get-tuple-element.21, f32[8,8,128]{1,2,0:T(8,128)S(1)} %copy.63, ...), kind=kLoop, calls=%fused_computation.8 | loop fusion | flops 12582912 | bytes 4849728 | tf_op jit(solution)/shard_map/convert
  20.1 2.3 %maximum_bitcast_fusion.table_ref = bf16[8,16,16384]{2,1,0:T(8,128)(2,1)} fusion(bf16[8,1,8,16384]{3,2,1,0:T(8,128)(2,1)S(1)} %get-tuple-element.14, bf16[8,1,8,16384]{3,2,1,0:T(8,128)(2,1)S(1)} %get-tuple-element.13), kind=kLoop, calls=%fused_computation.2 | loop fusion | flops 2097152 | bytes 8388608 | tf_op jit(solution)/shard_map/convert_element_type | solution.py:70
  22.4 0.1 copy.65
  22.5 0.2 broadcast_in_dim.26
  22.7 0.2 broadcast_in_dim.27
  23.0 2.3 %fusion.7 = bf16[8,8,128,128]{2,3,1,0:T(8,128)(2,1)} fusion(bf16[8,8,64,64]{2,3,1,0:T(8,128)(2,1)S(1)} %broadcast_in_dim.27, bf16[8,8,64,64]{2,3,1,0:T(8,128)(2,1)S(1)} %broadcast_in_dim.26), kind=kLoop, calls=%fused_computation.12 | loop fusion | flops 10485760 | bytes 3145728 | tf_op jit(solution)/shard_map/mul | solution.py:185
  25.3 4.1 %all-to-all-done = f32[128,8,128]{2,1,0:T(8,128)S(1)} async-done(((f32[128,8,128]{2,1,0:T(8,128)}), f32[128,8,128]{2,1,0:T(8,128)S(1)}, u32[]{:S(2)}, u32[]{:S(2)}) %all-to-all-start) | async-done | bytes 524320 | tf_op jit(solution)/shard_map/all_to_all | solution.py:33
  29.5 0.1 reshape.348
  29.6 0.8 copy.67.coeff_ref
  30.3 19.0 %shard_map.121 = bf16[8,8,128]{2,1,0:T(8,128)(2,1)} custom-call(s32[8,256]{1,0:T(8,128)} %index_ref.1, s32[8]{0:T(128)} %length_ref.1, bf16[8,64,16]{2,1,0:T(8,128)(2,1)} %copy.67.coeff_ref, bf16[8,16,16384]{2,1,0:T(8,128)(2,1)} %maximum_bitcast_fusion.table_ref, bf16[64,128,128]{2,1,0:T(8,128)(2,1)} %bitcast.95), custom_call_target="tpu_custom_call" | custom-call | tf_op jit(solution)/shard_map/pallas_call | solution.py:200
  49.3 0.8 broadcast_in_dim.28
  50.1 18.3 %all_to_all.15 = bf16[128,8,128]{2,1,0:T(8,128)(2,1)S(1)} all-to-all(bf16[128,8,128]{2,1,0:T(8,128)(2,1)S(1)} %bitcast.98), channel_id=1, replica_groups=mesh['mgrp'=8,'band'=16] {'mgrp','band'}, dimensions={0} | all-to-all | bytes 524288 | tf_op jit(solution)/shard_map/all_to_all | solution.py:43
  68.4 0.1 multiply_bitcast_fusion
  68.6 0.3 fusion.10
  68.9 1.3 %multiply_reduce_fusion.3 = (f32[64]{0:T(128)S(1)}, f32[64]{0:T(128)S(1)}, f32[64]{0:T(128)S(1)}, f32[64]{0:T(128)S(1)}, f32[2,64,1,512]{3,2,1,0:T(1,128)S(1)}) fusion(f32[2,64,1,512]{3,2,1,0:T(1,128)S(1)} %copy-done.2, f32[2,64,1,512]{3,2,1,0:T(1,128)S(1)} %copy-done.1, f32[2,64,1,512]{3,1,0,2:T(8,128)S(1)} %bitcast.100, f32[512]{0:T(512)S(1)} %copy-done.5), kind=kLoop, calls=%fused_computation.30 | loop fusion | flops 655104 | bytes 1051648 | tf_op jit(solution)/shard_map/reduce_sum | solution.py:254
  70.2 0.1 broadcast_in_dim.29
  70.4 14.2 %all_to_all.16 = f32[128,2,128]{2,1,0:T(2,128)S(1)} all-to-all(f32[128,2,128]{2,1,0:T(2,128)S(1)} %broadcast_in_dim.30), channel_id=1, replica_groups=mesh['mgrp'=8,'band'=16] {'mgrp','band'}, dimensions={0} | all-to-all | bytes 262144 | tf_op jit(solution)/shard_map/all_to_all | solution.py:24
  84.6 0.1 reduce_sum.59
  84.7 0.1 reshape.353
  84.8 1.6 %multiply_add_fusion = (f32[2,64,1,512]{3,2,1,0:T(1,128)}, f32[2,64,1,512]{3,2,1,0:T(1,128)}, f32[2,64,1,512]{3,2,1,0:T(1,128)}) fusion(f32[2,64,1,512]{3,2,1,0:T(1,128)S(1)} %copy-done.1, f32[64]{0:T(128)S(1)} %get-tuple-element.10, f32[2,64,1,512]{3,2,1,0:T(1,128)S(1)} %copy-done.2, f32[2,64,1,512]{3,2,1,0:T(1,128)S(1)} %get-tuple-element.12, ...), kind=kLoop, calls=%fused_computation.23 | loop fusion | flops 393216 | bytes 1835520 | tf_op jit(solution)/shard_map/add | solution.py:266
  (29 shorter events, 0.3 us)
Async XLA Ops:
  0.6 1.9 %copy-start = (bf16[1,1024,512]{2,1,0:T(8,128)(2,1)S(1)}, bf16[1,1024,512]{2,1,0:T(8,128)(2,1)}, u32[]{:S(2)}) copy-start(bf16[1,1024,512]{2,1,0:T(8,128)(2,1)} %param.15) | copy-start | bytes 3145732
  0.6 14.9 %copy-start.6 = (s32[8]{0:T(128)S(1)}, s32[8]{0:T(128)}, u32[]{:S(2)}) copy-start(s32[8]{0:T(128)} %length_ref.1) | copy-start | bytes 100
  0.7 15.1 %copy-start.7 = (s32[8]{0:T(128)S(1)}, s32[8]{0:T(128)}, u32[]{:S(2)}) copy-start(s32[8]{0:T(128)} %param.20) | copy-start | bytes 100
  4.1 25.3 %all-to-all-start = ((f32[128,8,128]{2,1,0:T(8,128)}), f32[128,8,128]{2,1,0:T(8,128)S(1)}, u32[]{:S(2)}, u32[]{:S(2)}) async-start(f32[128,8,128]{2,1,0:T(8,128)} %bitcast.7), calls=%async_computation | async-start | bytes 1048576 | tf_op jit(solution)/shard_map/all_to_all | solution.py:33
  20.0 2.3 %copy-start.4 = (bf16[8,64,64]{2,1,0:T(8,128)(2,1)S(1)}, bf16[8,64,64]{2,1,0:T(8,128)(2,1)}, u32[]{:S(2)}) copy-start(bf16[8,64,64]{2,1,0:T(8,128)(2,1)} %param.17) | copy-start | bytes 196612
  30.3 38.6 %copy-start.1 = (f32[2,64,1,512]{3,2,1,0:T(1,128)S(1)}, f32[2,64,1,512]{3,2,1,0:T(1,128)}, u32[]{:S(2)}) copy-start(f32[2,64,1,512]{3,2,1,0:T(1,128)} %param.14) | copy-start | bytes 786436
  30.3 38.6 %copy-start.2 = (f32[2,64,1,512]{3,2,1,0:T(1,128)S(1)}, f32[2,64,1,512]{3,2,1,0:T(1,128)}, u32[]{:S(2)}) copy-start(f32[2,64,1,512]{3,2,1,0:T(1,128)} %param.13) | copy-start | bytes 786436
  30.3 38.6 %copy-start.5 = (f32[512]{0:T(512)S(1)}, f32[512]{0:T(512)}, u32[]{:S(2)}) copy-start(f32[512]{0:T(512)} %param.16) | copy-start | bytes 6148
  30.3 54.5 %copy-start.3 = (f32[2,64,1,512]{3,2,1,0:T(1,128)S(1)}, f32[2,64,1,512]{3,2,1,0:T(1,128)}, u32[]{:S(2)}) copy-start(f32[2,64,1,512]{3,2,1,0:T(1,128)} %param.12) | copy-start | bytes 786436
